TPU v7x, 32 devices: a whole 2x2x4 slice. The times are simulated.
32 devices in a mesh: rep: 8 (over z, x), tile: 4 (over y, core).
Axes of the slice: x: 2, y: 2, z: 4, core: 2. Of those that a mesh axis runs over, the one named last changes fastest.
Arguments:
- features: bfloat16 [16, 48, 72, 1536], P('rep', 'tile'), may hold values from -6 to 6
- conv_out: bfloat16 [16, 48, 72, 256], P('rep', 'tile'), may hold values from -6 to 6
- conv_weight: bfloat16 [9, 1536, 256], replicated, may hold values from -0.0546875 to 0.0546875
- norm_gain_vector: float32 [256], replicated, may hold values from 0.5 to 1.5
- norm_shift_vector: float32 [256], replicated, may hold values from -3 to 3
- class_map: float32 [3, 256], replicated, may hold values from -3 to 3
- labels: int32 [16, 48, 72], P('rep', 'tile'), may hold values from 0 to 2
- class_weight: int32 [3], replicated, may hold values from 1 to 39
Outputs:
- grad_features: bfloat16 [16, 48, 72, 1536], P('rep', 'tile')
- grad_weight: float32 [1536, 9, 256], P(('rep', 'tile'))
- grad_gain: float32 [256], replicated
- grad_shift: float32 [256], replicated
- grad_class: float32 [3, 256], replicated
- loss: float32 [], replicated
All inputs are finite; a program needn't handle non-finite values.
Results may differ from a plain program's by a relative error of at most 0.0049.
Values may be sent and summed in bfloat16 or wider, within the bound.
No kernel may reach another device: no remote copies, remote signals or barrier semaphores. Data moves between devices by JAX's collectives and lax.ppermute only.
A program may use at most 256 MiB of HBM per device.

v0:
```python
import jax
import jax.numpy as jnp
from jax import lax
from jax.sharding import PartitionSpec as P

IMG_DEV = 2
H = 48
W = 72
RATE = 12


def padded(x, sides, width):
    for axis, dim in sides:
        size, length = (lax.axis_size(axis), x.shape[dim])
        up = [(i, (i + 1) % size) for i in range(size - 1)]
        down = [(j, i) for i, j in up]
        last = lax.slice_in_dim(x, length - width, length, axis=dim)
        first = lax.slice_in_dim(x, 0, width, axis=dim)
        before = lax.ppermute(last, axis, up)
        after = lax.ppermute(first, axis, down)
        x = jnp.concatenate([before, x, after], axis=dim)
    return x


def index_bits(axes):
    bits = []
    for axis in reversed(axes):
        size = lax.axis_size(axis)
        assert size & (size - 1) == 0
        bits += [(axis, b) for b in range(size.bit_length() - 1)]
    return bits


def exchange(x, axis, bit):
    size = lax.axis_size(axis)
    pairs = [(i, i ^ (1 << bit)) for i in range(size)]
    return lax.ppermute(x, axis, pairs)


def butterfly_sum(x, axes):
    for axis, bit in index_bits(axes):
        x = jax.tree.map(lambda v, w: v + w, x, exchange(x, axis, bit))
    return x


def halving_scatter(x, steps, bit_axes):
    bit_axes = list(bit_axes)
    for axis, bit, combined in steps:
        ax = bit_axes.index(combined)
        mine = (lax.axis_index(axis) >> bit) & 1
        keep = lax.dynamic_index_in_dim(x, mine, ax, keepdims=False)
        send = lax.dynamic_index_in_dim(x, 1 - mine, ax, keepdims=False)
        x = keep + exchange(send, axis, bit)
        bit_axes.pop(ax)
    return x


def body(
    features,
    conv_out,
    conv_weight,
    norm_gain_vector,
    norm_shift_vector,
    class_map,
    labels,
    class_weight,
):
    highest = lax.Precision.HIGHEST
    images, tile_rows, columns, in_chans = features.shape
    out_chans = conv_out.shape[3]
    taps = conv_weight.shape[0]
    local_pix = images * tile_rows * columns
    per_replica_part = IMG_DEV * H * W
    all_pix = lax.axis_size("rep") * per_replica_part
    classes = class_map.shape[0]

    onehot = (
        labels.reshape(local_pix, 1) == jnp.arange(classes, dtype=jnp.int32)
    ).astype(jnp.float32)
    weights_pix = jnp.sum(onehot * class_weight.astype(jnp.float32), -1)

    yvals = conv_out.astype(jnp.float32).reshape(local_pix, out_chans)
    first_sums = lax.psum(jnp.concatenate([jnp.sum(yvals, 0), jnp.sum(weights_pix)[None]]), "tile")
    column_sum, weight_tile = first_sums[:out_chans], first_sums[out_chans]
    weight_total = butterfly_sum(weight_tile, ("rep",))
    centre_offset = yvals - column_sum / per_replica_part
    variance = lax.psum(jnp.sum(centre_offset * centre_offset, 0), "tile") / per_replica_part
    inverse_deviation = lax.rsqrt(variance + 1e-05)
    normalized_input = centre_offset * inverse_deviation
    preactivation_values = norm_gain_vector * normalized_input + norm_shift_vector
    zvals = jnp.maximum(preactivation_values, 0.0)
    logits = jnp.dot(zvals, class_map.T, precision=highest)
    top_val = jnp.max(logits, -1, keepdims=True)
    log_total = top_val[:, 0] + jnp.log(jnp.sum(jnp.exp(logits - top_val), -1))
    cross = log_total - jnp.sum(onehot * logits, -1)
    mean_weight = weight_total / all_pix
    probs = jnp.exp(logits - log_total[:, None])
    grad_logit = (weights_pix / mean_weight)[:, None] * (probs - onehot)
    class_local_slice = jnp.dot(grad_logit.T, zvals, precision=highest)
    grad_z = jnp.dot(grad_logit, class_map, precision=highest)
    preactivation_gradient = jnp.where(preactivation_values > 0, grad_z, 0.0)
    first_gradient_sum, second_gradient_sum, class_tile, loss_tile = lax.psum(
        (
            jnp.sum(preactivation_gradient, 0),
            jnp.sum(preactivation_gradient * normalized_input, 0),
            class_local_slice,
            jnp.sum(weights_pix * cross),
        ),
        "tile",
    )
    packed = jnp.concatenate(
        [first_gradient_sum, second_gradient_sum, class_tile.reshape(-1), loss_tile[None]]
    )
    normalized_output_gradient = (
        norm_gain_vector
        * inverse_deviation
        * (
            preactivation_gradient
            - first_gradient_sum / per_replica_part
            - normalized_input * second_gradient_sum / per_replica_part
        )
    ).astype(jnp.bfloat16)
    normalized_output_gradient = normalized_output_gradient.reshape(
        images, tile_rows, columns, out_chans
    )
    column_pad = ((0, 0), (0, 0), (RATE, RATE), (0, 0))
    extended = jnp.pad(padded(normalized_output_gradient, (("tile", 1),), RATE), column_pad)
    own_rows = jnp.pad(normalized_output_gradient, column_pad)
    shifted_list = []
    for tap_index in range(taps):
        row_off = RATE - (tap_index // 3 - 1) * RATE
        col_off = RATE - (tap_index % 3 - 1) * RATE
        if tap_index // 3 == 1:
            piece = own_rows[:, :, col_off : col_off + columns, :]
        else:
            piece = extended[:, row_off : row_off + tile_rows, col_off : col_off + columns, :]
        shifted_list.append(piece.reshape(local_pix, out_chans))
    shifted = jnp.concatenate(shifted_list, 1)

    blocks = lax.axis_size("rep") * lax.axis_size("tile")
    nbits = blocks.bit_length() - 1
    rows = in_chans // blocks
    flat_x = features.reshape(local_pix, in_chans)
    packed, flat_x = lax.optimization_barrier((packed, flat_x))
    bits = [(axis, bit, combined) for combined, (axis, bit) in enumerate(index_bits(("rep", "tile")))]
    rest = bits[1:]
    orders = [rest, rest[1:] + rest[:1], rest[2:3] + rest[:2] + rest[3:]]
    group_taps = [taps - 2 * (taps // 3), taps // 3, taps // 3]
    starts = [sum(group_taps[:s]) for s in range(3)]
    parts = []
    for s in range(3):
        cols = jnp.concatenate(shifted_list[starts[s] : starts[s] + group_taps[s]], 1)
        part = lax.dot_general(
            flat_x, cols, (((0,), (0,)), ((), ())), preferred_element_type=jnp.float32
        )
        parts.append(part.reshape((2,) * nbits + (rows, group_taps[s] * out_chans)))

    halves = 2 if images % 2 == 0 else 1
    share = local_pix // halves
    grad_chunks = [
        lax.dot_general(
            shifted[h * share : (h + 1) * share].reshape(share, taps, out_chans),
            conv_weight,
            (((1, 2), (0, 2)), ((), ())),
            preferred_element_type=jnp.float32,
        ).astype(jnp.bfloat16)
        for h in range(halves)
    ]
    axis, bit, combined = bits[0]
    bit_axes = list(range(nbits - 1, -1, -1))
    ax = bit_axes.index(combined)
    mine = (lax.axis_index(axis) >> bit) & 1
    keeps = [lax.dynamic_index_in_dim(p, mine, ax, keepdims=False) for p in parts]
    sends = [lax.dynamic_index_in_dim(p, 1 - mine, ax, keepdims=False) for p in parts]
    received = lax.optimization_barrier([exchange(v, axis, bit) for v in sends])
    bit_axes.pop(ax)
    pieces = [keeps[s] + received[s] for s in range(3)]
    small_bits = index_bits(("rep",))
    axes_of = [list(bit_axes) for s in range(3)]
    for step in range(len(rest)):
        sends, keeps = [], []
        for s in range(3):
            axis, bit, combined = orders[s][step]
            ax = axes_of[s].index(combined)
            mine = (lax.axis_index(axis) >> bit) & 1
            keeps.append(lax.dynamic_index_in_dim(pieces[s], mine, ax, keepdims=False))
            sends.append(lax.dynamic_index_in_dim(pieces[s], 1 - mine, ax, keepdims=False))
            axes_of[s].pop(ax)
        received = []
        if step < len(small_bits):
            packed, sends = lax.optimization_barrier((packed, sends))
            received.append(exchange(packed, *small_bits[step]))
        received = [exchange(sends[s], orders[s][step][0], orders[s][step][1]) for s in range(3)] + received
        if step < halves:
            received, grad_chunks[step] = lax.optimization_barrier((received, grad_chunks[step]))
        else:
            received = lax.optimization_barrier(received)
        if step < len(small_bits):
            packed = packed + received.pop()
        pieces = [keeps[s] + received[s] for s in range(3)]
    grad_weight = jnp.concatenate(pieces, 1).reshape(rows, taps, out_chans)

    for step in range(len(rest), len(small_bits)):
        packed = packed + exchange(packed, *small_bits[step])
    grad_shift = packed[:out_chans]
    grad_gain = packed[out_chans : 2 * out_chans]
    grad_class = packed[2 * out_chans : (2 + classes) * out_chans].reshape(classes, out_chans)
    loss = packed[(2 + classes) * out_chans] / mean_weight / all_pix
    grad_features = jnp.concatenate(grad_chunks, 0).reshape(images, tile_rows, columns, in_chans)
    return (grad_features, grad_weight, grad_gain, grad_shift, grad_class, loss)


def solution(mesh):
    in_specs = (
        P("rep", "tile", None, None),
        P("rep", "tile", None, None),
        P(),
        P(),
        P(),
        P(),
        P("rep", "tile", None),
        P(),
    )
    out_specs = (P("rep", "tile", None, None), P(("rep", "tile"), None, None), P(), P(), P(), P())
    return jax.shard_map(body, mesh=mesh, in_specs=in_specs, out_specs=out_specs, check_vma=False)
```

profile of v0, /device:TPU:0, one launch (start us, length us, event | category | flops | bytes accessed | tf_op | source)
XLA Modules:
  0.0 190.8 jit_solution(1783754508769919940)
XLA Ops:
  4.9 8.4 %psum.42 = f32[257]{0:T(512)S(1)} all-reduce(f32[257]{0:T(512)S(1)} %pad_maximum_fusion.3), channel_id=1, replica_groups=mesh['rep'=8,'tile'=4] {'tile'}, use_global_device_ids=true, to_apply=%region_2.0 | all-reduce | flops 257 | bytes 2056 | tf_op jit(solution)/shard_map/psum | solution.py:83
  16.8 5.8 %psum.43 = f32[256]{0:T(256)S(1)} all-reduce(f32[256]{0:T(256)S(1)} %multiply_reduce_fusion.1), channel_id=1, replica_groups=mesh['rep'=8,'tile'=4] {'tile'}, use_global_device_ids=true, to_apply=%region_4.0 | all-reduce | flops 256 | bytes 2048 | tf_op jit(solution)/shard_map/psum | solution.py:87
  27.8 2.9 %collective-permute-start.1 = (f32[]{:T(128)}, f32[]{:T(128)}, u32[]{:S(2)}, u32[]{:S(2)}) collective-permute-start(f32[]{:T(128)} %add.168), channel_id=1, source_target_pairs={{0,8},{4,12},{8,0},{12,4},{16,24},{20,28},{24,16},{28,20},{1,9},{5... | collective-permute-start | bytes 20 | tf_op jit(solution)/shard_map/ppermute | solution.py:37
  32.0 4.0 %collective-permute-start.2 = (f32[]{:T(128)}, f32[]{:T(128)}, u32[]{:S(2)}, u32[]{:S(2)}) collective-permute-start(f32[]{:T(128)} %add.169), channel_id=1, source_target_pairs={{0,16},{4,20},{8,24},{12,28},{16,0},{20,4},{24,8},{28,12},{1,17},{... | collective-permute-start | bytes 20 | tf_op jit(solution)/shard_map/ppermute | solution.py:37
  37.7 3.3 %fusion.41 = (f32[256]{0:T(256)S(1)}, f32[256]{0:T(256)S(1)}, f32[1728,256]{1,0:T(8,128)}) fusion(f32[256]{0:T(256)S(1)} %get-tuple-element.116, f32[256]{0:T(256)S(1)} %slice_multiply_fusion, bf16[2,12,72,256]{3,2,1,0:T(8,128)(2,1)S(1)} %copy-done.2, f32[3,256]{1,0:T(4,128)S(1)} %copy-done, f32[1728,3]{0,1:T(4,128)S(1)} %get-tuple-element.118, ...), kind=kOutput, calls=%fused_computation.116 | convolution fusion | flops 20374336 | bytes 4474368 | tf_op jit(solution)/shard_map/dot_general | solution.py:100
  42.0 6.5 %all-reduce.2 = (f32[1]{0:T(128)}, f32[768]{0:T(1024)S(1)}, f32[256]{0:T(256)S(1)}, f32[256]{0:T(256)S(1)}) all-reduce(f32[1]{0:T(128)} %bitcast.3, f32[768]{0:T(1024)S(1)} %reshape.99, f32[256]{0:T(256)S(1)} %get-tuple-element.87, f32[256]{0:T(256)S(1)} %get-tuple-element.86), channel_id=1, replica_groups=mesh['rep'=8,'tile'=4] {'tile'}, use_global_device_ids=true, to_apply=%region_15.16 | all-reduce | flops 1281 | bytes 10248 | tf_op jit(solution)/shard_map/psum | solution.py:102
  55.0 6.5 %fusion.12 = f32[1536,768]{1,0:T(8,128)S(1)} fusion(bf16[1728,1536]{1,0:T(8,128)(2,1)} %bitcast.136, bf16[1728,256]{1,0:T(8,128)(2,1)S(1)} %bitcast.130, bf16[1728,256]{1,0:T(8,128)(2,1)S(1)} %multiply_convert_fusion, bf16[1728,256]{1,0:T(8,128)(2,1)S(1)} %bitcast.132), kind=kOutput, calls=%fused_computation.18 | convolution fusion | flops 4084826112 | bytes 12681216 | tf_op jit(solution)/shard_map/dot_general | solution.py:153
  68.0 4.5 %fusion.6 = f32[1536,768]{1,0:T(8,128)S(1)} fusion(bf16[1728,1536]{1,0:T(8,128)(2,1)S(1)} %bitcast.139, bf16[1728,256]{1,0:T(8,128)(2,1)S(1)} %bitcast.126, bf16[1728,256]{1,0:T(8,128)(2,1)S(1)} %bitcast.125, bf16[1728,256]{1,0:T(8,128)(2,1)S(1)} %bitcast.129), kind=kOutput, calls=%fused_computation.12 | convolution fusion | flops 4084826112 | bytes 12681216 | tf_op jit(solution)/shard_map/dot_general | solution.py:153
  72.6 4.5 %fusion.18 = f32[1536,768]{1,0:T(8,128)S(1)} fusion(bf16[1728,1536]{1,0:T(8,128)(2,1)S(1)} %bitcast.140, bf16[1728,256]{1,0:T(8,128)(2,1)S(1)} %bitcast.120, bf16[1728,256]{1,0:T(8,128)(2,1)S(1)} %bitcast.118, bf16[1728,256]{1,0:T(8,128)(2,1)S(1)} %bitcast.122), kind=kOutput, calls=%fused_computation.24 | convolution fusion | flops 4084826112 | bytes 12681216 | tf_op jit(solution)/shard_map/dot_general | solution.py:153
  80.4 2.5 %collective-permute-start.7 = (f32[2,2,2,2,48,768]{5,4,3,2,0,1:T(8,128)}, f32[2,2,2,2,48,768]{5,4,3,2,0,1:T(8,128)}, u32[]{:S(2)}, u32[]{:S(2)}) collective-permute-start(f32[2,2,2,2,48,768]{5,4,3,2,0,1:T(8,128)} %bitcast.104), channel_id=1, source_target_pairs={{0,1},{1,0},{2,3},{3,2},{4,5},{5,4},{6,7},{7,6},{8,9},{9,8},{10,11... | collective-permute-start | bytes 7077896 | tf_op jit(solution)/shard_map/ppermute | solution.py:37
  86.6 3.3 %fusion.42 = (bf16[864,2304]{1,0:T(8,128)(2,1)}, bf16[864,2304]{1,0:T(8,128)(2,1)}) fusion(bf16[1728,2304]{1,0:T(8,128)(2,1)S(1)} %constant_dynamic-update-slice_fusion), kind=kLoop, calls=%fused_computation.117 | loop fusion | bytes 15925248 | tf_op jit(solution)/shard_map/slice | solution.py:162
  89.9 6.3 %copy.32 = bf16[864,2304]{0,1:T(8,128)(2,1)} copy(bf16[864,2304]{1,0:T(8,128)(2,1)} %get-tuple-element.99) | data formatting | bytes 7962624 | tf_op jit(solution)/shard_map/slice | solution.py:162
  96.3 2.7 %bitcast_add_fusion = f32[2,2,2,2,48,768]{5,4,3,2,0,1:T(8,128)S(1)} fusion(f32[2,2,2,2,48,768]{5,4,3,2,0,1:T(8,128)} %collective-permute-done.7, f32[2,2,2,2,1,48,768]{6,5,4,3,2,1,0:T(8,128)} %get-tuple-element.100), kind=kLoop, calls=%fused_computation.30 | loop fusion | flops 589824 | bytes 7077888 | tf_op jit(solution)/shard_map/add | solution.py:177
  112.5 10.2 %bitcast_convert_fusion.1 = bf16[864,1536]{1,0:T(8,128)(2,1)} fusion(bf16[864,9,256]{0,2,1:T(8,128)(2,1)S(1)} %bitcast.117, bf16[9,1536,256]{2,1,0:T(8,128)(2,1)} %param.10), kind=kOutput, calls=%fused_computation.5 | convolution fusion | flops 6116622336 | bytes 13713408 | tf_op jit(solution)/shard_map/dot_general | solution.py:161
  122.8 6.3 %copy.34 = bf16[864,2304]{0,1:T(8,128)(2,1)} copy(bf16[864,2304]{1,0:T(8,128)(2,1)} %get-tuple-element.98) | data formatting | bytes 7962624 | tf_op jit(solution)/shard_map/slice | solution.py:162
  129.1 9.5 %collective-permute-done.11 = f32[1281]{0:T(1024)} collective-permute-done((f32[1281]{0:T(1024)S(1)}, f32[1281]{0:T(1024)}, u32[]{:S(2)}, u32[]{:S(2)}) %collective-permute-start.11) | collective-permute-done | bytes 5156 | tf_op jit(solution)/shard_map/ppermute | solution.py:37
  138.7 2.7 %bitcast_add_fusion.3 = (f32[2,2,2,48,768]{4,3,2,1,0:T(8,128)S(1)}, f32[2,2,2,48,768]{4,3,2,1,0:T(8,128)S(1)}) fusion(f32[2,2,2,48,768]{4,3,2,1,0:T(8,128)} %collective-permute-done.10, f32[2,2,2,2,48,768]{5,4,3,2,0,1:T(8,128)} %copy-done.4, s32[]{:T(128)S(6)} %select_n.71, f32[2,2,2,48,768]{4,3,2,1,0:T(8,128)} %collective-permute-done.9, ...), kind=kLoop, calls=%fused_computation.48 | loop fusion | flops 589824 | bytes 7077896 | tf_op jit(solution)/shard_map/add | solution.py:200
  148.2 9.1 %bitcast_convert_fusion = bf16[864,1536]{1,0:T(8,128)(2,1)S(1)} fusion(bf16[864,9,256]{0,2,1:T(8,128)(2,1)S(1)} %bitcast.116, bf16[9,1536,256]{2,1,0:T(8,128)(2,1)} %param.10), kind=kOutput, calls=%fused_computation.4 | convolution fusion | flops 6116622336 | bytes 13713408 | tf_op jit(solution)/shard_map/dot_general | solution.py:161
  161.0 2.6 %collective-permute-start.17 = (f32[2,48,768]{2,1,0:T(8,128)S(1)}, f32[2,48,768]{2,1,0:T(8,128)S(1)}, u32[]{:S(2)}, u32[]{:S(2)}) collective-permute-start(f32[2,48,768]{2,1,0:T(8,128)S(1)} %dynamic-slice_bitcast_fusion.7), channel_id=1, source_target_pairs={{0,16},{4,20},{8,24},{12,28},{16,0},{20,4},{24,8},{28,12},{1,17},{... | collective-permute-start | bytes 884744 | tf_op jit(solution)/shard_map/ppermute | solution.py:37
  165.4 2.7 %pad_maximum_fusion = bf16[1728,1536]{1,0:T(8,128)(2,1)} fusion(bf16[864,1536]{1,0:T(8,128)(2,1)S(1)} %bitcast_convert_fusion, bf16[864,1536]{1,0:T(8,128)(2,1)S(1)} %copy-done.8), kind=kLoop, calls=%fused_computation.3 | loop fusion | flops 10616832 | bytes 10616832 | tf_op jit(solution)/shard_map/concatenate | solution.py:209
  168.1 7.1 %collective-permute-done.19 = f32[1281]{0:T(1024)S(1)} collective-permute-done((f32[1281]{0:T(1024)S(1)}, f32[1281]{0:T(1024)S(1)}, u32[]{:S(2)}, u32[]{:S(2)}) %collective-permute-start.19) | collective-permute-done | bytes 5156 | tf_op jit(solution)/shard_map/ppermute | solution.py:37
  178.7 3.0 %collective-permute-start.20 = (f32[48,768]{1,0:T(8,128)S(1)}, f32[48,768]{1,0:T(8,128)S(1)}, u32[]{:S(2)}, u32[]{:S(2)}) collective-permute-start(f32[48,768]{1,0:T(8,128)S(1)} %dynamic-slice_bitcast_fusion.11), channel_id=1, source_target_pairs={{0,16},{4,20},{8,24},{12,28},{16,0},{20,4},{24,8},{28,12},{1,17},{... | collective-permute-start | bytes 442376 | tf_op jit(solution)/shard_map/ppermute | solution.py:37
  182.3 3.3 %collective-permute-done.22 = f32[48,768]{1,0:T(8,128)S(1)} collective-permute-done((f32[48,768]{1,0:T(8,128)S(1)}, f32[48,768]{1,0:T(8,128)S(1)}, u32[]{:S(2)}, u32[]{:S(2)}) %collective-permute-start.22) | collective-permute-done | bytes 147488 | tf_op jit(solution)/shard_map/ppermute | solution.py:37
  185.6 3.2 %collective-permute-done.20 = f32[48,768]{1,0:T(8,128)S(1)} collective-permute-done((f32[48,768]{1,0:T(8,128)S(1)}, f32[48,768]{1,0:T(8,128)S(1)}, u32[]{:S(2)}, u32[]{:S(2)}) %collective-permute-start.20) | collective-permute-done | bytes 147488 | tf_op jit(solution)/shard_map/ppermute | solution.py:37
  (134 shorter events, 64.2 us)
Async XLA Ops:
  0.6 24.1 %copy-start = (f32[3,256]{1,0:T(4,128)S(1)}, f32[3,256]{1,0:T(4,128)}, u32[]{:S(2)}) copy-start(f32[3,256]{1,0:T(4,128)} %param.13) | copy-start | bytes 9220
  13.8 12.8 %collective-permute-start = (f32[]{:T(128)}, f32[]{:T(128)}, u32[]{:S(2)}, u32[]{:S(2)}) collective-permute-start(f32[]{:T(128)} %bitcast.2), channel_id=1, source_target_pairs={{0,4},{4,0},{8,12},{12,8},{16,20},{20,16},{24,28},{28,24},{1,5},{5... | collective-permute-start | bytes 20 | tf_op jit(solution)/shard_map/ppermute | solution.py:37
  27.8 3.6 %collective-permute-start.1 = (f32[]{:T(128)}, f32[]{:T(128)}, u32[]{:S(2)}, u32[]{:S(2)}) collective-permute-start(f32[]{:T(128)} %add.168), channel_id=1, source_target_pairs={{0,8},{4,12},{8,0},{12,4},{16,24},{20,28},{24,16},{28,20},{1,9},{5... | collective-permute-start | bytes 20 | tf_op jit(solution)/shard_map/ppermute | solution.py:37
  32.0 4.5 %collective-permute-start.2 = (f32[]{:T(128)}, f32[]{:T(128)}, u32[]{:S(2)}, u32[]{:S(2)}) collective-permute-start(f32[]{:T(128)} %add.169), channel_id=1, source_target_pairs={{0,16},{4,20},{8,24},{12,28},{16,0},{20,4},{24,8},{28,12},{1,17},{... | collective-permute-start | bytes 20 | tf_op jit(solution)/shard_map/ppermute | solution.py:37
  50.5 14.1 %collective-permute-start.3 = (bf16[2,12,72,256]{3,2,1,0:T(8,128)(2,1)S(1)}, bf16[2,12,72,256]{3,2,1,0:T(8,128)(2,1)S(1)}, u32[]{:S(2)}, u32[]{:S(2)}) collective-permute-start(bf16[2,12,72,256]{3,2,1,0:T(8,128)(2,1)S(1)} %bitcast.108), channel_id=1, source_target_pairs={{0,1},{1,2},{2,3},{4,5},{5,6},{6,7},{8,9},{9,10},{10,11},{12,13},{... | collective-permute-start | bytes 2654216 | tf_op jit(solution)/shard_map/ppermute | solution.py:19
  52.2 12.4 %collective-permute-start.4 = (bf16[2,12,72,256]{3,2,1,0:T(8,128)(2,1)S(1)}, bf16[2,12,72,256]{3,2,1,0:T(8,128)(2,1)S(1)}, u32[]{:S(2)}, u32[]{:S(2)}) collective-permute-start(bf16[2,12,72,256]{3,2,1,0:T(8,128)(2,1)S(1)} %bitcast.109), channel_id=1, source_target_pairs={{1,0},{2,1},{3,2},{5,4},{6,5},{7,6},{9,8},{10,9},{11,10},{13,12},{... | collective-permute-start | bytes 2654216 | tf_op jit(solution)/shard_map/ppermute | solution.py:20
  63.5 32.8 %collective-permute-start.6 = (f32[2,2,2,2,48,768]{5,4,3,1,0,2:T(8,128)}, f32[2,2,2,2,48,768]{5,4,3,1,0,2:T(8,128)}, u32[]{:S(2)}, u32[]{:S(2)}) collective-permute-start(f32[2,2,2,2,48,768]{5,4,3,1,0,2:T(8,128)} %bitcast.105), channel_id=1, source_target_pairs={{0,1},{1,0},{2,3},{3,2},{4,5},{5,4},{6,7},{7,6},{8,9},{9,8},{10,11... | collective-permute-start | bytes 7077896 | tf_op jit(solution)/shard_map/ppermute | solution.py:37
  80.4 15.9 %collective-permute-start.7 = (f32[2,2,2,2,48,768]{5,4,3,2,0,1:T(8,128)}, f32[2,2,2,2,48,768]{5,4,3,2,0,1:T(8,128)}, u32[]{:S(2)}, u32[]{:S(2)}) collective-permute-start(f32[2,2,2,2,48,768]{5,4,3,2,0,1:T(8,128)} %bitcast.104), channel_id=1, source_target_pairs={{0,1},{1,0},{2,3},{3,2},{4,5},{5,4},{6,7},{7,6},{8,9},{9,8},{10,11... | collective-permute-start | bytes 7077896 | tf_op jit(solution)/shard_map/ppermute | solution.py:37
  86.2 10.1 %collective-permute-start.5 = (f32[2,2,2,2,48,768]{5,4,2,1,0,3:T(8,128)}, f32[2,2,2,2,48,768]{5,4,2,1,0,3:T(8,128)}, u32[]{:S(2)}, u32[]{:S(2)}) collective-permute-start(f32[2,2,2,2,48,768]{5,4,2,1,0,3:T(8,128)} %bitcast.106), channel_id=1, source_target_pairs={{0,1},{1,0},{2,3},{3,2},{4,5},{5,4},{6,7},{7,6},{8,9},{9,8},{10,11... | collective-permute-start | bytes 7077896 | tf_op jit(solution)/shard_map/ppermute | solution.py:37
  108.7 30.0 %collective-permute-start.10 = (f32[2,2,2,48,768]{4,3,2,1,0:T(8,128)}, f32[2,2,2,48,768]{4,3,2,1,0:T(8,128)}, u32[]{:S(2)}, u32[]{:S(2)}) collective-permute-start(f32[2,2,2,48,768]{4,3,2,1,0:T(8,128)} %dynamic-slice_bitcast_fusion), channel_id=1, source_target_pairs={{0,8},{4,12},{8,0},{12,4},{16,24},{20,28},{24,16},{28,20},{1,9},{5... | collective-permute-start | bytes 3538952 | tf_op jit(solution)/shard_map/ppermute | solution.py:37
  110.3 28.4 %collective-permute-start.8 = (f32[2,2,2,48,768]{4,3,2,1,0:T(8,128)}, f32[2,2,2,48,768]{4,3,2,1,0:T(8,128)}, u32[]{:S(2)}, u32[]{:S(2)}) collective-permute-start(f32[2,2,2,48,768]{4,3,2,1,0:T(8,128)} %dynamic-slice_bitcast_fusion.2), channel_id=1, source_target_pairs={{0,2},{1,3},{2,0},{3,1},{4,6},{5,7},{6,4},{7,5},{8,10},{9,11},{10,... | collective-permute-start | bytes 3538952 | tf_op jit(solution)/shard_map/ppermute | solution.py:37
  110.5 28.2 %collective-permute-start.9 = (f32[2,2,2,48,768]{4,3,2,1,0:T(8,128)S(1)}, f32[2,2,2,48,768]{4,3,2,1,0:T(8,128)}, u32[]{:S(2)}, u32[]{:S(2)}) collective-permute-start(f32[2,2,2,48,768]{4,3,2,1,0:T(8,128)S(1)} %dynamic-slice_bitcast_fusion.1), channel_id=1, source_target_pairs={{0,4},{4,0},{8,12},{12,8},{16,20},{20,16},{24,28},{28,24},{1,5},{5... | collective-permute-start | bytes 3538952 | tf_op jit(solution)/shard_map/ppermute | solution.py:37
  111.0 27.6 %collective-permute-start.11 = (f32[1281]{0:T(1024)S(1)}, f32[1281]{0:T(1024)}, u32[]{:S(2)}, u32[]{:S(2)}) collective-permute-start(f32[1281]{0:T(1024)S(1)} %pad_maximum_fusion.2), channel_id=1, source_target_pairs={{0,4},{4,0},{8,12},{12,8},{16,20},{20,16},{24,28},{28,24},{1,5},{5... | collective-permute-start | bytes 15380 | tf_op jit(solution)/shard_map/ppermute | solution.py:37
  143.9 15.1 %collective-permute-start.12 = (f32[2,2,48,768]{3,2,1,0:T(8,128)S(1)}, f32[2,2,48,768]{3,2,1,0:T(8,128)S(1)}, u32[]{:S(2)}, u32[]{:S(2)}) collective-permute-start(f32[2,2,48,768]{3,2,1,0:T(8,128)S(1)} %dynamic-slice_bitcast_fusion.5), channel_id=1, source_target_pairs={{0,4},{4,0},{8,12},{12,8},{16,20},{20,16},{24,28},{28,24},{1,5},{5... | collective-permute-start | bytes 1769480 | tf_op jit(solution)/shard_map/ppermute | solution.py:37
  144.5 14.5 %collective-permute-start.13 = (f32[2,2,48,768]{3,2,1,0:T(8,128)S(1)}, f32[2,2,48,768]{3,2,1,0:T(8,128)S(1)}, u32[]{:S(2)}, u32[]{:S(2)}) collective-permute-start(f32[2,2,48,768]{3,2,1,0:T(8,128)S(1)} %dynamic-slice_bitcast_fusion.4), channel_id=1, source_target_pairs={{0,8},{4,12},{8,0},{12,4},{16,24},{20,28},{24,16},{28,20},{1,9},{5... | collective-permute-start | bytes 1769480 | tf_op jit(solution)/shard_map/ppermute | solution.py:37
  144.8 14.3 %collective-permute-start.14 = (f32[2,2,48,768]{3,2,1,0:T(8,128)S(1)}, f32[2,2,48,768]{3,2,1,0:T(8,128)S(1)}, u32[]{:S(2)}, u32[]{:S(2)}) collective-permute-start(f32[2,2,48,768]{3,2,1,0:T(8,128)S(1)} %dynamic-slice_bitcast_fusion.3), channel_id=1, source_target_pairs={{0,2},{1,3},{2,0},{3,1},{4,6},{5,7},{6,4},{7,5},{8,10},{9,11},{10,... | collective-permute-start | bytes 1769480 | tf_op jit(solution)/shard_map/ppermute | solution.py:37
  146.5 12.5 %collective-permute-start.15 = (f32[1281]{0:T(1024)S(1)}, f32[1281]{0:T(1024)S(1)}, u32[]{:S(2)}, u32[]{:S(2)}) collective-permute-start(f32[1281]{0:T(1024)S(1)} %add.180), channel_id=1, source_target_pairs={{0,8},{4,12},{8,0},{12,4},{16,24},{20,28},{24,16},{28,20},{1,9},{5... | collective-permute-start | bytes 15380 | tf_op jit(solution)/shard_map/ppermute | solution.py:37
  159.5 15.8 %collective-permute-start.16 = (f32[2,48,768]{2,1,0:T(8,128)S(1)}, f32[2,48,768]{2,1,0:T(8,128)S(1)}, u32[]{:S(2)}, u32[]{:S(2)}) collective-permute-start(f32[2,48,768]{2,1,0:T(8,128)S(1)} %dynamic-slice_bitcast_fusion.8), channel_id=1, source_target_pairs={{0,8},{4,12},{8,0},{12,4},{16,24},{20,28},{24,16},{28,20},{1,9},{5... | collective-permute-start | bytes 884744 | tf_op jit(solution)/shard_map/ppermute | solution.py:37
  161.0 14.3 %collective-permute-start.17 = (f32[2,48,768]{2,1,0:T(8,128)S(1)}, f32[2,48,768]{2,1,0:T(8,128)S(1)}, u32[]{:S(2)}, u32[]{:S(2)}) collective-permute-start(f32[2,48,768]{2,1,0:T(8,128)S(1)} %dynamic-slice_bitcast_fusion.7), channel_id=1, source_target_pairs={{0,16},{4,20},{8,24},{12,28},{16,0},{20,4},{24,8},{28,12},{1,17},{... | collective-permute-start | bytes 884744 | tf_op jit(solution)/shard_map/ppermute | solution.py:37
  163.6 11.7 %collective-permute-start.18 = (f32[2,48,768]{2,1,0:T(8,128)S(1)}, f32[2,48,768]{2,1,0:T(8,128)S(1)}, u32[]{:S(2)}, u32[]{:S(2)}) collective-permute-start(f32[2,48,768]{2,1,0:T(8,128)S(1)} %dynamic-slice_bitcast_fusion.6), channel_id=1, source_target_pairs={{0,4},{4,0},{8,12},{12,8},{16,20},{20,16},{24,28},{28,24},{1,5},{5... | collective-permute-start | bytes 884744 | tf_op jit(solution)/shard_map/ppermute | solution.py:37
  165.1 10.2 %collective-permute-start.19 = (f32[1281]{0:T(1024)S(1)}, f32[1281]{0:T(1024)S(1)}, u32[]{:S(2)}, u32[]{:S(2)}) collective-permute-start(f32[1281]{0:T(1024)S(1)} %add.188), channel_id=1, source_target_pairs={{0,16},{4,20},{8,24},{12,28},{16,0},{20,4},{24,8},{28,12},{1,17},{... | collective-permute-start | bytes 15380 | tf_op jit(solution)/shard_map/ppermute | solution.py:37
  177.2 8.4 %collective-permute-start.22 = (f32[48,768]{1,0:T(8,128)S(1)}, f32[48,768]{1,0:T(8,128)S(1)}, u32[]{:S(2)}, u32[]{:S(2)}) collective-permute-start(f32[48,768]{1,0:T(8,128)S(1)} %dynamic-slice_bitcast_fusion.9), channel_id=1, source_target_pairs={{0,16},{4,20},{8,24},{12,28},{16,0},{20,4},{24,8},{28,12},{1,17},{... | collective-permute-start | bytes 442376 | tf_op jit(solution)/shard_map/ppermute | solution.py:37
  177.3 8.2 %collective-permute-start.21 = (f32[48,768]{1,0:T(8,128)S(1)}, f32[48,768]{1,0:T(8,128)S(1)}, u32[]{:S(2)}, u32[]{:S(2)}) collective-permute-start(f32[48,768]{1,0:T(8,128)S(1)} %dynamic-slice_bitcast_fusion.10), channel_id=1, source_target_pairs={{0,2},{1,3},{2,0},{3,1},{4,6},{5,7},{6,4},{7,5},{8,10},{9,11},{10,... | collective-permute-start | bytes 442376 | tf_op jit(solution)/shard_map/ppermute | solution.py:37
  178.7 10.0 %collective-permute-start.20 = (f32[48,768]{1,0:T(8,128)S(1)}, f32[48,768]{1,0:T(8,128)S(1)}, u32[]{:S(2)}, u32[]{:S(2)}) collective-permute-start(f32[48,768]{1,0:T(8,128)S(1)} %dynamic-slice_bitcast_fusion.11), channel_id=1, source_target_pairs={{0,16},{4,20},{8,24},{12,28},{16,0},{20,4},{24,8},{28,12},{1,17},{... | collective-permute-start | bytes 442376 | tf_op jit(solution)/shard_map/ppermute | solution.py:37
  (12 other events, 115.9 us)
where the time goes:
time: 192 us; the launch traced here: 191 us
  matrix products  41 us (21%)
  local copies, waits for them, and re-layouts  36.7 us (19%)
  starting transfers between devices  33.4 us (17%)
  other arithmetic  27.4 us (14%)
  waiting for transfers between devices  26.1 us (14%)
  blocking collectives  20.7 us (11%)
  between operations  5.5 us (3%)
    ppermute x21, starting transfers between devices, exchange(): return lax.ppermute(x, axis, pairs)  30.5 us
    ppermute x21, waiting for transfers between devices, exchange(): return lax.ppermute(x, axis, pairs)  26.1 us
    dot_general x2, matrix products, body(): lax.dot_general(shifted[h * share:(h + 1) * share].reshape(share, taps, o...  19.4 us
    slice x3, local copies, waits for them, and re-layouts, body(): shifted[h * share:(h + 1) * share].reshape(share, taps, out_chans)  16 us
    dot_general x3, matrix products, body(): lax.dot_general(flat_x, cols, (((0,), (0,)), ((), ())), preferred_element...  15.6 us
    add x14, other arithmetic, body(): pieces = [keeps[s] + received[s] for s in range(3)]  11.6 us
    psum x1, blocking collectives, body(): lax.psum(jnp.concatenate([jnp.sum(yvals, 0), jnp.sum(weights_pix)[None]])...  8.37 us
    psum x1, blocking collectives, body(): lax.psum((jnp.sum(preactivation_gradient, 0), jnp.sum(preactivation_gradi...  6.46 us
  transfers between devices with their start and end apart: 23, of which 8 were waited for; matrix products, arithmetic and copies ran while one was open for 38% of the time, Pallas kernels for 0%

commit v1 on v0

--- a/solution.py
+++ b/solution.py
@@ -155,12 +155,12 @@
         )
         parts.append(part.reshape((2,) * nbits + (rows, group_taps[s] * out_chans)))
 
-    halves = 2 if images % 2 == 0 else 1
-    share = local_pix // halves
+    halves = 2
+    share = in_chans // halves
     grad_chunks = [
         lax.dot_general(
-            shifted[h * share : (h + 1) * share].reshape(share, taps, out_chans),
-            conv_weight,
+            shifted.reshape(local_pix, taps, out_chans),
+            conv_weight[:, h * share : (h + 1) * share, :],
             (((1, 2), (0, 2)), ((), ())),
             preferred_element_type=jnp.float32,
         ).astype(jnp.bfloat16)
@@ -206,7 +206,7 @@
     grad_gain = packed[out_chans : 2 * out_chans]
     grad_class = packed[2 * out_chans : (2 + classes) * out_chans].reshape(classes, out_chans)
     loss = packed[(2 + classes) * out_chans] / mean_weight / all_pix
-    grad_features = jnp.concatenate(grad_chunks, 0).reshape(images, tile_rows, columns, in_chans)
+    grad_features = jnp.concatenate(grad_chunks, 1).reshape(images, tile_rows, columns, in_chans)
     return (grad_features, grad_weight, grad_gain, grad_shift, grad_class, loss)
 
 

time: 192 us -> 163 us (0.85)
  local copies, waits for them, and re-layouts: 36.7 us -> 7.91 us
  other arithmetic: 27.4 us -> 15.7 us
  waiting for transfers between devices: 26.1 us -> 35.6 us
    slice x3 -> x0, local copies, waits for them, and re-layouts: 16 us -> none  [body(): shifted[h * share:(h + 1) * share].reshape(share, taps, out_chans)]
    add x14, other arithmetic: 11.6 us -> 1.96 us  [body(): pieces = [keeps[s] + received[s] for s in range(3)]]
    ppermute x21, waiting for transfers between devices: 26.1 us -> 35.6 us  [exchange(): return lax.ppermute(x, axis, pairs)]
    dynamic_slice x3, local copies, waits for them, and re-layouts: 4.78 us -> 0.52 us  [body(): lax.dynamic_index_in_dim(p, 1 - mine, ax, keepdims=False)]
    unnamed x35 -> x23, local copies, waits for them, and re-layouts: 5.05 us -> 1.31 us
    dot_general x3, matrix products: 15.6 us -> 18.4 us  [body(): lax.dot_general(flat_x, cols, (((0,), (0,)), ((), ())), preferred_element...]
    dynamic_slice x3, local copies, waits for them, and re-layouts: 3.75 us -> 1.18 us  [body(): lax.dynamic_index_in_dim(p, mine, ax, keepdims=False)]
    dot_general x2, matrix products: 19.4 us -> 17.2 us  [body(): lax.dot_general(shifted.reshape(local_pix, taps, out_chans), conv_weight[...]
  transfers between devices with their start and end apart: 23 -> 23, of which waited for: 8 -> 9; matrix products, arithmetic and copies ran while one was open for 38% -> 30% of each run, Pallas kernels for 0% -> 0%
where the time goes in v1:
time: 163 us; the launch traced here: 161 us
  matrix products  41.6 us (26%)
  waiting for transfers between devices  35.6 us (22%)
  starting transfers between devices  34.5 us (21%)
  blocking collectives  20.7 us (13%)
  other arithmetic  15.7 us (10%)
  local copies, waits for them, and re-layouts  7.91 us (5%)
  between operations  5.35 us (3%)
    ppermute x21, waiting for transfers between devices, exchange(): return lax.ppermute(x, axis, pairs)  35.6 us
    ppermute x21, starting transfers between devices, exchange(): return lax.ppermute(x, axis, pairs)  31.5 us
    dot_general x3, matrix products, body(): lax.dot_general(flat_x, cols, (((0,), (0,)), ((), ())), preferred_element...  18.4 us
    dot_general x2, matrix products, body(): lax.dot_general(shifted.reshape(local_pix, taps, out_chans), conv_weight[...  17.2 us
    psum x1, blocking collectives, body(): lax.psum(jnp.concatenate([jnp.sum(yvals, 0), jnp.sum(weights_pix)[None]])...  8.37 us
    psum x1, blocking collectives, body(): lax.psum((jnp.sum(preactivation_gradient, 0), jnp.sum(preactivation_gradi...  6.46 us
    psum x1, blocking collectives, body(): lax.psum(jnp.sum(centre_offset * centre_offset, 0), 'tile')  5.84 us
    dot_general x1, matrix products, body(): grad_z = jnp.dot(grad_logit, class_map, precision=highest)  3.28 us
  transfers between devices with their start and end apart: 23, of which 9 were waited for; matrix products, arithmetic and copies ran while one was open for 30% of the time, Pallas kernels for 0%

profile of v1, /device:TPU:0, one launch (start us, length us, event | category | flops | bytes accessed | tf_op | source)
XLA Modules:
  0.0 161.3 jit_solution(9169081297159121826)
XLA Ops:
  5.0 8.4 %psum.42 = f32[257]{0:T(512)S(1)} all-reduce(f32[257]{0:T(512)S(1)} %pad_maximum_fusion.3), channel_id=1, replica_groups=mesh['rep'=8,'tile'=4] {'tile'}, use_global_device_ids=true, to_apply=%region_2.0 | all-reduce | flops 257 | bytes 2056 | tf_op jit(solution)/shard_map/psum | solution.py:83
  16.8 5.8 %psum.43 = f32[256]{0:T(256)S(1)} all-reduce(f32[256]{0:T(256)S(1)} %multiply_reduce_fusion.1), channel_id=1, replica_groups=mesh['rep'=8,'tile'=4] {'tile'}, use_global_device_ids=true, to_apply=%region_4.0 | all-reduce | flops 256 | bytes 2048 | tf_op jit(solution)/shard_map/psum | solution.py:87
  23.5 1.8 %fusion.46 = (f32[1728]{0:T(1024)S(1)}, f32[1728,3]{0,1:T(4,128)S(1)}) fusion(f32[3,256]{1,0:T(4,128)S(1)} %copy-done, f32[1728,256]{1,0:T(8,128)S(1)} %fusion.26, f32[256]{0:T(256)S(1)} %copy-done.4, f32[256]{0:T(256)S(1)} %copy-done.3), kind=kOutput, calls=%fused_computation.121 | convolution fusion | flops 17255808 | bytes 1802240 | tf_op jit(solution)/shard_map/dot_general | solution.py:92
  26.6 2.9 %collective-permute-start.1 = (f32[]{:T(128)}, f32[]{:T(128)}, u32[]{:S(2)}, u32[]{:S(2)}) collective-permute-start(f32[]{:T(128)} %add.168), channel_id=1, source_target_pairs={{0,8},{4,12},{8,0},{12,4},{16,24},{20,28},{24,16},{28,20},{1,9},{5... | collective-permute-start | bytes 20 | tf_op jit(solution)/shard_map/ppermute | solution.py:37
  30.8 4.0 %collective-permute-start.2 = (f32[]{:T(128)}, f32[]{:T(128)}, u32[]{:S(2)}, u32[]{:S(2)}) collective-permute-start(f32[]{:T(128)} %add.169), channel_id=1, source_target_pairs={{0,16},{4,20},{8,24},{12,28},{16,0},{20,4},{24,8},{28,12},{1,17},{... | collective-permute-start | bytes 20 | tf_op jit(solution)/shard_map/ppermute | solution.py:37
  36.6 3.3 %fusion.43 = (f32[256]{0:T(256)S(1)}, f32[256]{0:T(256)S(1)}, f32[1728,256]{1,0:T(8,128)}) fusion(f32[256]{0:T(256)S(1)} %get-tuple-element.114, f32[256]{0:T(256)S(1)} %slice_multiply_fusion, bf16[2,12,72,256]{3,2,1,0:T(8,128)(2,1)S(1)} %copy-done.2, f32[3,256]{1,0:T(4,128)S(1)} %copy-done, f32[1728,3]{0,1:T(4,128)S(1)} %get-tuple-element.116, ...), kind=kOutput, calls=%fused_computation.118 | convolution fusion | flops 20374336 | bytes 4474368 | tf_op jit(solution)/shard_map/dot_general | solution.py:100
  40.9 6.5 %all-reduce.2 = (f32[1]{0:T(128)}, f32[768]{0:T(1024)S(1)}, f32[256]{0:T(256)S(1)}, f32[256]{0:T(256)S(1)}) all-reduce(f32[1]{0:T(128)} %bitcast.3, f32[768]{0:T(1024)S(1)} %reshape.112, f32[256]{0:T(256)S(1)} %get-tuple-element.87, f32[256]{0:T(256)S(1)} %get-tuple-element.86), channel_id=1, replica_groups=mesh['rep'=8,'tile'=4] {'tile'}, use_global_device_ids=true, to_apply=%region_15.16 | all-reduce | flops 1281 | bytes 10248 | tf_op jit(solution)/shard_map/psum | solution.py:102
  47.4 2.0 %multiply_convert_fusion = bf16[1728,256]{1,0:T(8,128)(2,1)S(1)} fusion(f32[1728,256]{1,0:T(8,128)} %get-tuple-element.117, f32[256]{0:T(256)S(1)} %get-tuple-element.94, f32[256]{0:T(256)S(1)} %broadcast_multiply_fusion, f32[256]{0:T(256)S(1)} %get-tuple-element.113, f32[256]{0:T(256)S(1)} %get-tuple-element.114, f32[256]{0:T(256)S(1)} %slice_multiply_fusion, ...), kind=kLoop, calls=%fused_computation.40 | loop fusion | flops 3981312 | bytes 3544064 | tf_op jit(solution)/shard_map/convert_element_type | solution.py:122
  49.4 1.7 %collective-permute-start.3 = (bf16[2,12,72,256]{3,2,1,0:T(8,128)(2,1)S(1)}, bf16[2,12,72,256]{3,2,1,0:T(8,128)(2,1)S(1)}, u32[]{:S(2)}, u32[]{:S(2)}) collective-permute-start(bf16[2,12,72,256]{3,2,1,0:T(8,128)(2,1)S(1)} %bitcast.114), channel_id=1, source_target_pairs={{0,1},{1,2},{2,3},{4,5},{5,6},{6,7},{8,9},{9,10},{10,11},{12,13},{... | collective-permute-start | bytes 2654216 | tf_op jit(solution)/shard_map/ppermute | solution.py:19
  53.9 6.8 %fusion.14 = f32[1536,768]{1,0:T(8,128)S(1)} fusion(bf16[1728,1536]{1,0:T(8,128)(2,1)} %bitcast.143, bf16[1728,256]{1,0:T(8,128)(2,1)S(1)} %bitcast.134, bf16[1728,256]{1,0:T(8,128)(2,1)S(1)} %multiply_convert_fusion, bf16[1728,256]{1,0:T(8,128)(2,1)S(1)} %bitcast.136), kind=kOutput, calls=%fused_computation.20 | convolution fusion | flops 4084826112 | bytes 12681216 | tf_op jit(solution)/shard_map/dot_general | solution.py:153
  62.5 1.9 %fusion.5 = bf16[2,36,96,256]{3,2,1,0:T(8,128)(2,1)S(1)} fusion(bf16[2,12,72,256]{3,2,1,0:T(8,128)(2,1)S(1)} %collective-permute-done.4, bf16[2,12,72,256]{3,2,1,0:T(8,128)(2,1)S(1)} %bitcast.117, bf16[2,12,72,256]{3,2,1,0:T(8,128)(2,1)S(1)} %collective-permute-done.3), kind=kLoop, calls=%fused_computation.10 | loop fusion | flops 21233664 | bytes 6193152 | tf_op jit(solution)/shard_map/concatenate | solution.py:21
  64.8 4.7 %fusion.20 = f32[1536,768]{1,0:T(8,128)S(1)} fusion(bf16[1728,1536]{1,0:T(8,128)(2,1)S(1)} %bitcast.147, bf16[1728,256]{1,0:T(8,128)(2,1)S(1)} %bitcast.126, bf16[1728,256]{1,0:T(8,128)(2,1)S(1)} %bitcast.122, bf16[1728,256]{1,0:T(8,128)(2,1)S(1)} %bitcast.128), kind=kOutput, calls=%fused_computation.26 | convolution fusion | flops 4084826112 | bytes 12681216 | tf_op jit(solution)/shard_map/dot_general | solution.py:153
  70.1 3.6 %collective-permute-start.7 = (f32[2,2,2,2,48,768]{5,4,3,2,0,1:T(8,128)S(1)}, f32[2,2,2,2,48,768]{5,4,3,2,0,1:T(8,128)S(1)}, u32[]{:S(2)}, u32[]{:S(2)}) collective-permute-start(f32[2,2,2,2,48,768]{5,4,3,2,0,1:T(8,128)S(1)} %bitcast.139), channel_id=1, source_target_pairs={{0,1},{1,0},{2,3},{3,2},{4,5},{5,4},{6,7},{7,6},{8,9},{9,8},{10,11... | collective-permute-start | bytes 7077896 | tf_op jit(solution)/shard_map/ppermute | solution.py:37
  73.7 6.8 %fusion.8 = f32[1536,768]{1,0:T(8,128)S(1)} fusion(bf16[1728,1536]{1,0:T(8,128)(2,1)} %bitcast.144, bf16[1728,256]{1,0:T(8,128)(2,1)S(1)} %bitcast.130, bf16[1728,256]{1,0:T(8,128)(2,1)S(1)} %bitcast.124, bf16[1728,256]{1,0:T(8,128)(2,1)S(1)} %bitcast.132), kind=kOutput, calls=%fused_computation.14 | convolution fusion | flops 4084826112 | bytes 12681216 | tf_op jit(solution)/shard_map/dot_general | solution.py:153
  81.8 3.9 %collective-permute-done.5 = f32[2,2,2,2,48,768]{5,4,2,1,0,3:T(8,128)S(1)} collective-permute-done((f32[2,2,2,2,48,768]{5,4,2,1,0,3:T(8,128)S(1)}, f32[2,2,2,2,48,768]{5,4,2,1,0,3:T(8,128)S(1)}, u32[]{:S(2)}, u32[]{:S(2)}) %collective-permute-start.5) | collective-permute-done | bytes 2359328 | tf_op jit(solution)/shard_map/ppermute | solution.py:37
  90.7 8.6 %bitcast_convert_fusion.1 = bf16[1728,768]{1,0:T(8,128)(2,1)S(1)} fusion(bf16[1728,9,256]{2,0,1:T(8,128)(2,1)S(1)} %constant_dynamic-update-slice_fusion, bf16[9,1536,256]{2,1,0:T(8,128)(2,1)} %param.10), kind=kOutput, calls=%fused_computation.5 | convolution fusion | flops 6116622336 | bytes 14155776 | tf_op jit(solution)/shard_map/dot_general | solution.py:161
  99.3 17.3 %collective-permute-done.11 = f32[1281]{0:T(1024)S(1)} collective-permute-done((f32[1281]{0:T(1024)S(1)}, f32[1281]{0:T(1024)S(1)}, u32[]{:S(2)}, u32[]{:S(2)}) %collective-permute-start.11) | collective-permute-done | bytes 5156 | tf_op jit(solution)/shard_map/ppermute | solution.py:37
  121.7 8.6 %bitcast_convert_fusion = bf16[1728,768]{1,0:T(8,128)(2,1)S(1)} fusion(bf16[1728,9,256]{2,0,1:T(8,128)(2,1)S(1)} %constant_dynamic-update-slice_fusion, bf16[9,1536,256]{2,1,0:T(8,128)(2,1)} %param.10), kind=kOutput, calls=%fused_computation.4 | convolution fusion | flops 6116622336 | bytes 14155776 | tf_op jit(solution)/shard_map/dot_general | solution.py:161
  130.3 1.8 %collective-permute-done.15 = f32[1281]{0:T(1024)S(1)} collective-permute-done((f32[1281]{0:T(1024)S(1)}, f32[1281]{0:T(1024)S(1)}, u32[]{:S(2)}, u32[]{:S(2)}) %collective-permute-start.15) | collective-permute-done | bytes 5156 | tf_op jit(solution)/shard_map/ppermute | solution.py:37
  134.1 2.6 %collective-permute-start.17 = (f32[2,48,768]{2,1,0:T(8,128)S(1)}, f32[2,48,768]{2,1,0:T(8,128)S(1)}, u32[]{:S(2)}, u32[]{:S(2)}) collective-permute-start(f32[2,48,768]{2,1,0:T(8,128)S(1)} %dynamic-slice_bitcast_fusion.7), channel_id=1, source_target_pairs={{0,16},{4,20},{8,24},{12,28},{16,0},{20,4},{24,8},{28,12},{1,17},{... | collective-permute-start | bytes 884744 | tf_op jit(solution)/shard_map/ppermute | solution.py:37
  138.5 2.8 %pad_maximum_fusion = bf16[1728,1536]{1,0:T(8,128)(2,1)} fusion(bf16[1728,768]{1,0:T(8,128)(2,1)S(1)} %bitcast_convert_fusion, bf16[1728,768]{1,0:T(8,128)(2,1)S(1)} %bitcast_convert_fusion.1), kind=kLoop, calls=%fused_computation.3 | loop fusion | flops 10616832 | bytes 10616832 | tf_op jit(solution)/shard_map/concatenate | solution.py:209
  141.3 6.8 %collective-permute-done.19 = f32[1281]{0:T(1024)S(1)} collective-permute-done((f32[1281]{0:T(1024)S(1)}, f32[1281]{0:T(1024)S(1)}, u32[]{:S(2)}, u32[]{:S(2)}) %collective-permute-start.19) | collective-permute-done | bytes 5156 | tf_op jit(solution)/shard_map/ppermute | solution.py:37
  151.5 3.0 %collective-permute-start.20 = (f32[48,768]{1,0:T(8,128)S(1)}, f32[48,768]{1,0:T(8,128)S(1)}, u32[]{:S(2)}, u32[]{:S(2)}) collective-permute-start(f32[48,768]{1,0:T(8,128)S(1)} %dynamic-slice_bitcast_fusion.11), channel_id=1, source_target_pairs={{0,16},{4,20},{8,24},{12,28},{16,0},{20,4},{24,8},{28,12},{1,17},{... | collective-permute-start | bytes 442376 | tf_op jit(solution)/shard_map/ppermute | solution.py:37
  156.1 3.2 %collective-permute-done.20 = f32[48,768]{1,0:T(8,128)S(1)} collective-permute-done((f32[48,768]{1,0:T(8,128)S(1)}, f32[48,768]{1,0:T(8,128)S(1)}, u32[]{:S(2)}, u32[]{:S(2)}) %collective-permute-start.20) | collective-permute-done | bytes 147488 | tf_op jit(solution)/shard_map/ppermute | solution.py:37
  (119 shorter events, 37.5 us)
Async XLA Ops:
  0.6 22.9 %copy-start = (f32[3,256]{1,0:T(4,128)S(1)}, f32[3,256]{1,0:T(4,128)}, u32[]{:S(2)}) copy-start(f32[3,256]{1,0:T(4,128)} %param.13) | copy-start | bytes 9220
  13.9 11.5 %collective-permute-start = (f32[]{:T(128)}, f32[]{:T(128)}, u32[]{:S(2)}, u32[]{:S(2)}) collective-permute-start(f32[]{:T(128)} %bitcast.2), channel_id=1, source_target_pairs={{0,4},{4,0},{8,12},{12,8},{16,20},{20,16},{24,28},{28,24},{1,5},{5... | collective-permute-start | bytes 20 | tf_op jit(solution)/shard_map/ppermute | solution.py:37
  26.6 3.7 %collective-permute-start.1 = (f32[]{:T(128)}, f32[]{:T(128)}, u32[]{:S(2)}, u32[]{:S(2)}) collective-permute-start(f32[]{:T(128)} %add.168), channel_id=1, source_target_pairs={{0,8},{4,12},{8,0},{12,4},{16,24},{20,28},{24,16},{28,20},{1,9},{5... | collective-permute-start | bytes 20 | tf_op jit(solution)/shard_map/ppermute | solution.py:37
  30.8 4.6 %collective-permute-start.2 = (f32[]{:T(128)}, f32[]{:T(128)}, u32[]{:S(2)}, u32[]{:S(2)}) collective-permute-start(f32[]{:T(128)} %add.169), channel_id=1, source_target_pairs={{0,16},{4,20},{8,24},{12,28},{16,0},{20,4},{24,8},{28,12},{1,17},{... | collective-permute-start | bytes 20 | tf_op jit(solution)/shard_map/ppermute | solution.py:37
  49.4 13.1 %collective-permute-start.3 = (bf16[2,12,72,256]{3,2,1,0:T(8,128)(2,1)S(1)}, bf16[2,12,72,256]{3,2,1,0:T(8,128)(2,1)S(1)}, u32[]{:S(2)}, u32[]{:S(2)}) collective-permute-start(bf16[2,12,72,256]{3,2,1,0:T(8,128)(2,1)S(1)} %bitcast.114), channel_id=1, source_target_pairs={{0,1},{1,2},{2,3},{4,5},{5,6},{6,7},{8,9},{9,10},{10,11},{12,13},{... | collective-permute-start | bytes 2654216 | tf_op jit(solution)/shard_map/ppermute | solution.py:19
  51.1 11.4 %collective-permute-start.4 = (bf16[2,12,72,256]{3,2,1,0:T(8,128)(2,1)S(1)}, bf16[2,12,72,256]{3,2,1,0:T(8,128)(2,1)S(1)}, u32[]{:S(2)}, u32[]{:S(2)}) collective-permute-start(bf16[2,12,72,256]{3,2,1,0:T(8,128)(2,1)S(1)} %bitcast.115), channel_id=1, source_target_pairs={{1,0},{2,1},{3,2},{5,4},{6,5},{7,6},{9,8},{10,9},{11,10},{13,12},{... | collective-permute-start | bytes 2654216 | tf_op jit(solution)/shard_map/ppermute | solution.py:20
  61.3 20.6 %collective-permute-start.6 = (f32[2,2,2,2,48,768]{5,4,3,1,0,2:T(8,128)S(1)}, f32[2,2,2,2,48,768]{5,4,3,1,0,2:T(8,128)S(1)}, u32[]{:S(2)}, u32[]{:S(2)}) collective-permute-start(f32[2,2,2,2,48,768]{5,4,3,1,0,2:T(8,128)S(1)} %bitcast.138), channel_id=1, source_target_pairs={{0,1},{1,0},{2,3},{3,2},{4,5},{5,4},{6,7},{7,6},{8,9},{9,8},{10,11... | collective-permute-start | bytes 7077896 | tf_op jit(solution)/shard_map/ppermute | solution.py:37
  70.1 11.7 %collective-permute-start.7 = (f32[2,2,2,2,48,768]{5,4,3,2,0,1:T(8,128)S(1)}, f32[2,2,2,2,48,768]{5,4,3,2,0,1:T(8,128)S(1)}, u32[]{:S(2)}, u32[]{:S(2)}) collective-permute-start(f32[2,2,2,2,48,768]{5,4,3,2,0,1:T(8,128)S(1)} %bitcast.139), channel_id=1, source_target_pairs={{0,1},{1,0},{2,3},{3,2},{4,5},{5,4},{6,7},{7,6},{8,9},{9,8},{10,11... | collective-permute-start | bytes 7077896 | tf_op jit(solution)/shard_map/ppermute | solution.py:37
  81.1 4.6 %collective-permute-start.5 = (f32[2,2,2,2,48,768]{5,4,2,1,0,3:T(8,128)S(1)}, f32[2,2,2,2,48,768]{5,4,2,1,0,3:T(8,128)S(1)}, u32[]{:S(2)}, u32[]{:S(2)}) collective-permute-start(f32[2,2,2,2,48,768]{5,4,2,1,0,3:T(8,128)S(1)} %bitcast.140), channel_id=1, source_target_pairs={{0,1},{1,0},{2,3},{3,2},{4,5},{5,4},{6,7},{7,6},{8,9},{9,8},{10,11... | collective-permute-start | bytes 7077896 | tf_op jit(solution)/shard_map/ppermute | solution.py:37
  87.0 29.6 %collective-permute-start.10 = (f32[2,2,2,48,768]{4,3,2,1,0:T(8,128)S(1)}, f32[2,2,2,48,768]{4,3,2,1,0:T(8,128)S(1)}, u32[]{:S(2)}, u32[]{:S(2)}) collective-permute-start(f32[2,2,2,48,768]{4,3,2,1,0:T(8,128)S(1)} %dynamic-slice_bitcast_fusion), channel_id=1, source_target_pairs={{0,8},{4,12},{8,0},{12,4},{16,24},{20,28},{24,16},{28,20},{1,9},{5... | collective-permute-start | bytes 3538952 | tf_op jit(solution)/shard_map/ppermute | solution.py:37
  88.7 27.9 %collective-permute-start.8 = (f32[2,2,2,48,768]{4,3,2,1,0:T(8,128)S(1)}, f32[2,2,2,48,768]{4,3,2,1,0:T(8,128)S(1)}, u32[]{:S(2)}, u32[]{:S(2)}) collective-permute-start(f32[2,2,2,48,768]{4,3,2,1,0:T(8,128)S(1)} %dynamic-slice_bitcast_fusion.2), channel_id=1, source_target_pairs={{0,2},{1,3},{2,0},{3,1},{4,6},{5,7},{6,4},{7,5},{8,10},{9,11},{10,... | collective-permute-start | bytes 3538952 | tf_op jit(solution)/shard_map/ppermute | solution.py:37
  88.7 27.9 %collective-permute-start.9 = (f32[2,2,2,48,768]{4,3,2,1,0:T(8,128)S(1)}, f32[2,2,2,48,768]{4,3,2,1,0:T(8,128)S(1)}, u32[]{:S(2)}, u32[]{:S(2)}) collective-permute-start(f32[2,2,2,48,768]{4,3,2,1,0:T(8,128)S(1)} %dynamic-slice_bitcast_fusion.1), channel_id=1, source_target_pairs={{0,4},{4,0},{8,12},{12,8},{16,20},{20,16},{24,28},{28,24},{1,5},{5... | collective-permute-start | bytes 3538952 | tf_op jit(solution)/shard_map/ppermute | solution.py:37
  89.2 27.4 %collective-permute-start.11 = (f32[1281]{0:T(1024)S(1)}, f32[1281]{0:T(1024)S(1)}, u32[]{:S(2)}, u32[]{:S(2)}) collective-permute-start(f32[1281]{0:T(1024)S(1)} %pad_maximum_fusion.2), channel_id=1, source_target_pairs={{0,4},{4,0},{8,12},{12,8},{16,20},{20,16},{24,28},{28,24},{1,5},{5... | collective-permute-start | bytes 15380 | tf_op jit(solution)/shard_map/ppermute | solution.py:37
  117.4 14.7 %collective-permute-start.12 = (f32[2,2,48,768]{3,2,1,0:T(8,128)S(1)}, f32[2,2,48,768]{3,2,1,0:T(8,128)S(1)}, u32[]{:S(2)}, u32[]{:S(2)}) collective-permute-start(f32[2,2,48,768]{3,2,1,0:T(8,128)S(1)} %dynamic-slice_bitcast_fusion.5), channel_id=1, source_target_pairs={{0,4},{4,0},{8,12},{12,8},{16,20},{20,16},{24,28},{28,24},{1,5},{5... | collective-permute-start | bytes 1769480 | tf_op jit(solution)/shard_map/ppermute | solution.py:37
  118.0 14.1 %collective-permute-start.13 = (f32[2,2,48,768]{3,2,1,0:T(8,128)S(1)}, f32[2,2,48,768]{3,2,1,0:T(8,128)S(1)}, u32[]{:S(2)}, u32[]{:S(2)}) collective-permute-start(f32[2,2,48,768]{3,2,1,0:T(8,128)S(1)} %dynamic-slice_bitcast_fusion.4), channel_id=1, source_target_pairs={{0,8},{4,12},{8,0},{12,4},{16,24},{20,28},{24,16},{28,20},{1,9},{5... | collective-permute-start | bytes 1769480 | tf_op jit(solution)/shard_map/ppermute | solution.py:37
  118.4 13.8 %collective-permute-start.14 = (f32[2,2,48,768]{3,2,1,0:T(8,128)S(1)}, f32[2,2,48,768]{3,2,1,0:T(8,128)S(1)}, u32[]{:S(2)}, u32[]{:S(2)}) collective-permute-start(f32[2,2,48,768]{3,2,1,0:T(8,128)S(1)} %dynamic-slice_bitcast_fusion.3), channel_id=1, source_target_pairs={{0,2},{1,3},{2,0},{3,1},{4,6},{5,7},{6,4},{7,5},{8,10},{9,11},{10,... | collective-permute-start | bytes 1769480 | tf_op jit(solution)/shard_map/ppermute | solution.py:37
  120.1 12.0 %collective-permute-start.15 = (f32[1281]{0:T(1024)S(1)}, f32[1281]{0:T(1024)S(1)}, u32[]{:S(2)}, u32[]{:S(2)}) collective-permute-start(f32[1281]{0:T(1024)S(1)} %add.180), channel_id=1, source_target_pairs={{0,8},{4,12},{8,0},{12,4},{16,24},{20,28},{24,16},{28,20},{1,9},{5... | collective-permute-start | bytes 15380 | tf_op jit(solution)/shard_map/ppermute | solution.py:37
  132.6 15.6 %collective-permute-start.16 = (f32[2,48,768]{2,1,0:T(8,128)S(1)}, f32[2,48,768]{2,1,0:T(8,128)S(1)}, u32[]{:S(2)}, u32[]{:S(2)}) collective-permute-start(f32[2,48,768]{2,1,0:T(8,128)S(1)} %dynamic-slice_bitcast_fusion.8), channel_id=1, source_target_pairs={{0,8},{4,12},{8,0},{12,4},{16,24},{20,28},{24,16},{28,20},{1,9},{5... | collective-permute-start | bytes 884744 | tf_op jit(solution)/shard_map/ppermute | solution.py:37
  134.1 14.0 %collective-permute-start.17 = (f32[2,48,768]{2,1,0:T(8,128)S(1)}, f32[2,48,768]{2,1,0:T(8,128)S(1)}, u32[]{:S(2)}, u32[]{:S(2)}) collective-permute-start(f32[2,48,768]{2,1,0:T(8,128)S(1)} %dynamic-slice_bitcast_fusion.7), channel_id=1, source_target_pairs={{0,16},{4,20},{8,24},{12,28},{16,0},{20,4},{24,8},{28,12},{1,17},{... | collective-permute-start | bytes 884744 | tf_op jit(solution)/shard_map/ppermute | solution.py:37
  136.7 11.5 %collective-permute-start.18 = (f32[2,48,768]{2,1,0:T(8,128)S(1)}, f32[2,48,768]{2,1,0:T(8,128)S(1)}, u32[]{:S(2)}, u32[]{:S(2)}) collective-permute-start(f32[2,48,768]{2,1,0:T(8,128)S(1)} %dynamic-slice_bitcast_fusion.6), channel_id=1, source_target_pairs={{0,4},{4,0},{8,12},{12,8},{16,20},{20,16},{24,28},{28,24},{1,5},{5... | collective-permute-start | bytes 884744 | tf_op jit(solution)/shard_map/ppermute | solution.py:37
  138.2 10.0 %collective-permute-start.19 = (f32[1281]{0:T(1024)S(1)}, f32[1281]{0:T(1024)S(1)}, u32[]{:S(2)}, u32[]{:S(2)}) collective-permute-start(f32[1281]{0:T(1024)S(1)} %add.188), channel_id=1, source_target_pairs={{0,16},{4,20},{8,24},{12,28},{16,0},{20,4},{24,8},{28,12},{1,17},{... | collective-permute-start | bytes 15380 | tf_op jit(solution)/shard_map/ppermute | solution.py:37
  150.0 6.1 %collective-permute-start.22 = (f32[48,768]{1,0:T(8,128)S(1)}, f32[48,768]{1,0:T(8,128)S(1)}, u32[]{:S(2)}, u32[]{:S(2)}) collective-permute-start(f32[48,768]{1,0:T(8,128)S(1)} %dynamic-slice_bitcast_fusion.9), channel_id=1, source_target_pairs={{0,16},{4,20},{8,24},{12,28},{16,0},{20,4},{24,8},{28,12},{1,17},{... | collective-permute-start | bytes 442376 | tf_op jit(solution)/shard_map/ppermute | solution.py:37
  150.2 5.9 %collective-permute-start.21 = (f32[48,768]{1,0:T(8,128)S(1)}, f32[48,768]{1,0:T(8,128)S(1)}, u32[]{:S(2)}, u32[]{:S(2)}) collective-permute-start(f32[48,768]{1,0:T(8,128)S(1)} %dynamic-slice_bitcast_fusion.10), channel_id=1, source_target_pairs={{0,2},{1,3},{2,0},{3,1},{4,6},{5,7},{6,4},{7,5},{8,10},{9,11},{10,... | collective-permute-start | bytes 442376 | tf_op jit(solution)/shard_map/ppermute | solution.py:37
  151.5 7.8 %collective-permute-start.20 = (f32[48,768]{1,0:T(8,128)S(1)}, f32[48,768]{1,0:T(8,128)S(1)}, u32[]{:S(2)}, u32[]{:S(2)}) collective-permute-start(f32[48,768]{1,0:T(8,128)S(1)} %dynamic-slice_bitcast_fusion.11), channel_id=1, source_target_pairs={{0,16},{4,20},{8,24},{12,28},{16,0},{20,4},{24,8},{28,12},{1,17},{... | collective-permute-start | bytes 442376 | tf_op jit(solution)/shard_map/ppermute | solution.py:37
  (6 other events, 85.7 us)

commit v2 on v1

--- a/solution.py
+++ b/solution.py
@@ -80,11 +80,23 @@
     weights_pix = jnp.sum(onehot * class_weight.astype(jnp.float32), -1)
 
     yvals = conv_out.astype(jnp.float32).reshape(local_pix, out_chans)
-    first_sums = lax.psum(jnp.concatenate([jnp.sum(yvals, 0), jnp.sum(weights_pix)[None]]), "tile")
-    column_sum, weight_tile = first_sums[:out_chans], first_sums[out_chans]
-    weight_total = butterfly_sum(weight_tile, ("rep",))
+    tiles = lax.axis_size("tile")
+    local_sum = jnp.sum(yvals, 0)
+    local_offset = yvals - local_sum / local_pix
+    local_stats = jnp.concatenate(
+        [local_sum, jnp.sum(local_offset * local_offset, 0), jnp.sum(weights_pix)[None]]
+    )
+    slot = (jnp.arange(tiles) == lax.axis_index("tile")).astype(jnp.float32)
+    tile_stats = lax.psum(slot[:, None] * local_stats[None, :], "tile")
+    tile_sums = tile_stats[:, :out_chans]
+    column_sum = jnp.sum(tile_sums, 0)
+    tile_means = tile_sums / local_pix - column_sum / per_replica_part
+    variance = (
+        jnp.sum(tile_stats[:, out_chans : 2 * out_chans] + local_pix * tile_means * tile_means, 0)
+        / per_replica_part
+    )
+    weight_total = butterfly_sum(jnp.sum(tile_stats[:, 2 * out_chans]), ("rep",))
     centre_offset = yvals - column_sum / per_replica_part
-    variance = lax.psum(jnp.sum(centre_offset * centre_offset, 0), "tile") / per_replica_part
     inverse_deviation = lax.rsqrt(variance + 1e-05)
     normalized_input = centre_offset * inverse_deviation
     preactivation_values = norm_gain_vector * normalized_input + norm_shift_vector

time: 163 us -> 163 us (level)
    psum x2 -> x1, blocking collectives: 14.2 us -> 12.6 us  [body(): tile_stats = lax.psum(slot[:, None] * local_stats[None, :], 'tile')]
    reduce_sum x2 -> x5, other arithmetic: 2.87 us -> 3.51 us  [the longest x1 1.46 us: body(): jnp.sum(local_offset * local_offset, 0)]
  transfers between devices with their start and end apart: 23 -> 23, of which waited for: 9 -> 8; matrix products, arithmetic and copies ran while one was open for 30% -> 30% of each run, Pallas kernels for 0% -> 0%
where the time goes in v2:
time: 163 us; the launch traced here: 161 us
  matrix products  41.6 us (26%)
  waiting for transfers between devices  36.1 us (22%)
  starting transfers between devices  34.6 us (21%)
  blocking collectives  19.2 us (12%)
  other arithmetic  16.4 us (10%)
  local copies, waits for them, and re-layouts  7.39 us (5%)
  between operations  5.59 us (3%)
    ppermute x21, waiting for transfers between devices, exchange(): return lax.ppermute(x, axis, pairs)  36.1 us
    ppermute x21, starting transfers between devices, exchange(): return lax.ppermute(x, axis, pairs)  31.7 us
    dot_general x3, matrix products, body(): lax.dot_general(flat_x, cols, (((0,), (0,)), ((), ())), preferred_element...  18.4 us
    dot_general x2, matrix products, body(): lax.dot_general(shifted.reshape(local_pix, taps, out_chans), conv_weight[...  17.2 us
    psum x1, blocking collectives, body(): tile_stats = lax.psum(slot[:, None] * local_stats[None, :], 'tile')  12.6 us
    psum x1, blocking collectives, body(): lax.psum((jnp.sum(preactivation_gradient, 0), jnp.sum(preactivation_gradi...  6.56 us
    dot_general x1, matrix products, body(): grad_z = jnp.dot(grad_logit, class_map, precision=highest)  3.28 us
  transfers between devices with their start and end apart: 23, of which 8 were waited for; matrix products, arithmetic and copies ran while one was open for 30% of the time, Pallas kernels for 0%

profile of v2, /device:TPU:0, one launch (start us, length us, event | category | flops | bytes accessed | tf_op | source)
XLA Modules:
  0.0 160.9 jit_solution(10395384154006890632)
XLA Ops:
  6.5 12.6 %psum.35 = f32[4,513]{1,0:T(4,128)S(1)} all-reduce(f32[4,513]{1,0:T(4,128)S(1)} %broadcast_multiply_fusion), channel_id=1, replica_groups=mesh['rep'=8,'tile'=4] {'tile'}, use_global_device_ids=true, to_apply=%region_3.0 | all-reduce | flops 2052 | bytes 16416 | tf_op jit(solution)/shard_map/psum | solution.py:90
  22.2 1.8 %fusion.48 = (f32[1728]{0:T(1024)S(1)}, f32[1728,3]{0,1:T(4,128)S(1)}) fusion(f32[3,256]{1,0:T(4,128)S(1)} %copy-done, f32[1728,256]{1,0:T(8,128)S(1)} %fusion.26, f32[256]{0:T(256)S(1)} %copy-done.4, f32[256]{0:T(256)S(1)} %copy-done.3), kind=kOutput, calls=%fused_computation.129 | convolution fusion | flops 17255808 | bytes 1802240 | tf_op jit(solution)/shard_map/dot_general | solution.py:104
  25.3 2.9 %collective-permute-start.1 = (f32[]{:T(128)}, f32[]{:T(128)}, u32[]{:S(2)}, u32[]{:S(2)}) collective-permute-start(f32[]{:T(128)} %add.174), channel_id=1, source_target_pairs={{0,8},{4,12},{8,0},{12,4},{16,24},{20,28},{24,16},{28,20},{1,9},{5... | collective-permute-start | bytes 20 | tf_op jit(solution)/shard_map/ppermute | solution.py:37
  29.6 4.0 %collective-permute-start.2 = (f32[]{:T(128)}, f32[]{:T(128)}, u32[]{:S(2)}, u32[]{:S(2)}) collective-permute-start(f32[]{:T(128)} %add.175), channel_id=1, source_target_pairs={{0,16},{4,20},{8,24},{12,28},{16,0},{20,4},{24,8},{28,12},{1,17},{... | collective-permute-start | bytes 20 | tf_op jit(solution)/shard_map/ppermute | solution.py:37
  35.5 3.3 %fusion.45 = (f32[256]{0:T(256)S(1)}, f32[256]{0:T(256)S(1)}, f32[1728,256]{1,0:T(8,128)}) fusion(f32[256]{0:T(256)S(1)} %get-tuple-element.126, f32[256]{0:T(256)S(1)} %broadcast_multiply_fusion.2, bf16[2,12,72,256]{3,2,1,0:T(8,128)(2,1)S(1)} %copy-done.2, f32[3,256]{1,0:T(4,128)S(1)} %copy-done, f32[1728,3]{0,1:T(4,128)S(1)} %get-tuple-element.128, ...), kind=kOutput, calls=%fused_computation.126 | convolution fusion | flops 20374336 | bytes 4474368 | tf_op jit(solution)/shard_map/dot_general | solution.py:112
  39.8 6.6 %all-reduce.2 = (f32[1]{0:T(128)}, f32[768]{0:T(1024)S(1)}, f32[256]{0:T(256)S(1)}, f32[256]{0:T(256)S(1)}) all-reduce(f32[1]{0:T(128)} %bitcast.2, f32[768]{0:T(1024)S(1)} %reshape.128, f32[256]{0:T(256)S(1)} %get-tuple-element.99, f32[256]{0:T(256)S(1)} %get-tuple-element.98), channel_id=1, replica_groups=mesh['rep'=8,'tile'=4] {'tile'}, use_global_device_ids=true, to_apply=%region_17.18 | all-reduce | flops 1281 | bytes 10248 | tf_op jit(solution)/shard_map/psum | solution.py:114
  46.4 2.0 %multiply_convert_fusion = bf16[1728,256]{1,0:T(8,128)(2,1)S(1)} fusion(f32[1728,256]{1,0:T(8,128)} %get-tuple-element.129, f32[256]{0:T(256)S(1)} %get-tuple-element.106, f32[256]{0:T(256)S(1)} %broadcast_multiply_fusion.1, f32[256]{0:T(256)S(1)} %get-tuple-element.125, f32[256]{0:T(256)S(1)} %get-tuple-element.126, f32[256]{0:T(256)S(1)} %broadcast_multiply_fusion.2, ...), kind=kLoop, calls=%fused_computation.40 | loop fusion | flops 3981312 | bytes 3544064 | tf_op jit(solution)/shard_map/convert_element_type | solution.py:134
  52.8 6.8 %fusion.14 = f32[1536,768]{1,0:T(8,128)S(1)} fusion(bf16[1728,1536]{1,0:T(8,128)(2,1)} %bitcast.142, bf16[1728,256]{1,0:T(8,128)(2,1)S(1)} %bitcast.133, bf16[1728,256]{1,0:T(8,128)(2,1)S(1)} %multiply_convert_fusion, bf16[1728,256]{1,0:T(8,128)(2,1)S(1)} %bitcast.135), kind=kOutput, calls=%fused_computation.20 | convolution fusion | flops 4084826112 | bytes 12681216 | tf_op jit(solution)/shard_map/dot_general | solution.py:165
  61.6 1.9 %fusion.5 = bf16[2,36,96,256]{3,2,1,0:T(8,128)(2,1)S(1)} fusion(bf16[2,12,72,256]{3,2,1,0:T(8,128)(2,1)S(1)} %collective-permute-done.4, bf16[2,12,72,256]{3,2,1,0:T(8,128)(2,1)S(1)} %bitcast.116, bf16[2,12,72,256]{3,2,1,0:T(8,128)(2,1)S(1)} %collective-permute-done.3), kind=kLoop, calls=%fused_computation.10 | loop fusion | flops 21233664 | bytes 6193152 | tf_op jit(solution)/shard_map/concatenate | solution.py:21
  63.8 4.7 %fusion.20 = f32[1536,768]{1,0:T(8,128)S(1)} fusion(bf16[1728,1536]{1,0:T(8,128)(2,1)S(1)} %bitcast.146, bf16[1728,256]{1,0:T(8,128)(2,1)S(1)} %bitcast.125, bf16[1728,256]{1,0:T(8,128)(2,1)S(1)} %bitcast.121, bf16[1728,256]{1,0:T(8,128)(2,1)S(1)} %bitcast.127), kind=kOutput, calls=%fused_computation.26 | convolution fusion | flops 4084826112 | bytes 12681216 | tf_op jit(solution)/shard_map/dot_general | solution.py:165
  69.2 3.6 %collective-permute-start.7 = (f32[2,2,2,2,48,768]{5,4,3,2,0,1:T(8,128)S(1)}, f32[2,2,2,2,48,768]{5,4,3,2,0,1:T(8,128)S(1)}, u32[]{:S(2)}, u32[]{:S(2)}) collective-permute-start(f32[2,2,2,2,48,768]{5,4,3,2,0,1:T(8,128)S(1)} %bitcast.138), channel_id=1, source_target_pairs={{0,1},{1,0},{2,3},{3,2},{4,5},{5,4},{6,7},{7,6},{8,9},{9,8},{10,11... | collective-permute-start | bytes 7077896 | tf_op jit(solution)/shard_map/ppermute | solution.py:37
  72.7 6.8 %fusion.8 = f32[1536,768]{1,0:T(8,128)S(1)} fusion(bf16[1728,1536]{1,0:T(8,128)(2,1)} %bitcast.143, bf16[1728,256]{1,0:T(8,128)(2,1)S(1)} %bitcast.129, bf16[1728,256]{1,0:T(8,128)(2,1)S(1)} %bitcast.123, bf16[1728,256]{1,0:T(8,128)(2,1)S(1)} %bitcast.131), kind=kOutput, calls=%fused_computation.14 | convolution fusion | flops 4084826112 | bytes 12681216 | tf_op jit(solution)/shard_map/dot_general | solution.py:165
  80.9 3.9 %collective-permute-done.5 = f32[2,2,2,2,48,768]{5,4,2,1,0,3:T(8,128)S(1)} collective-permute-done((f32[2,2,2,2,48,768]{5,4,2,1,0,3:T(8,128)S(1)}, f32[2,2,2,2,48,768]{5,4,2,1,0,3:T(8,128)S(1)}, u32[]{:S(2)}, u32[]{:S(2)}) %collective-permute-start.5) | collective-permute-done | bytes 2359328 | tf_op jit(solution)/shard_map/ppermute | solution.py:37
  86.1 1.6 %collective-permute-start.10 = (f32[2,2,2,48,768]{4,3,2,1,0:T(8,128)S(1)}, f32[2,2,2,48,768]{4,3,2,1,0:T(8,128)S(1)}, u32[]{:S(2)}, u32[]{:S(2)}) collective-permute-start(f32[2,2,2,48,768]{4,3,2,1,0:T(8,128)S(1)} %dynamic-slice_bitcast_fusion), channel_id=1, source_target_pairs={{0,8},{4,12},{8,0},{12,4},{16,24},{20,28},{24,16},{28,20},{1,9},{5... | collective-permute-start | bytes 3538952 | tf_op jit(solution)/shard_map/ppermute | solution.py:37
  89.8 8.6 %bitcast_convert_fusion.1 = bf16[1728,768]{1,0:T(8,128)(2,1)S(1)} fusion(bf16[1728,9,256]{2,0,1:T(8,128)(2,1)S(1)} %constant_dynamic-update-slice_fusion, bf16[9,1536,256]{2,1,0:T(8,128)(2,1)} %param.10), kind=kOutput, calls=%fused_computation.5 | convolution fusion | flops 6116622336 | bytes 14155776 | tf_op jit(solution)/shard_map/dot_general | solution.py:173
  98.3 17.3 %collective-permute-done.11 = f32[1281]{0:T(1024)S(1)} collective-permute-done((f32[1281]{0:T(1024)S(1)}, f32[1281]{0:T(1024)S(1)}, u32[]{:S(2)}, u32[]{:S(2)}) %collective-permute-start.11) | collective-permute-done | bytes 5156 | tf_op jit(solution)/shard_map/ppermute | solution.py:37
  117.9 1.7 %collective-permute-start.14 = (f32[2,2,48,768]{3,2,1,0:T(8,128)S(1)}, f32[2,2,48,768]{3,2,1,0:T(8,128)S(1)}, u32[]{:S(2)}, u32[]{:S(2)}) collective-permute-start(f32[2,2,48,768]{3,2,1,0:T(8,128)S(1)} %dynamic-slice_bitcast_fusion.3), channel_id=1, source_target_pairs={{0,2},{1,3},{2,0},{3,1},{4,6},{5,7},{6,4},{7,5},{8,10},{9,11},{10,... | collective-permute-start | bytes 1769480 | tf_op jit(solution)/shard_map/ppermute | solution.py:37
  121.3 8.6 %bitcast_convert_fusion = bf16[1728,768]{1,0:T(8,128)(2,1)S(1)} fusion(bf16[1728,9,256]{2,0,1:T(8,128)(2,1)S(1)} %constant_dynamic-update-slice_fusion, bf16[9,1536,256]{2,1,0:T(8,128)(2,1)} %param.10), kind=kOutput, calls=%fused_computation.4 | convolution fusion | flops 6116622336 | bytes 14155776 | tf_op jit(solution)/shard_map/dot_general | solution.py:173
  129.8 1.8 %collective-permute-done.15 = f32[1281]{0:T(1024)S(1)} collective-permute-done((f32[1281]{0:T(1024)S(1)}, f32[1281]{0:T(1024)S(1)}, u32[]{:S(2)}, u32[]{:S(2)}) %collective-permute-start.15) | collective-permute-done | bytes 5156 | tf_op jit(solution)/shard_map/ppermute | solution.py:37
  133.6 2.6 %collective-permute-start.17 = (f32[2,48,768]{2,1,0:T(8,128)S(1)}, f32[2,48,768]{2,1,0:T(8,128)S(1)}, u32[]{:S(2)}, u32[]{:S(2)}) collective-permute-start(f32[2,48,768]{2,1,0:T(8,128)S(1)} %dynamic-slice_bitcast_fusion.7), channel_id=1, source_target_pairs={{0,16},{4,20},{8,24},{12,28},{16,0},{20,4},{24,8},{28,12},{1,17},{... | collective-permute-start | bytes 884744 | tf_op jit(solution)/shard_map/ppermute | solution.py:37
  137.6 2.8 %pad_maximum_fusion = bf16[1728,1536]{1,0:T(8,128)(2,1)} fusion(bf16[1728,768]{1,0:T(8,128)(2,1)S(1)} %bitcast_convert_fusion, bf16[1728,768]{1,0:T(8,128)(2,1)S(1)} %bitcast_convert_fusion.1), kind=kLoop, calls=%fused_computation.3 | loop fusion | flops 10616832 | bytes 10616832 | tf_op jit(solution)/shard_map/concatenate | solution.py:221
  140.4 7.3 %collective-permute-done.19 = f32[1281]{0:T(1024)S(1)} collective-permute-done((f32[1281]{0:T(1024)S(1)}, f32[1281]{0:T(1024)S(1)}, u32[]{:S(2)}, u32[]{:S(2)}) %collective-permute-start.19) | collective-permute-done | bytes 5156 | tf_op jit(solution)/shard_map/ppermute | solution.py:37
  150.9 3.0 %collective-permute-start.20 = (f32[48,768]{1,0:T(8,128)S(1)}, f32[48,768]{1,0:T(8,128)S(1)}, u32[]{:S(2)}, u32[]{:S(2)}) collective-permute-start(f32[48,768]{1,0:T(8,128)S(1)} %dynamic-slice_bitcast_fusion.11), channel_id=1, source_target_pairs={{0,16},{4,20},{8,24},{12,28},{16,0},{20,4},{24,8},{28,12},{1,17},{... | collective-permute-start | bytes 442376 | tf_op jit(solution)/shard_map/ppermute | solution.py:37
  155.6 3.2 %collective-permute-done.20 = f32[48,768]{1,0:T(8,128)S(1)} collective-permute-done((f32[48,768]{1,0:T(8,128)S(1)}, f32[48,768]{1,0:T(8,128)S(1)}, u32[]{:S(2)}, u32[]{:S(2)}) %collective-permute-start.20) | collective-permute-done | bytes 147488 | tf_op jit(solution)/shard_map/ppermute | solution.py:37
  (123 shorter events, 36.0 us)
Async XLA Ops:
  0.6 21.5 %copy-start = (f32[3,256]{1,0:T(4,128)S(1)}, f32[3,256]{1,0:T(4,128)}, u32[]{:S(2)}) copy-start(f32[3,256]{1,0:T(4,128)} %param.13) | copy-start | bytes 9220
  19.8 4.3 %collective-permute-start = (f32[]{:T(128)}, f32[]{:T(128)}, u32[]{:S(2)}, u32[]{:S(2)}) collective-permute-start(f32[]{:T(128)} %slice_reduce_fusion.1), channel_id=1, source_target_pairs={{0,4},{4,0},{8,12},{12,8},{16,20},{20,16},{24,28},{28,24},{1,5},{5... | collective-permute-start | bytes 20 | tf_op jit(solution)/shard_map/ppermute | solution.py:37
  25.3 3.7 %collective-permute-start.1 = (f32[]{:T(128)}, f32[]{:T(128)}, u32[]{:S(2)}, u32[]{:S(2)}) collective-permute-start(f32[]{:T(128)} %add.174), channel_id=1, source_target_pairs={{0,8},{4,12},{8,0},{12,4},{16,24},{20,28},{24,16},{28,20},{1,9},{5... | collective-permute-start | bytes 20 | tf_op jit(solution)/shard_map/ppermute | solution.py:37
  29.6 4.6 %collective-permute-start.2 = (f32[]{:T(128)}, f32[]{:T(128)}, u32[]{:S(2)}, u32[]{:S(2)}) collective-permute-start(f32[]{:T(128)} %add.175), channel_id=1, source_target_pairs={{0,16},{4,20},{8,24},{12,28},{16,0},{20,4},{24,8},{28,12},{1,17},{... | collective-permute-start | bytes 20 | tf_op jit(solution)/shard_map/ppermute | solution.py:37
  48.4 13.2 %collective-permute-start.3 = (bf16[2,12,72,256]{3,2,1,0:T(8,128)(2,1)S(1)}, bf16[2,12,72,256]{3,2,1,0:T(8,128)(2,1)S(1)}, u32[]{:S(2)}, u32[]{:S(2)}) collective-permute-start(bf16[2,12,72,256]{3,2,1,0:T(8,128)(2,1)S(1)} %bitcast.113), channel_id=1, source_target_pairs={{0,1},{1,2},{2,3},{4,5},{5,6},{6,7},{8,9},{9,10},{10,11},{12,13},{... | collective-permute-start | bytes 2654216 | tf_op jit(solution)/shard_map/ppermute | solution.py:19
  50.0 11.6 %collective-permute-start.4 = (bf16[2,12,72,256]{3,2,1,0:T(8,128)(2,1)S(1)}, bf16[2,12,72,256]{3,2,1,0:T(8,128)(2,1)S(1)}, u32[]{:S(2)}, u32[]{:S(2)}) collective-permute-start(bf16[2,12,72,256]{3,2,1,0:T(8,128)(2,1)S(1)} %bitcast.114), channel_id=1, source_target_pairs={{1,0},{2,1},{3,2},{5,4},{6,5},{7,6},{9,8},{10,9},{11,10},{13,12},{... | collective-permute-start | bytes 2654216 | tf_op jit(solution)/shard_map/ppermute | solution.py:20
  60.1 20.7 %collective-permute-start.6 = (f32[2,2,2,2,48,768]{5,4,3,1,0,2:T(8,128)S(1)}, f32[2,2,2,2,48,768]{5,4,3,1,0,2:T(8,128)S(1)}, u32[]{:S(2)}, u32[]{:S(2)}) collective-permute-start(f32[2,2,2,2,48,768]{5,4,3,1,0,2:T(8,128)S(1)} %bitcast.137), channel_id=1, source_target_pairs={{0,1},{1,0},{2,3},{3,2},{4,5},{5,4},{6,7},{7,6},{8,9},{9,8},{10,11... | collective-permute-start | bytes 7077896 | tf_op jit(solution)/shard_map/ppermute | solution.py:37
  69.2 11.7 %collective-permute-start.7 = (f32[2,2,2,2,48,768]{5,4,3,2,0,1:T(8,128)S(1)}, f32[2,2,2,2,48,768]{5,4,3,2,0,1:T(8,128)S(1)}, u32[]{:S(2)}, u32[]{:S(2)}) collective-permute-start(f32[2,2,2,2,48,768]{5,4,3,2,0,1:T(8,128)S(1)} %bitcast.138), channel_id=1, source_target_pairs={{0,1},{1,0},{2,3},{3,2},{4,5},{5,4},{6,7},{7,6},{8,9},{9,8},{10,11... | collective-permute-start | bytes 7077896 | tf_op jit(solution)/shard_map/ppermute | solution.py:37
  80.2 4.6 %collective-permute-start.5 = (f32[2,2,2,2,48,768]{5,4,2,1,0,3:T(8,128)S(1)}, f32[2,2,2,2,48,768]{5,4,2,1,0,3:T(8,128)S(1)}, u32[]{:S(2)}, u32[]{:S(2)}) collective-permute-start(f32[2,2,2,2,48,768]{5,4,2,1,0,3:T(8,128)S(1)} %bitcast.139), channel_id=1, source_target_pairs={{0,1},{1,0},{2,3},{3,2},{4,5},{5,4},{6,7},{7,6},{8,9},{9,8},{10,11... | collective-permute-start | bytes 7077896 | tf_op jit(solution)/shard_map/ppermute | solution.py:37
  86.1 29.6 %collective-permute-start.10 = (f32[2,2,2,48,768]{4,3,2,1,0:T(8,128)S(1)}, f32[2,2,2,48,768]{4,3,2,1,0:T(8,128)S(1)}, u32[]{:S(2)}, u32[]{:S(2)}) collective-permute-start(f32[2,2,2,48,768]{4,3,2,1,0:T(8,128)S(1)} %dynamic-slice_bitcast_fusion), channel_id=1, source_target_pairs={{0,8},{4,12},{8,0},{12,4},{16,24},{20,28},{24,16},{28,20},{1,9},{5... | collective-permute-start | bytes 3538952 | tf_op jit(solution)/shard_map/ppermute | solution.py:37
  87.7 27.9 %collective-permute-start.8 = (f32[2,2,2,48,768]{4,3,2,1,0:T(8,128)S(1)}, f32[2,2,2,48,768]{4,3,2,1,0:T(8,128)S(1)}, u32[]{:S(2)}, u32[]{:S(2)}) collective-permute-start(f32[2,2,2,48,768]{4,3,2,1,0:T(8,128)S(1)} %dynamic-slice_bitcast_fusion.2), channel_id=1, source_target_pairs={{0,2},{1,3},{2,0},{3,1},{4,6},{5,7},{6,4},{7,5},{8,10},{9,11},{10,... | collective-permute-start | bytes 3538952 | tf_op jit(solution)/shard_map/ppermute | solution.py:37
  87.7 27.9 %collective-permute-start.9 = (f32[2,2,2,48,768]{4,3,2,1,0:T(8,128)S(1)}, f32[2,2,2,48,768]{4,3,2,1,0:T(8,128)S(1)}, u32[]{:S(2)}, u32[]{:S(2)}) collective-permute-start(f32[2,2,2,48,768]{4,3,2,1,0:T(8,128)S(1)} %dynamic-slice_bitcast_fusion.1), channel_id=1, source_target_pairs={{0,4},{4,0},{8,12},{12,8},{16,20},{20,16},{24,28},{28,24},{1,5},{5... | collective-permute-start | bytes 3538952 | tf_op jit(solution)/shard_map/ppermute | solution.py:37
  88.7 26.9 %collective-permute-start.11 = (f32[1281]{0:T(1024)S(1)}, f32[1281]{0:T(1024)S(1)}, u32[]{:S(2)}, u32[]{:S(2)}) collective-permute-start(f32[1281]{0:T(1024)S(1)} %pad_maximum_fusion.2), channel_id=1, source_target_pairs={{0,4},{4,0},{8,12},{12,8},{16,20},{20,16},{24,28},{28,24},{1,5},{5... | collective-permute-start | bytes 15380 | tf_op jit(solution)/shard_map/ppermute | solution.py:37
  116.4 15.2 %collective-permute-start.12 = (f32[2,2,48,768]{3,2,1,0:T(8,128)S(1)}, f32[2,2,48,768]{3,2,1,0:T(8,128)S(1)}, u32[]{:S(2)}, u32[]{:S(2)}) collective-permute-start(f32[2,2,48,768]{3,2,1,0:T(8,128)S(1)} %dynamic-slice_bitcast_fusion.5), channel_id=1, source_target_pairs={{0,4},{4,0},{8,12},{12,8},{16,20},{20,16},{24,28},{28,24},{1,5},{5... | collective-permute-start | bytes 1769480 | tf_op jit(solution)/shard_map/ppermute | solution.py:37
  117.5 14.1 %collective-permute-start.13 = (f32[2,2,48,768]{3,2,1,0:T(8,128)S(1)}, f32[2,2,48,768]{3,2,1,0:T(8,128)S(1)}, u32[]{:S(2)}, u32[]{:S(2)}) collective-permute-start(f32[2,2,48,768]{3,2,1,0:T(8,128)S(1)} %dynamic-slice_bitcast_fusion.4), channel_id=1, source_target_pairs={{0,8},{4,12},{8,0},{12,4},{16,24},{20,28},{24,16},{28,20},{1,9},{5... | collective-permute-start | bytes 1769480 | tf_op jit(solution)/shard_map/ppermute | solution.py:37
  117.9 13.7 %collective-permute-start.14 = (f32[2,2,48,768]{3,2,1,0:T(8,128)S(1)}, f32[2,2,48,768]{3,2,1,0:T(8,128)S(1)}, u32[]{:S(2)}, u32[]{:S(2)}) collective-permute-start(f32[2,2,48,768]{3,2,1,0:T(8,128)S(1)} %dynamic-slice_bitcast_fusion.3), channel_id=1, source_target_pairs={{0,2},{1,3},{2,0},{3,1},{4,6},{5,7},{6,4},{7,5},{8,10},{9,11},{10,... | collective-permute-start | bytes 1769480 | tf_op jit(solution)/shard_map/ppermute | solution.py:37
  119.7 11.9 %collective-permute-start.15 = (f32[1281]{0:T(1024)S(1)}, f32[1281]{0:T(1024)S(1)}, u32[]{:S(2)}, u32[]{:S(2)}) collective-permute-start(f32[1281]{0:T(1024)S(1)} %add.186), channel_id=1, source_target_pairs={{0,8},{4,12},{8,0},{12,4},{16,24},{20,28},{24,16},{28,20},{1,9},{5... | collective-permute-start | bytes 15380 | tf_op jit(solution)/shard_map/ppermute | solution.py:37
  132.0 15.7 %collective-permute-start.16 = (f32[2,48,768]{2,1,0:T(8,128)S(1)}, f32[2,48,768]{2,1,0:T(8,128)S(1)}, u32[]{:S(2)}, u32[]{:S(2)}) collective-permute-start(f32[2,48,768]{2,1,0:T(8,128)S(1)} %dynamic-slice_bitcast_fusion.8), channel_id=1, source_target_pairs={{0,8},{4,12},{8,0},{12,4},{16,24},{20,28},{24,16},{28,20},{1,9},{5... | collective-permute-start | bytes 884744 | tf_op jit(solution)/shard_map/ppermute | solution.py:37
  133.6 14.0 %collective-permute-start.17 = (f32[2,48,768]{2,1,0:T(8,128)S(1)}, f32[2,48,768]{2,1,0:T(8,128)S(1)}, u32[]{:S(2)}, u32[]{:S(2)}) collective-permute-start(f32[2,48,768]{2,1,0:T(8,128)S(1)} %dynamic-slice_bitcast_fusion.7), channel_id=1, source_target_pairs={{0,16},{4,20},{8,24},{12,28},{16,0},{20,4},{24,8},{28,12},{1,17},{... | collective-permute-start | bytes 884744 | tf_op jit(solution)/shard_map/ppermute | solution.py:37
  136.2 11.5 %collective-permute-start.18 = (f32[2,48,768]{2,1,0:T(8,128)S(1)}, f32[2,48,768]{2,1,0:T(8,128)S(1)}, u32[]{:S(2)}, u32[]{:S(2)}) collective-permute-start(f32[2,48,768]{2,1,0:T(8,128)S(1)} %dynamic-slice_bitcast_fusion.6), channel_id=1, source_target_pairs={{0,4},{4,0},{8,12},{12,8},{16,20},{20,16},{24,28},{28,24},{1,5},{5... | collective-permute-start | bytes 884744 | tf_op jit(solution)/shard_map/ppermute | solution.py:37
  137.2 10.4 %collective-permute-start.19 = (f32[1281]{0:T(1024)S(1)}, f32[1281]{0:T(1024)S(1)}, u32[]{:S(2)}, u32[]{:S(2)}) collective-permute-start(f32[1281]{0:T(1024)S(1)} %add.194), channel_id=1, source_target_pairs={{0,16},{4,20},{8,24},{12,28},{16,0},{20,4},{24,8},{28,12},{1,17},{... | collective-permute-start | bytes 15380 | tf_op jit(solution)/shard_map/ppermute | solution.py:37
  149.5 6.1 %collective-permute-start.22 = (f32[48,768]{1,0:T(8,128)S(1)}, f32[48,768]{1,0:T(8,128)S(1)}, u32[]{:S(2)}, u32[]{:S(2)}) collective-permute-start(f32[48,768]{1,0:T(8,128)S(1)} %dynamic-slice_bitcast_fusion.9), channel_id=1, source_target_pairs={{0,16},{4,20},{8,24},{12,28},{16,0},{20,4},{24,8},{28,12},{1,17},{... | collective-permute-start | bytes 442376 | tf_op jit(solution)/shard_map/ppermute | solution.py:37
  149.7 5.9 %collective-permute-start.21 = (f32[48,768]{1,0:T(8,128)S(1)}, f32[48,768]{1,0:T(8,128)S(1)}, u32[]{:S(2)}, u32[]{:S(2)}) collective-permute-start(f32[48,768]{1,0:T(8,128)S(1)} %dynamic-slice_bitcast_fusion.10), channel_id=1, source_target_pairs={{0,2},{1,3},{2,0},{3,1},{4,6},{5,7},{6,4},{7,5},{8,10},{9,11},{10,... | collective-permute-start | bytes 442376 | tf_op jit(solution)/shard_map/ppermute | solution.py:37
  150.9 7.9 %collective-permute-start.20 = (f32[48,768]{1,0:T(8,128)S(1)}, f32[48,768]{1,0:T(8,128)S(1)}, u32[]{:S(2)}, u32[]{:S(2)}) collective-permute-start(f32[48,768]{1,0:T(8,128)S(1)} %dynamic-slice_bitcast_fusion.11), channel_id=1, source_target_pairs={{0,16},{4,20},{8,24},{12,28},{16,0},{20,4},{24,8},{28,12},{1,17},{... | collective-permute-start | bytes 442376 | tf_op jit(solution)/shard_map/ppermute | solution.py:37
  (6 other events, 82.0 us)

commit v3 on v2

--- a/solution.py
+++ b/solution.py
@@ -167,8 +167,9 @@
         )
         parts.append(part.reshape((2,) * nbits + (rows, group_taps[s] * out_chans)))
 
-    halves = 2
+    halves = 3
     share = in_chans // halves
+    under = {0: [0, 1], 2: [2]}
     grad_chunks = [
         lax.dot_general(
             shifted.reshape(local_pix, taps, out_chans),
@@ -203,8 +204,11 @@
             packed, sends = lax.optimization_barrier((packed, sends))
             received.append(exchange(packed, *small_bits[step]))
         received = [exchange(sends[s], orders[s][step][0], orders[s][step][1]) for s in range(3)] + received
-        if step < halves:
-            received, grad_chunks[step] = lax.optimization_barrier((received, grad_chunks[step]))
+        if step in under:
+            covered = [grad_chunks[i] for i in under[step]]
+            received, covered = lax.optimization_barrier((received, covered))
+            for i, chunk in zip(under[step], covered):
+                grad_chunks[i] = chunk
         else:
             received = lax.optimization_barrier(received)
         if step < len(small_bits):

time: 163 us -> 172 us (1.055)
  other arithmetic: 16.4 us -> 25.1 us
  local copies, waits for them, and re-layouts: 7.39 us -> 10.3 us
    add x14, other arithmetic: 1.96 us -> 8.53 us  [body(): pieces = [keeps[s] + received[s] for s in range(3)]]
    dot_general x2 -> x3, matrix products: 17.2 us -> 20.5 us  [body(): lax.dot_general(shifted.reshape(local_pix, taps, out_chans), conv_weight[...]
    dot_general x3, matrix products: 18.4 us -> 15.6 us  [body(): lax.dot_general(flat_x, cols, (((0,), (0,)), ((), ())), preferred_element...]
    squeeze x12, local copies, waits for them, and re-layouts: 0.57 us -> 3.29 us  [body(): lax.dynamic_index_in_dim(pieces[s], 1 - mine, ax, keepdims=False)]
where the time goes in v3:
time: 172 us; the launch traced here: 171 us
  matrix products  42.1 us (24%)
  starting transfers between devices  34.7 us (20%)
  waiting for transfers between devices  34.4 us (20%)
  other arithmetic  25.1 us (15%)
  blocking collectives  19.2 us (11%)
  local copies, waits for them, and re-layouts  10.3 us (6%)
  between operations  5.58 us (3%)
    ppermute x21, waiting for transfers between devices, exchange(): return lax.ppermute(x, axis, pairs)  34.3 us
    ppermute x21, starting transfers between devices, exchange(): return lax.ppermute(x, axis, pairs)  31.8 us
    dot_general x3, matrix products, body(): lax.dot_general(shifted.reshape(local_pix, taps, out_chans), conv_weight[...  20.5 us
    dot_general x3, matrix products, body(): lax.dot_general(flat_x, cols, (((0,), (0,)), ((), ())), preferred_element...  15.6 us
    psum x1, blocking collectives, body(): tile_stats = lax.psum(slot[:, None] * local_stats[None, :], 'tile')  12.6 us
    add x14, other arithmetic, body(): pieces = [keeps[s] + received[s] for s in range(3)]  8.53 us
    psum x1, blocking collectives, body(): lax.psum((jnp.sum(preactivation_gradient, 0), jnp.sum(preactivation_gradi...  6.56 us
    concatenate x1, other arithmetic, body(): jnp.concatenate(grad_chunks, 1)  4.03 us
  transfers between devices with their start and end apart: 23, of which 8 were waited for; matrix products, arithmetic and copies ran while one was open for 30% of the time, Pallas kernels for 0%

profile of v3, /device:TPU:0, one launch (start us, length us, event | category | flops | bytes accessed | tf_op | source)
XLA Modules:
  0.0 171.3 jit_solution(7934087230787782676)
XLA Ops:
  6.5 12.6 %psum.35 = f32[4,513]{1,0:T(4,128)S(1)} all-reduce(f32[4,513]{1,0:T(4,128)S(1)} %broadcast_multiply_fusion), channel_id=1, replica_groups=mesh['rep'=8,'tile'=4] {'tile'}, use_global_device_ids=true, to_apply=%region_3.0 | all-reduce | flops 2052 | bytes 16416 | tf_op jit(solution)/shard_map/psum | solution.py:90
  22.2 1.8 %fusion.49 = (f32[1728]{0:T(1024)S(1)}, f32[1728,3]{0,1:T(4,128)S(1)}) fusion(f32[3,256]{1,0:T(4,128)S(1)} %copy-done, f32[1728,256]{1,0:T(8,128)S(1)} %fusion.27, f32[256]{0:T(256)S(1)} %copy-done.11, f32[256]{0:T(256)S(1)} %copy-done.10), kind=kOutput, calls=%fused_computation.131 | convolution fusion | flops 17255808 | bytes 1802240 | tf_op jit(solution)/shard_map/dot_general | solution.py:104
  25.3 2.9 %collective-permute-start.1 = (f32[]{:T(128)}, f32[]{:T(128)}, u32[]{:S(2)}, u32[]{:S(2)}) collective-permute-start(f32[]{:T(128)} %add.174), channel_id=1, source_target_pairs={{0,8},{4,12},{8,0},{12,4},{16,24},{20,28},{24,16},{28,20},{1,9},{5... | collective-permute-start | bytes 20 | tf_op jit(solution)/shard_map/ppermute | solution.py:37
  29.6 4.0 %collective-permute-start.2 = (f32[]{:T(128)}, f32[]{:T(128)}, u32[]{:S(2)}, u32[]{:S(2)}) collective-permute-start(f32[]{:T(128)} %add.175), channel_id=1, source_target_pairs={{0,16},{4,20},{8,24},{12,28},{16,0},{20,4},{24,8},{28,12},{1,17},{... | collective-permute-start | bytes 20 | tf_op jit(solution)/shard_map/ppermute | solution.py:37
  35.5 3.3 %fusion.46 = (f32[256]{0:T(256)S(1)}, f32[256]{0:T(256)S(1)}, f32[1728,256]{1,0:T(8,128)}) fusion(f32[256]{0:T(256)S(1)} %get-tuple-element.128, f32[256]{0:T(256)S(1)} %broadcast_multiply_fusion.2, bf16[2,12,72,256]{3,2,1,0:T(8,128)(2,1)S(1)} %copy-done.2, f32[3,256]{1,0:T(4,128)S(1)} %copy-done, f32[1728,3]{0,1:T(4,128)S(1)} %get-tuple-element.130, ...), kind=kOutput, calls=%fused_computation.128 | convolution fusion | flops 20374336 | bytes 4474368 | tf_op jit(solution)/shard_map/dot_general | solution.py:112
  39.8 6.6 %all-reduce.2 = (f32[1]{0:T(128)}, f32[768]{0:T(1024)S(1)}, f32[256]{0:T(256)S(1)}, f32[256]{0:T(256)S(1)}) all-reduce(f32[1]{0:T(128)} %bitcast.2, f32[768]{0:T(1024)S(1)} %reshape.129, f32[256]{0:T(256)S(1)} %get-tuple-element.101, f32[256]{0:T(256)S(1)} %get-tuple-element.100), channel_id=1, replica_groups=mesh['rep'=8,'tile'=4] {'tile'}, use_global_device_ids=true, to_apply=%region_17.18 | all-reduce | flops 1281 | bytes 10248 | tf_op jit(solution)/shard_map/psum | solution.py:114
  46.4 2.0 %multiply_convert_fusion = bf16[1728,256]{1,0:T(8,128)(2,1)S(1)} fusion(f32[1728,256]{1,0:T(8,128)} %get-tuple-element.131, f32[256]{0:T(256)S(1)} %get-tuple-element.108, f32[256]{0:T(256)S(1)} %broadcast_multiply_fusion.1, f32[256]{0:T(256)S(1)} %get-tuple-element.127, f32[256]{0:T(256)S(1)} %get-tuple-element.128, f32[256]{0:T(256)S(1)} %broadcast_multiply_fusion.2, ...), kind=kLoop, calls=%fused_computation.42 | loop fusion | flops 3981312 | bytes 3544064 | tf_op jit(solution)/shard_map/convert_element_type | solution.py:134
  52.8 6.5 %fusion.12 = f32[1536,768]{1,0:T(8,128)S(1)} fusion(bf16[1728,1536]{1,0:T(8,128)(2,1)} %bitcast.147, bf16[1728,256]{1,0:T(8,128)(2,1)S(1)} %bitcast.136, bf16[1728,256]{1,0:T(8,128)(2,1)S(1)} %multiply_convert_fusion, bf16[1728,256]{1,0:T(8,128)(2,1)S(1)} %bitcast.138), kind=kOutput, calls=%fused_computation.19 | convolution fusion | flops 4084826112 | bytes 12681216 | tf_op jit(solution)/shard_map/dot_general | solution.py:165
  61.4 2.0 %fusion.5 = bf16[2,36,96,256]{3,2,1,0:T(8,128)(2,1)S(1)} fusion(bf16[2,12,72,256]{3,2,1,0:T(8,128)(2,1)S(1)} %collective-permute-done.4, bf16[2,12,72,256]{3,2,1,0:T(8,128)(2,1)S(1)} %bitcast.119, bf16[2,12,72,256]{3,2,1,0:T(8,128)(2,1)S(1)} %collective-permute-done.3), kind=kLoop, calls=%fused_computation.8 | loop fusion | flops 21233664 | bytes 6193152 | tf_op jit(solution)/shard_map/concatenate | solution.py:21
  63.8 4.5 %fusion.18 = f32[1536,768]{1,0:T(8,128)S(1)} fusion(bf16[1728,1536]{1,0:T(8,128)(2,1)S(1)} %bitcast.150, bf16[1728,256]{1,0:T(8,128)(2,1)S(1)} %bitcast.128, bf16[1728,256]{1,0:T(8,128)(2,1)S(1)} %bitcast.124, bf16[1728,256]{1,0:T(8,128)(2,1)S(1)} %bitcast.130), kind=kOutput, calls=%fused_computation.25 | convolution fusion | flops 4084826112 | bytes 12681216 | tf_op jit(solution)/shard_map/dot_general | solution.py:165
  69.0 3.7 %collective-permute-start.7 = (f32[2,2,2,2,48,768]{5,4,3,2,0,1:T(8,128)S(1)}, f32[2,2,2,2,48,768]{5,4,3,2,0,1:T(8,128)S(1)}, u32[]{:S(2)}, u32[]{:S(2)}) collective-permute-start(f32[2,2,2,2,48,768]{5,4,3,2,0,1:T(8,128)S(1)} %bitcast.141), channel_id=1, source_target_pairs={{0,1},{1,0},{2,3},{3,2},{4,5},{5,4},{6,7},{7,6},{8,9},{9,8},{10,11... | collective-permute-start | bytes 7077896 | tf_op jit(solution)/shard_map/ppermute | solution.py:37
  72.7 4.5 %fusion.6 = f32[1536,768]{1,0:T(8,128)S(1)} fusion(bf16[1728,1536]{1,0:T(8,128)(2,1)S(1)} %bitcast.151, bf16[1728,256]{1,0:T(8,128)(2,1)S(1)} %bitcast.132, bf16[1728,256]{1,0:T(8,128)(2,1)S(1)} %bitcast.126, bf16[1728,256]{1,0:T(8,128)(2,1)S(1)} %bitcast.134), kind=kOutput, calls=%fused_computation.13 | convolution fusion | flops 4084826112 | bytes 12681216 | tf_op jit(solution)/shard_map/dot_general | solution.py:165
  78.6 3.9 %collective-permute-done.5 = f32[2,2,2,2,48,768]{5,4,2,1,0,3:T(8,128)S(1)} collective-permute-done((f32[2,2,2,2,48,768]{5,4,2,1,0,3:T(8,128)S(1)}, f32[2,2,2,2,48,768]{5,4,2,1,0,3:T(8,128)S(1)}, u32[]{:S(2)}, u32[]{:S(2)}) %collective-permute-start.5) | collective-permute-done | bytes 2359328 | tf_op jit(solution)/shard_map/ppermute | solution.py:37
  84.2 1.6 collective-permute-start.10
  86.8 5.5 %bitcast_convert_fusion.1 = bf16[1728,512]{1,0:T(8,128)(2,1)} fusion(bf16[1728,9,256]{2,0,1:T(8,128)(2,1)S(1)} %constant_dynamic-update-slice_fusion, bf16[9,1536,256]{2,1,0:T(8,128)(2,1)S(1)} %bitcast.146), kind=kOutput, calls=%fused_computation.10 | convolution fusion | flops 4077748224 | bytes 12091392 | tf_op jit(solution)/shard_map/dot_general | solution.py:174
  93.3 5.5 %bitcast_convert_fusion.2 = bf16[1728,512]{1,0:T(8,128)(2,1)} fusion(bf16[1728,9,256]{2,0,1:T(8,128)(2,1)S(1)} %constant_dynamic-update-slice_fusion, bf16[9,1536,256]{2,1,0:T(8,128)(2,1)S(1)} %bitcast.146), kind=kOutput, calls=%fused_computation.11 | convolution fusion | flops 4077748224 | bytes 12091392 | tf_op jit(solution)/shard_map/dot_general | solution.py:174
  98.9 14.8 %collective-permute-done.11 = f32[1281]{0:T(1024)S(1)} collective-permute-done((f32[1281]{0:T(1024)S(1)}, f32[1281]{0:T(1024)S(1)}, u32[]{:S(2)}, u32[]{:S(2)}) %collective-permute-start.11) | collective-permute-done | bytes 5156 | tf_op jit(solution)/shard_map/ppermute | solution.py:37
  118.4 1.7 %collective-permute-start.14 = (f32[2,2,48,768]{3,2,1,0:T(8,128)}, f32[2,2,48,768]{3,2,1,0:T(8,128)}, u32[]{:S(2)}, u32[]{:S(2)}) collective-permute-start(f32[2,2,48,768]{3,2,1,0:T(8,128)} %dynamic-slice_bitcast_fusion.3), channel_id=1, source_target_pairs={{0,2},{1,3},{2,0},{3,1},{4,6},{5,7},{6,4},{7,5},{8,10},{9,11},{10,... | collective-permute-start | bytes 1769480 | tf_op jit(solution)/shard_map/ppermute | solution.py:37
  121.7 10.7 %collective-permute-done.15 = f32[1281]{0:T(1024)} collective-permute-done((f32[1281]{0:T(1024)S(1)}, f32[1281]{0:T(1024)}, u32[]{:S(2)}, u32[]{:S(2)}) %collective-permute-start.15) | collective-permute-done | bytes 5156 | tf_op jit(solution)/shard_map/ppermute | solution.py:37
  136.9 1.6 collective-permute-start.16
  138.5 2.6 %collective-permute-start.17 = (f32[2,48,768]{2,1,0:T(8,128)S(1)}, f32[2,48,768]{2,1,0:T(8,128)}, u32[]{:S(2)}, u32[]{:S(2)}) collective-permute-start(f32[2,48,768]{2,1,0:T(8,128)S(1)} %dynamic-slice_bitcast_fusion.7), channel_id=1, source_target_pairs={{0,16},{4,20},{8,24},{12,28},{16,0},{20,4},{24,8},{28,12},{1,17},{... | collective-permute-start | bytes 884744 | tf_op jit(solution)/shard_map/ppermute | solution.py:37
  142.5 9.5 %bitcast_convert_fusion = bf16[1728,512]{1,0:T(8,128)(2,1)} fusion(bf16[1728,9,256]{2,0,1:T(8,128)(2,1)} %copy-done.7, bf16[9,1536,256]{2,1,0:T(8,128)(2,1)} %param.10), kind=kOutput, calls=%fused_computation.9 | convolution fusion | flops 4077748224 | bytes 12091392 | tf_op jit(solution)/shard_map/dot_general | solution.py:174
  155.4 2.1 %collective-permute-start.22 = (f32[48,768]{1,0:T(8,128)S(1)}, f32[48,768]{1,0:T(8,128)S(1)}, u32[]{:S(2)}, u32[]{:S(2)}) collective-permute-start(f32[48,768]{1,0:T(8,128)S(1)} %dynamic-slice_bitcast_fusion.9), channel_id=1, source_target_pairs={{0,16},{4,20},{8,24},{12,28},{16,0},{20,4},{24,8},{28,12},{1,17},{... | collective-permute-start | bytes 442376 | tf_op jit(solution)/shard_map/ppermute | solution.py:37
  161.8 4.0 %pad_maximum_fusion = bf16[1728,1536]{1,0:T(8,128)(2,1)} fusion(bf16[1728,512]{1,0:T(8,128)(2,1)} %bitcast_convert_fusion, bf16[1728,512]{1,0:T(8,128)(2,1)S(1)} %copy-done.5, bf16[1728,512]{1,0:T(8,128)(2,1)S(1)} %copy-done.6), kind=kLoop, calls=%fused_computation.3 | loop fusion | flops 15925248 | bytes 10616832 | tf_op jit(solution)/shard_map/concatenate | solution.py:225
  (143 shorter events, 47.7 us)
Async XLA Ops:
  19.8 4.3 %collective-permute-start = (f32[]{:T(128)}, f32[]{:T(128)}, u32[]{:S(2)}, u32[]{:S(2)}) collective-permute-start(f32[]{:T(128)} %slice_reduce_fusion.1), channel_id=1, source_target_pairs={{0,4},{4,0},{8,12},{12,8},{16,20},{20,16},{24,28},{28,24},{1,5},{5... | collective-permute-start | bytes 20 | tf_op jit(solution)/shard_map/ppermute | solution.py:37
  25.3 3.7 %collective-permute-start.1 = (f32[]{:T(128)}, f32[]{:T(128)}, u32[]{:S(2)}, u32[]{:S(2)}) collective-permute-start(f32[]{:T(128)} %add.174), channel_id=1, source_target_pairs={{0,8},{4,12},{8,0},{12,4},{16,24},{20,28},{24,16},{28,20},{1,9},{5... | collective-permute-start | bytes 20 | tf_op jit(solution)/shard_map/ppermute | solution.py:37
  29.6 4.6 %collective-permute-start.2 = (f32[]{:T(128)}, f32[]{:T(128)}, u32[]{:S(2)}, u32[]{:S(2)}) collective-permute-start(f32[]{:T(128)} %add.175), channel_id=1, source_target_pairs={{0,16},{4,20},{8,24},{12,28},{16,0},{20,4},{24,8},{28,12},{1,17},{... | collective-permute-start | bytes 20 | tf_op jit(solution)/shard_map/ppermute | solution.py:37
  48.4 13.0 %collective-permute-start.3 = (bf16[2,12,72,256]{3,2,1,0:T(8,128)(2,1)S(1)}, bf16[2,12,72,256]{3,2,1,0:T(8,128)(2,1)S(1)}, u32[]{:S(2)}, u32[]{:S(2)}) collective-permute-start(bf16[2,12,72,256]{3,2,1,0:T(8,128)(2,1)S(1)} %bitcast.116), channel_id=1, source_target_pairs={{0,1},{1,2},{2,3},{4,5},{5,6},{6,7},{8,9},{9,10},{10,11},{12,13},{... | collective-permute-start | bytes 2654216 | tf_op jit(solution)/shard_map/ppermute | solution.py:19
  50.0 11.4 %collective-permute-start.4 = (bf16[2,12,72,256]{3,2,1,0:T(8,128)(2,1)S(1)}, bf16[2,12,72,256]{3,2,1,0:T(8,128)(2,1)S(1)}, u32[]{:S(2)}, u32[]{:S(2)}) collective-permute-start(bf16[2,12,72,256]{3,2,1,0:T(8,128)(2,1)S(1)} %bitcast.117), channel_id=1, source_target_pairs={{1,0},{2,1},{3,2},{5,4},{6,5},{7,6},{9,8},{10,9},{11,10},{13,12},{... | collective-permute-start | bytes 2654216 | tf_op jit(solution)/shard_map/ppermute | solution.py:20
  52.8 39.5 %copy-start.8 = (f32[1281]{0:T(1024)}, f32[1281]{0:T(1024)S(1)}, u32[]{:S(2)}) copy-start(f32[1281]{0:T(1024)S(1)} %pad_maximum_fusion.2) | copy-start | bytes 15376
  60.0 18.6 %collective-permute-start.6 = (f32[2,2,2,2,48,768]{5,4,3,1,0,2:T(8,128)S(1)}, f32[2,2,2,2,48,768]{5,4,3,1,0,2:T(8,128)S(1)}, u32[]{:S(2)}, u32[]{:S(2)}) collective-permute-start(f32[2,2,2,2,48,768]{5,4,3,1,0,2:T(8,128)S(1)} %bitcast.140), channel_id=1, source_target_pairs={{0,1},{1,0},{2,3},{3,2},{4,5},{5,4},{6,7},{7,6},{8,9},{9,8},{10,11... | collective-permute-start | bytes 7077896 | tf_op jit(solution)/shard_map/ppermute | solution.py:37
  69.0 9.6 %collective-permute-start.7 = (f32[2,2,2,2,48,768]{5,4,3,2,0,1:T(8,128)S(1)}, f32[2,2,2,2,48,768]{5,4,3,2,0,1:T(8,128)S(1)}, u32[]{:S(2)}, u32[]{:S(2)}) collective-permute-start(f32[2,2,2,2,48,768]{5,4,3,2,0,1:T(8,128)S(1)} %bitcast.141), channel_id=1, source_target_pairs={{0,1},{1,0},{2,3},{3,2},{4,5},{5,4},{6,7},{7,6},{8,9},{9,8},{10,11... | collective-permute-start | bytes 7077896 | tf_op jit(solution)/shard_map/ppermute | solution.py:37
  77.9 4.6 %collective-permute-start.5 = (f32[2,2,2,2,48,768]{5,4,2,1,0,3:T(8,128)S(1)}, f32[2,2,2,2,48,768]{5,4,2,1,0,3:T(8,128)S(1)}, u32[]{:S(2)}, u32[]{:S(2)}) collective-permute-start(f32[2,2,2,2,48,768]{5,4,2,1,0,3:T(8,128)S(1)} %bitcast.142), channel_id=1, source_target_pairs={{0,1},{1,0},{2,3},{3,2},{4,5},{5,4},{6,7},{7,6},{8,9},{9,8},{10,11... | collective-permute-start | bytes 7077896 | tf_op jit(solution)/shard_map/ppermute | solution.py:37
  84.2 29.6 %collective-permute-start.10 = (f32[2,2,2,48,768]{4,3,2,1,0:T(8,128)S(1)}, f32[2,2,2,48,768]{4,3,2,1,0:T(8,128)S(1)}, u32[]{:S(2)}, u32[]{:S(2)}) collective-permute-start(f32[2,2,2,48,768]{4,3,2,1,0:T(8,128)S(1)} %dynamic-slice_bitcast_fusion), channel_id=1, source_target_pairs={{0,8},{4,12},{8,0},{12,4},{16,24},{20,28},{24,16},{28,20},{1,9},{5... | collective-permute-start | bytes 3538952 | tf_op jit(solution)/shard_map/ppermute | solution.py:37
  85.8 27.9 %collective-permute-start.8 = (f32[2,2,2,48,768]{4,3,2,1,0:T(8,128)S(1)}, f32[2,2,2,48,768]{4,3,2,1,0:T(8,128)S(1)}, u32[]{:S(2)}, u32[]{:S(2)}) collective-permute-start(f32[2,2,2,48,768]{4,3,2,1,0:T(8,128)S(1)} %dynamic-slice_bitcast_fusion.2), channel_id=1, source_target_pairs={{0,2},{1,3},{2,0},{3,1},{4,6},{5,7},{6,4},{7,5},{8,10},{9,11},{10,... | collective-permute-start | bytes 3538952 | tf_op jit(solution)/shard_map/ppermute | solution.py:37
  85.8 27.9 %collective-permute-start.9 = (f32[2,2,2,48,768]{4,3,2,1,0:T(8,128)S(1)}, f32[2,2,2,48,768]{4,3,2,1,0:T(8,128)S(1)}, u32[]{:S(2)}, u32[]{:S(2)}) collective-permute-start(f32[2,2,2,48,768]{4,3,2,1,0:T(8,128)S(1)} %dynamic-slice_bitcast_fusion.1), channel_id=1, source_target_pairs={{0,4},{4,0},{8,12},{12,8},{16,20},{20,16},{24,28},{28,24},{1,5},{5... | collective-permute-start | bytes 3538952 | tf_op jit(solution)/shard_map/ppermute | solution.py:37
  92.3 21.4 %collective-permute-start.11 = (f32[1281]{0:T(1024)S(1)}, f32[1281]{0:T(1024)S(1)}, u32[]{:S(2)}, u32[]{:S(2)}) collective-permute-start(f32[1281]{0:T(1024)S(1)} %pad_maximum_fusion.2), channel_id=1, source_target_pairs={{0,4},{4,0},{8,12},{12,8},{16,20},{20,16},{24,28},{28,24},{1,5},{5... | collective-permute-start | bytes 15380 | tf_op jit(solution)/shard_map/ppermute | solution.py:37
  116.9 15.5 %collective-permute-start.12 = (f32[2,2,48,768]{3,2,1,0:T(8,128)}, f32[2,2,48,768]{3,2,1,0:T(8,128)}, u32[]{:S(2)}, u32[]{:S(2)}) collective-permute-start(f32[2,2,48,768]{3,2,1,0:T(8,128)} %dynamic-slice_bitcast_fusion.5), channel_id=1, source_target_pairs={{0,4},{4,0},{8,12},{12,8},{16,20},{20,16},{24,28},{28,24},{1,5},{5... | collective-permute-start | bytes 1769480 | tf_op jit(solution)/shard_map/ppermute | solution.py:37
  117.9 14.4 %collective-permute-start.13 = (f32[2,2,48,768]{3,2,1,0:T(8,128)}, f32[2,2,48,768]{3,2,1,0:T(8,128)}, u32[]{:S(2)}, u32[]{:S(2)}) collective-permute-start(f32[2,2,48,768]{3,2,1,0:T(8,128)} %dynamic-slice_bitcast_fusion.4), channel_id=1, source_target_pairs={{0,8},{4,12},{8,0},{12,4},{16,24},{20,28},{24,16},{28,20},{1,9},{5... | collective-permute-start | bytes 1769480 | tf_op jit(solution)/shard_map/ppermute | solution.py:37
  118.4 14.0 %collective-permute-start.14 = (f32[2,2,48,768]{3,2,1,0:T(8,128)}, f32[2,2,48,768]{3,2,1,0:T(8,128)}, u32[]{:S(2)}, u32[]{:S(2)}) collective-permute-start(f32[2,2,48,768]{3,2,1,0:T(8,128)} %dynamic-slice_bitcast_fusion.3), channel_id=1, source_target_pairs={{0,2},{1,3},{2,0},{3,1},{4,6},{5,7},{6,4},{7,5},{8,10},{9,11},{10,... | collective-permute-start | bytes 1769480 | tf_op jit(solution)/shard_map/ppermute | solution.py:37
  120.1 12.2 %collective-permute-start.15 = (f32[1281]{0:T(1024)S(1)}, f32[1281]{0:T(1024)}, u32[]{:S(2)}, u32[]{:S(2)}) collective-permute-start(f32[1281]{0:T(1024)S(1)} %add.186), channel_id=1, source_target_pairs={{0,8},{4,12},{8,0},{12,4},{16,24},{20,28},{24,16},{28,20},{1,9},{5... | collective-permute-start | bytes 15380 | tf_op jit(solution)/shard_map/ppermute | solution.py:37
  136.9 15.6 %collective-permute-start.16 = (f32[2,48,768]{2,1,0:T(8,128)S(1)}, f32[2,48,768]{2,1,0:T(8,128)}, u32[]{:S(2)}, u32[]{:S(2)}) collective-permute-start(f32[2,48,768]{2,1,0:T(8,128)S(1)} %dynamic-slice_bitcast_fusion.8), channel_id=1, source_target_pairs={{0,8},{4,12},{8,0},{12,4},{16,24},{20,28},{24,16},{28,20},{1,9},{5... | collective-permute-start | bytes 884744 | tf_op jit(solution)/shard_map/ppermute | solution.py:37
  138.5 14.0 %collective-permute-start.17 = (f32[2,48,768]{2,1,0:T(8,128)S(1)}, f32[2,48,768]{2,1,0:T(8,128)}, u32[]{:S(2)}, u32[]{:S(2)}) collective-permute-start(f32[2,48,768]{2,1,0:T(8,128)S(1)} %dynamic-slice_bitcast_fusion.7), channel_id=1, source_target_pairs={{0,16},{4,20},{8,24},{12,28},{16,0},{20,4},{24,8},{28,12},{1,17},{... | collective-permute-start | bytes 884744 | tf_op jit(solution)/shard_map/ppermute | solution.py:37
  141.1 11.4 %collective-permute-start.18 = (f32[2,48,768]{2,1,0:T(8,128)S(1)}, f32[2,48,768]{2,1,0:T(8,128)}, u32[]{:S(2)}, u32[]{:S(2)}) collective-permute-start(f32[2,48,768]{2,1,0:T(8,128)S(1)} %dynamic-slice_bitcast_fusion.6), channel_id=1, source_target_pairs={{0,4},{4,0},{8,12},{12,8},{16,20},{20,16},{24,28},{28,24},{1,5},{5... | collective-permute-start | bytes 884744 | tf_op jit(solution)/shard_map/ppermute | solution.py:37
  142.1 10.4 %collective-permute-start.19 = (f32[1281]{0:T(1024)S(1)}, f32[1281]{0:T(1024)S(1)}, u32[]{:S(2)}, u32[]{:S(2)}) collective-permute-start(f32[1281]{0:T(1024)S(1)} %add.193), channel_id=1, source_target_pairs={{0,16},{4,20},{8,24},{12,28},{16,0},{20,4},{24,8},{28,12},{1,17},{... | collective-permute-start | bytes 15380 | tf_op jit(solution)/shard_map/ppermute | solution.py:37
  155.4 12.2 %collective-permute-start.22 = (f32[48,768]{1,0:T(8,128)S(1)}, f32[48,768]{1,0:T(8,128)S(1)}, u32[]{:S(2)}, u32[]{:S(2)}) collective-permute-start(f32[48,768]{1,0:T(8,128)S(1)} %dynamic-slice_bitcast_fusion.9), channel_id=1, source_target_pairs={{0,16},{4,20},{8,24},{12,28},{16,0},{20,4},{24,8},{28,12},{1,17},{... | collective-permute-start | bytes 442376 | tf_op jit(solution)/shard_map/ppermute | solution.py:37
  158.6 9.1 %collective-permute-start.21 = (f32[48,768]{1,0:T(8,128)S(1)}, f32[48,768]{1,0:T(8,128)S(1)}, u32[]{:S(2)}, u32[]{:S(2)}) collective-permute-start(f32[48,768]{1,0:T(8,128)S(1)} %dynamic-slice_bitcast_fusion.10), channel_id=1, source_target_pairs={{0,2},{1,3},{2,0},{3,1},{4,6},{5,7},{6,4},{7,5},{8,10},{9,11},{10,... | collective-permute-start | bytes 442376 | tf_op jit(solution)/shard_map/ppermute | solution.py:37
  161.1 8.2 %collective-permute-start.20 = (f32[48,768]{1,0:T(8,128)S(1)}, f32[48,768]{1,0:T(8,128)S(1)}, u32[]{:S(2)}, u32[]{:S(2)}) collective-permute-start(f32[48,768]{1,0:T(8,128)S(1)} %dynamic-slice_bitcast_fusion.11), channel_id=1, source_target_pairs={{0,16},{4,20},{8,24},{12,28},{16,0},{20,4},{24,8},{28,12},{1,17},{... | collective-permute-start | bytes 442376 | tf_op jit(solution)/shard_map/ppermute | solution.py:37
  (15 other events, 162.5 us)

commit v4 on v2

--- a/solution.py
+++ b/solution.py
@@ -107,7 +107,7 @@
     cross = log_total - jnp.sum(onehot * logits, -1)
     mean_weight = weight_total / all_pix
     probs = jnp.exp(logits - log_total[:, None])
-    grad_logit = (weights_pix / mean_weight)[:, None] * (probs - onehot)
+    grad_logit = weights_pix[:, None] * (probs - onehot)
     class_local_slice = jnp.dot(grad_logit.T, zvals, precision=highest)
     grad_z = jnp.dot(grad_logit, class_map, precision=highest)
     preactivation_gradient = jnp.where(preactivation_values > 0, grad_z, 0.0)
@@ -127,9 +127,12 @@
         norm_gain_vector
         * inverse_deviation
         * (
-            preactivation_gradient
-            - first_gradient_sum / per_replica_part
-            - normalized_input * second_gradient_sum / per_replica_part
+            (
+                preactivation_gradient
+                - first_gradient_sum / per_replica_part
+                - normalized_input * second_gradient_sum / per_replica_part
+            )
+            / mean_weight
         )
     ).astype(jnp.bfloat16)
     normalized_output_gradient = normalized_output_gradient.reshape(
@@ -214,9 +217,9 @@
 
     for step in range(len(rest), len(small_bits)):
         packed = packed + exchange(packed, *small_bits[step])
-    grad_shift = packed[:out_chans]
-    grad_gain = packed[out_chans : 2 * out_chans]
-    grad_class = packed[2 * out_chans : (2 + classes) * out_chans].reshape(classes, out_chans)
+    grad_shift = packed[:out_chans] / mean_weight
+    grad_gain = packed[out_chans : 2 * out_chans] / mean_weight
+    grad_class = packed[2 * out_chans : (2 + classes) * out_chans].reshape(classes, out_chans) / mean_weight
     loss = packed[(2 + classes) * out_chans] / mean_weight / all_pix
     grad_features = jnp.concatenate(grad_chunks, 1).reshape(images, tile_rows, columns, in_chans)
     return (grad_features, grad_weight, grad_gain, grad_shift, grad_class, loss)

time: 163 us -> 160 us (0.982)
  transfers between devices with their start and end apart: 23 -> 23, of which waited for: 8 -> 8; matrix products, arithmetic and copies ran while one was open for 30% -> 32% of each run, Pallas kernels for 0% -> 0%
where the time goes in v4:
time: 160 us; the launch traced here: 158 us
  matrix products  40 us (25%)
  waiting for transfers between devices  35.5 us (22%)
  starting transfers between devices  35.3 us (22%)
  blocking collectives  19.2 us (12%)
  other arithmetic  15.6 us (10%)
  local copies, waits for them, and re-layouts  6.95 us (4%)
  between operations  5.62 us (4%)
    ppermute x21, waiting for transfers between devices, exchange(): return lax.ppermute(x, axis, pairs)  35.5 us
    ppermute x21, starting transfers between devices, exchange(): return lax.ppermute(x, axis, pairs)  32.7 us
    dot_general x3, matrix products, body(): lax.dot_general(flat_x, cols, (((0,), (0,)), ((), ())), preferred_element...  18 us
    dot_general x2, matrix products, body(): lax.dot_general(shifted.reshape(local_pix, taps, out_chans), conv_weight[...  17.2 us
    psum x1, blocking collectives, body(): tile_stats = lax.psum(slot[:, None] * local_stats[None, :], 'tile')  12.6 us
    psum x1, blocking collectives, body(): lax.psum((jnp.sum(preactivation_gradient, 0), jnp.sum(preactivation_gradi...  6.56 us
  transfers between devices with their start and end apart: 23, of which 8 were waited for; matrix products, arithmetic and copies ran while one was open for 32% of the time, Pallas kernels for 0%

profile of v4, /device:TPU:0, one launch (start us, length us, event | category | flops | bytes accessed | tf_op | source)
XLA Modules:
  0.0 158.2 jit_solution(8133751318955836424)
XLA Ops:
  6.5 12.6 %psum.35 = f32[4,513]{1,0:T(4,128)S(1)} all-reduce(f32[4,513]{1,0:T(4,128)S(1)} %broadcast_multiply_fusion), channel_id=1, replica_groups=mesh['rep'=8,'tile'=4] {'tile'}, use_global_device_ids=true, to_apply=%region_3.0 | all-reduce | flops 2052 | bytes 16416 | tf_op jit(solution)/shard_map/psum | solution.py:90
  22.2 1.8 %fusion.47 = (f32[1728]{0:T(1024)S(1)}, f32[1728,3]{0,1:T(4,128)S(1)}) fusion(f32[3,256]{1,0:T(4,128)S(1)} %copy-done, f32[1728,256]{1,0:T(8,128)S(1)} %fusion.26, f32[256]{0:T(256)S(1)} %copy-done.4, f32[256]{0:T(256)S(1)} %copy-done.3), kind=kOutput, calls=%fused_computation.130 | convolution fusion | flops 17255808 | bytes 1802240 | tf_op jit(solution)/shard_map/dot_general | solution.py:104
  24.6 2.2 %fusion.45 = (f32[256]{0:T(256)S(1)}, f32[256]{0:T(256)S(1)}, f32[1728,256]{1,0:T(8,128)S(1)}) fusion(f32[256]{0:T(256)S(1)} %get-tuple-element.125, f32[256]{0:T(256)S(1)} %broadcast_multiply_fusion.2, bf16[2,12,72,256]{3,2,1,0:T(8,128)(2,1)S(1)} %copy-done.2, f32[3,256]{1,0:T(4,128)S(1)} %copy-done, f32[1728,3]{0,1:T(4,128)S(1)} %get-tuple-element.127, ...), kind=kOutput, calls=%fused_computation.128 | convolution fusion | flops 20374336 | bytes 4474368 | tf_op jit(solution)/shard_map/dot_general | solution.py:112
  27.8 6.6 %all-reduce.2 = (f32[1]{0:T(128)}, f32[768]{0:T(1024)S(1)}, f32[256]{0:T(256)S(1)}, f32[256]{0:T(256)S(1)}) all-reduce(f32[1]{0:T(128)} %bitcast.2, f32[768]{0:T(1024)S(1)} %reshape.126, f32[256]{0:T(256)S(1)} %get-tuple-element.99, f32[256]{0:T(256)S(1)} %get-tuple-element.98), channel_id=1, replica_groups=mesh['rep'=8,'tile'=4] {'tile'}, use_global_device_ids=true, to_apply=%region_16.17 | all-reduce | flops 1281 | bytes 10248 | tf_op jit(solution)/shard_map/psum | solution.py:114
  36.3 2.9 %collective-permute-start.1 = (f32[]{:T(128)}, f32[]{:T(128)}, u32[]{:S(2)}, u32[]{:S(2)}) collective-permute-start(f32[]{:T(128)} %add.175), channel_id=1, source_target_pairs={{0,8},{4,12},{8,0},{12,4},{16,24},{20,28},{24,16},{28,20},{1,9},{5... | collective-permute-start | bytes 20 | tf_op jit(solution)/shard_map/ppermute | solution.py:37
  40.7 3.9 %collective-permute-start.2 = (f32[]{:T(128)}, f32[]{:T(128)}, u32[]{:S(2)}, u32[]{:S(2)}) collective-permute-start(f32[]{:T(128)} %add.176), channel_id=1, source_target_pairs={{0,16},{4,20},{8,24},{12,28},{16,0},{20,4},{24,8},{28,12},{1,17},{... | collective-permute-start | bytes 20 | tf_op jit(solution)/shard_map/ppermute | solution.py:37
  50.0 6.7 %fusion.14 = f32[1536,768]{1,0:T(8,128)S(1)} fusion(bf16[1728,1536]{1,0:T(8,128)(2,1)} %bitcast.142, bf16[1728,256]{1,0:T(8,128)(2,1)S(1)} %bitcast.133, bf16[1728,256]{1,0:T(8,128)(2,1)S(1)} %multiply_convert_fusion, bf16[1728,256]{1,0:T(8,128)(2,1)S(1)} %bitcast.135), kind=kOutput, calls=%fused_computation.20 | convolution fusion | flops 4084826112 | bytes 12681216 | tf_op jit(solution)/shard_map/dot_general | solution.py:168
  57.4 1.7 %collective-permute-start.6 = (f32[2,2,2,2,48,768]{5,4,3,1,0,2:T(8,128)S(1)}, f32[2,2,2,2,48,768]{5,4,3,1,0,2:T(8,128)S(1)}, u32[]{:S(2)}, u32[]{:S(2)}) collective-permute-start(f32[2,2,2,2,48,768]{5,4,3,1,0,2:T(8,128)S(1)} %bitcast.137), channel_id=1, source_target_pairs={{0,1},{1,0},{2,3},{3,2},{4,5},{5,4},{6,7},{7,6},{8,9},{9,8},{10,11... | collective-permute-start | bytes 7077896 | tf_op jit(solution)/shard_map/ppermute | solution.py:37
  59.0 1.9 %fusion.5 = bf16[2,36,96,256]{3,2,1,0:T(8,128)(2,1)S(1)} fusion(bf16[2,12,72,256]{3,2,1,0:T(8,128)(2,1)S(1)} %collective-permute-done.4, bf16[2,12,72,256]{3,2,1,0:T(8,128)(2,1)S(1)} %bitcast.116, bf16[2,12,72,256]{3,2,1,0:T(8,128)(2,1)S(1)} %collective-permute-done.3), kind=kLoop, calls=%fused_computation.10 | loop fusion | flops 21233664 | bytes 6193152 | tf_op jit(solution)/shard_map/concatenate | solution.py:21
  61.3 4.5 %fusion.20 = f32[1536,768]{1,0:T(8,128)S(1)} fusion(bf16[1728,1536]{1,0:T(8,128)(2,1)S(1)} %bitcast.146, bf16[1728,256]{1,0:T(8,128)(2,1)S(1)} %bitcast.125, bf16[1728,256]{1,0:T(8,128)(2,1)S(1)} %bitcast.121, bf16[1728,256]{1,0:T(8,128)(2,1)S(1)} %bitcast.127), kind=kOutput, calls=%fused_computation.26 | convolution fusion | flops 4084826112 | bytes 12681216 | tf_op jit(solution)/shard_map/dot_general | solution.py:168
  66.4 4.2 %collective-permute-start.7 = (f32[2,2,2,2,48,768]{5,4,3,2,0,1:T(8,128)S(1)}, f32[2,2,2,2,48,768]{5,4,3,2,0,1:T(8,128)S(1)}, u32[]{:S(2)}, u32[]{:S(2)}) collective-permute-start(f32[2,2,2,2,48,768]{5,4,3,2,0,1:T(8,128)S(1)} %bitcast.138), channel_id=1, source_target_pairs={{0,1},{1,0},{2,3},{3,2},{4,5},{5,4},{6,7},{7,6},{8,9},{9,8},{10,11... | collective-permute-start | bytes 7077896 | tf_op jit(solution)/shard_map/ppermute | solution.py:37
  70.7 6.7 %fusion.8 = f32[1536,768]{1,0:T(8,128)S(1)} fusion(bf16[1728,1536]{1,0:T(8,128)(2,1)} %bitcast.143, bf16[1728,256]{1,0:T(8,128)(2,1)S(1)} %bitcast.129, bf16[1728,256]{1,0:T(8,128)(2,1)S(1)} %bitcast.123, bf16[1728,256]{1,0:T(8,128)(2,1)S(1)} %bitcast.131), kind=kOutput, calls=%fused_computation.14 | convolution fusion | flops 4084826112 | bytes 12681216 | tf_op jit(solution)/shard_map/dot_general | solution.py:168
  78.7 3.9 %collective-permute-done.5 = f32[2,2,2,2,48,768]{5,4,2,1,0,3:T(8,128)S(1)} collective-permute-done((f32[2,2,2,2,48,768]{5,4,2,1,0,3:T(8,128)S(1)}, f32[2,2,2,2,48,768]{5,4,2,1,0,3:T(8,128)S(1)}, u32[]{:S(2)}, u32[]{:S(2)}) %collective-permute-start.5) | collective-permute-done | bytes 2359328 | tf_op jit(solution)/shard_map/ppermute | solution.py:37
  84.0 1.6 %collective-permute-start.10 = (f32[2,2,2,48,768]{4,3,2,1,0:T(8,128)S(1)}, f32[2,2,2,48,768]{4,3,2,1,0:T(8,128)S(1)}, u32[]{:S(2)}, u32[]{:S(2)}) collective-permute-start(f32[2,2,2,48,768]{4,3,2,1,0:T(8,128)S(1)} %dynamic-slice_bitcast_fusion), channel_id=1, source_target_pairs={{0,8},{4,12},{8,0},{12,4},{16,24},{20,28},{24,16},{28,20},{1,9},{5... | collective-permute-start | bytes 3538952 | tf_op jit(solution)/shard_map/ppermute | solution.py:37
  87.7 8.6 %bitcast_convert_fusion.1 = bf16[1728,768]{1,0:T(8,128)(2,1)S(1)} fusion(bf16[1728,9,256]{2,0,1:T(8,128)(2,1)S(1)} %constant_dynamic-update-slice_fusion, bf16[9,1536,256]{2,1,0:T(8,128)(2,1)} %param.10), kind=kOutput, calls=%fused_computation.5 | convolution fusion | flops 6116622336 | bytes 14155776 | tf_op jit(solution)/shard_map/dot_general | solution.py:176
  96.3 17.3 %collective-permute-done.11 = f32[1281]{0:T(1024)S(1)} collective-permute-done((f32[1281]{0:T(1024)S(1)}, f32[1281]{0:T(1024)S(1)}, u32[]{:S(2)}, u32[]{:S(2)}) %collective-permute-start.11) | collective-permute-done | bytes 5156 | tf_op jit(solution)/shard_map/ppermute | solution.py:37
  115.3 1.7 %collective-permute-start.14 = (f32[2,2,48,768]{3,2,1,0:T(8,128)S(1)}, f32[2,2,48,768]{3,2,1,0:T(8,128)S(1)}, u32[]{:S(2)}, u32[]{:S(2)}) collective-permute-start(f32[2,2,48,768]{3,2,1,0:T(8,128)S(1)} %dynamic-slice_bitcast_fusion.3), channel_id=1, source_target_pairs={{0,2},{1,3},{2,0},{3,1},{4,6},{5,7},{6,4},{7,5},{8,10},{9,11},{10,... | collective-permute-start | bytes 1769480 | tf_op jit(solution)/shard_map/ppermute | solution.py:37
  118.6 8.6 %bitcast_convert_fusion = bf16[1728,768]{1,0:T(8,128)(2,1)S(1)} fusion(bf16[1728,9,256]{2,0,1:T(8,128)(2,1)S(1)} %constant_dynamic-update-slice_fusion, bf16[9,1536,256]{2,1,0:T(8,128)(2,1)} %param.10), kind=kOutput, calls=%fused_computation.4 | convolution fusion | flops 6116622336 | bytes 14155776 | tf_op jit(solution)/shard_map/dot_general | solution.py:176
  127.2 1.8 %collective-permute-done.15 = f32[1281]{0:T(1024)S(1)} collective-permute-done((f32[1281]{0:T(1024)S(1)}, f32[1281]{0:T(1024)S(1)}, u32[]{:S(2)}, u32[]{:S(2)}) %collective-permute-start.15) | collective-permute-done | bytes 5156 | tf_op jit(solution)/shard_map/ppermute | solution.py:37
  131.0 2.6 %collective-permute-start.17 = (f32[2,48,768]{2,1,0:T(8,128)S(1)}, f32[2,48,768]{2,1,0:T(8,128)S(1)}, u32[]{:S(2)}, u32[]{:S(2)}) collective-permute-start(f32[2,48,768]{2,1,0:T(8,128)S(1)} %dynamic-slice_bitcast_fusion.7), channel_id=1, source_target_pairs={{0,16},{4,20},{8,24},{12,28},{16,0},{20,4},{24,8},{28,12},{1,17},{... | collective-permute-start | bytes 884744 | tf_op jit(solution)/shard_map/ppermute | solution.py:37
  135.4 2.8 %pad_maximum_fusion = bf16[1728,1536]{1,0:T(8,128)(2,1)} fusion(bf16[1728,768]{1,0:T(8,128)(2,1)S(1)} %bitcast_convert_fusion, bf16[1728,768]{1,0:T(8,128)(2,1)S(1)} %bitcast_convert_fusion.1), kind=kLoop, calls=%fused_computation.3 | loop fusion | flops 10616832 | bytes 10616832 | tf_op jit(solution)/shard_map/concatenate | solution.py:224
  138.2 6.8 %collective-permute-done.19 = f32[1281]{0:T(1024)S(1)} collective-permute-done((f32[1281]{0:T(1024)S(1)}, f32[1281]{0:T(1024)S(1)}, u32[]{:S(2)}, u32[]{:S(2)}) %collective-permute-start.19) | collective-permute-done | bytes 5156 | tf_op jit(solution)/shard_map/ppermute | solution.py:37
  148.4 3.0 %collective-permute-start.20 = (f32[48,768]{1,0:T(8,128)S(1)}, f32[48,768]{1,0:T(8,128)S(1)}, u32[]{:S(2)}, u32[]{:S(2)}) collective-permute-start(f32[48,768]{1,0:T(8,128)S(1)} %dynamic-slice_bitcast_fusion.11), channel_id=1, source_target_pairs={{0,16},{4,20},{8,24},{12,28},{16,0},{20,4},{24,8},{28,12},{1,17},{... | collective-permute-start | bytes 442376 | tf_op jit(solution)/shard_map/ppermute | solution.py:37
  153.0 3.2 %collective-permute-done.20 = f32[48,768]{1,0:T(8,128)S(1)} collective-permute-done((f32[48,768]{1,0:T(8,128)S(1)}, f32[48,768]{1,0:T(8,128)S(1)}, u32[]{:S(2)}, u32[]{:S(2)}) %collective-permute-start.20) | collective-permute-done | bytes 147488 | tf_op jit(solution)/shard_map/ppermute | solution.py:37
  (123 shorter events, 35.1 us)
Async XLA Ops:
  0.6 21.5 %copy-start = (f32[3,256]{1,0:T(4,128)S(1)}, f32[3,256]{1,0:T(4,128)}, u32[]{:S(2)}) copy-start(f32[3,256]{1,0:T(4,128)} %param.13) | copy-start | bytes 9220
  19.8 15.3 %collective-permute-start = (f32[]{:T(128)}, f32[]{:T(128)}, u32[]{:S(2)}, u32[]{:S(2)}) collective-permute-start(f32[]{:T(128)} %slice_reduce_fusion.1), channel_id=1, source_target_pairs={{0,4},{4,0},{8,12},{12,8},{16,20},{20,16},{24,28},{28,24},{1,5},{5... | collective-permute-start | bytes 20 | tf_op jit(solution)/shard_map/ppermute | solution.py:37
  36.3 3.7 %collective-permute-start.1 = (f32[]{:T(128)}, f32[]{:T(128)}, u32[]{:S(2)}, u32[]{:S(2)}) collective-permute-start(f32[]{:T(128)} %add.175), channel_id=1, source_target_pairs={{0,8},{4,12},{8,0},{12,4},{16,24},{20,28},{24,16},{28,20},{1,9},{5... | collective-permute-start | bytes 20 | tf_op jit(solution)/shard_map/ppermute | solution.py:37
  40.7 4.6 %collective-permute-start.2 = (f32[]{:T(128)}, f32[]{:T(128)}, u32[]{:S(2)}, u32[]{:S(2)}) collective-permute-start(f32[]{:T(128)} %add.176), channel_id=1, source_target_pairs={{0,16},{4,20},{8,24},{12,28},{16,0},{20,4},{24,8},{28,12},{1,17},{... | collective-permute-start | bytes 20 | tf_op jit(solution)/shard_map/ppermute | solution.py:37
  46.5 12.5 %collective-permute-start.3 = (bf16[2,12,72,256]{3,2,1,0:T(8,128)(2,1)S(1)}, bf16[2,12,72,256]{3,2,1,0:T(8,128)(2,1)S(1)}, u32[]{:S(2)}, u32[]{:S(2)}) collective-permute-start(bf16[2,12,72,256]{3,2,1,0:T(8,128)(2,1)S(1)} %bitcast.113), channel_id=1, source_target_pairs={{0,1},{1,2},{2,3},{4,5},{5,6},{6,7},{8,9},{9,10},{10,11},{12,13},{... | collective-permute-start | bytes 2654216 | tf_op jit(solution)/shard_map/ppermute | solution.py:19
  47.9 11.2 %collective-permute-start.4 = (bf16[2,12,72,256]{3,2,1,0:T(8,128)(2,1)S(1)}, bf16[2,12,72,256]{3,2,1,0:T(8,128)(2,1)S(1)}, u32[]{:S(2)}, u32[]{:S(2)}) collective-permute-start(bf16[2,12,72,256]{3,2,1,0:T(8,128)(2,1)S(1)} %bitcast.114), channel_id=1, source_target_pairs={{1,0},{2,1},{3,2},{5,4},{6,5},{7,6},{9,8},{10,9},{11,10},{13,12},{... | collective-permute-start | bytes 2654216 | tf_op jit(solution)/shard_map/ppermute | solution.py:20
  57.4 21.4 %collective-permute-start.6 = (f32[2,2,2,2,48,768]{5,4,3,1,0,2:T(8,128)S(1)}, f32[2,2,2,2,48,768]{5,4,3,1,0,2:T(8,128)S(1)}, u32[]{:S(2)}, u32[]{:S(2)}) collective-permute-start(f32[2,2,2,2,48,768]{5,4,3,1,0,2:T(8,128)S(1)} %bitcast.137), channel_id=1, source_target_pairs={{0,1},{1,0},{2,3},{3,2},{4,5},{5,4},{6,7},{7,6},{8,9},{9,8},{10,11... | collective-permute-start | bytes 7077896 | tf_op jit(solution)/shard_map/ppermute | solution.py:37
  66.4 12.3 %collective-permute-start.7 = (f32[2,2,2,2,48,768]{5,4,3,2,0,1:T(8,128)S(1)}, f32[2,2,2,2,48,768]{5,4,3,2,0,1:T(8,128)S(1)}, u32[]{:S(2)}, u32[]{:S(2)}) collective-permute-start(f32[2,2,2,2,48,768]{5,4,3,2,0,1:T(8,128)S(1)} %bitcast.138), channel_id=1, source_target_pairs={{0,1},{1,0},{2,3},{3,2},{4,5},{5,4},{6,7},{7,6},{8,9},{9,8},{10,11... | collective-permute-start | bytes 7077896 | tf_op jit(solution)/shard_map/ppermute | solution.py:37
  78.0 4.6 %collective-permute-start.5 = (f32[2,2,2,2,48,768]{5,4,2,1,0,3:T(8,128)S(1)}, f32[2,2,2,2,48,768]{5,4,2,1,0,3:T(8,128)S(1)}, u32[]{:S(2)}, u32[]{:S(2)}) collective-permute-start(f32[2,2,2,2,48,768]{5,4,2,1,0,3:T(8,128)S(1)} %bitcast.139), channel_id=1, source_target_pairs={{0,1},{1,0},{2,3},{3,2},{4,5},{5,4},{6,7},{7,6},{8,9},{9,8},{10,11... | collective-permute-start | bytes 7077896 | tf_op jit(solution)/shard_map/ppermute | solution.py:37
  84.0 29.6 %collective-permute-start.10 = (f32[2,2,2,48,768]{4,3,2,1,0:T(8,128)S(1)}, f32[2,2,2,48,768]{4,3,2,1,0:T(8,128)S(1)}, u32[]{:S(2)}, u32[]{:S(2)}) collective-permute-start(f32[2,2,2,48,768]{4,3,2,1,0:T(8,128)S(1)} %dynamic-slice_bitcast_fusion), channel_id=1, source_target_pairs={{0,8},{4,12},{8,0},{12,4},{16,24},{20,28},{24,16},{28,20},{1,9},{5... | collective-permute-start | bytes 3538952 | tf_op jit(solution)/shard_map/ppermute | solution.py:37
  85.7 27.9 %collective-permute-start.8 = (f32[2,2,2,48,768]{4,3,2,1,0:T(8,128)S(1)}, f32[2,2,2,48,768]{4,3,2,1,0:T(8,128)S(1)}, u32[]{:S(2)}, u32[]{:S(2)}) collective-permute-start(f32[2,2,2,48,768]{4,3,2,1,0:T(8,128)S(1)} %dynamic-slice_bitcast_fusion.2), channel_id=1, source_target_pairs={{0,2},{1,3},{2,0},{3,1},{4,6},{5,7},{6,4},{7,5},{8,10},{9,11},{10,... | collective-permute-start | bytes 3538952 | tf_op jit(solution)/shard_map/ppermute | solution.py:37
  85.7 27.9 %collective-permute-start.9 = (f32[2,2,2,48,768]{4,3,2,1,0:T(8,128)S(1)}, f32[2,2,2,48,768]{4,3,2,1,0:T(8,128)S(1)}, u32[]{:S(2)}, u32[]{:S(2)}) collective-permute-start(f32[2,2,2,48,768]{4,3,2,1,0:T(8,128)S(1)} %dynamic-slice_bitcast_fusion.1), channel_id=1, source_target_pairs={{0,4},{4,0},{8,12},{12,8},{16,20},{20,16},{24,28},{28,24},{1,5},{5... | collective-permute-start | bytes 3538952 | tf_op jit(solution)/shard_map/ppermute | solution.py:37
  86.2 27.4 %collective-permute-start.11 = (f32[1281]{0:T(1024)S(1)}, f32[1281]{0:T(1024)S(1)}, u32[]{:S(2)}, u32[]{:S(2)}) collective-permute-start(f32[1281]{0:T(1024)S(1)} %pad_maximum_fusion.2), channel_id=1, source_target_pairs={{0,4},{4,0},{8,12},{12,8},{16,20},{20,16},{24,28},{28,24},{1,5},{5... | collective-permute-start | bytes 15380 | tf_op jit(solution)/shard_map/ppermute | solution.py:37
  114.2 14.7 %collective-permute-start.12 = (f32[2,2,48,768]{3,2,1,0:T(8,128)S(1)}, f32[2,2,48,768]{3,2,1,0:T(8,128)S(1)}, u32[]{:S(2)}, u32[]{:S(2)}) collective-permute-start(f32[2,2,48,768]{3,2,1,0:T(8,128)S(1)} %dynamic-slice_bitcast_fusion.5), channel_id=1, source_target_pairs={{0,4},{4,0},{8,12},{12,8},{16,20},{20,16},{24,28},{28,24},{1,5},{5... | collective-permute-start | bytes 1769480 | tf_op jit(solution)/shard_map/ppermute | solution.py:37
  114.8 14.1 %collective-permute-start.13 = (f32[2,2,48,768]{3,2,1,0:T(8,128)S(1)}, f32[2,2,48,768]{3,2,1,0:T(8,128)S(1)}, u32[]{:S(2)}, u32[]{:S(2)}) collective-permute-start(f32[2,2,48,768]{3,2,1,0:T(8,128)S(1)} %dynamic-slice_bitcast_fusion.4), channel_id=1, source_target_pairs={{0,8},{4,12},{8,0},{12,4},{16,24},{20,28},{24,16},{28,20},{1,9},{5... | collective-permute-start | bytes 1769480 | tf_op jit(solution)/shard_map/ppermute | solution.py:37
  115.3 13.7 %collective-permute-start.14 = (f32[2,2,48,768]{3,2,1,0:T(8,128)S(1)}, f32[2,2,48,768]{3,2,1,0:T(8,128)S(1)}, u32[]{:S(2)}, u32[]{:S(2)}) collective-permute-start(f32[2,2,48,768]{3,2,1,0:T(8,128)S(1)} %dynamic-slice_bitcast_fusion.3), channel_id=1, source_target_pairs={{0,2},{1,3},{2,0},{3,1},{4,6},{5,7},{6,4},{7,5},{8,10},{9,11},{10,... | collective-permute-start | bytes 1769480 | tf_op jit(solution)/shard_map/ppermute | solution.py:37
  117.0 12.0 %collective-permute-start.15 = (f32[1281]{0:T(1024)S(1)}, f32[1281]{0:T(1024)S(1)}, u32[]{:S(2)}, u32[]{:S(2)}) collective-permute-start(f32[1281]{0:T(1024)S(1)} %add.186), channel_id=1, source_target_pairs={{0,8},{4,12},{8,0},{12,4},{16,24},{20,28},{24,16},{28,20},{1,9},{5... | collective-permute-start | bytes 15380 | tf_op jit(solution)/shard_map/ppermute | solution.py:37
  129.3 15.7 %collective-permute-start.16 = (f32[2,48,768]{2,1,0:T(8,128)S(1)}, f32[2,48,768]{2,1,0:T(8,128)S(1)}, u32[]{:S(2)}, u32[]{:S(2)}) collective-permute-start(f32[2,48,768]{2,1,0:T(8,128)S(1)} %dynamic-slice_bitcast_fusion.8), channel_id=1, source_target_pairs={{0,8},{4,12},{8,0},{12,4},{16,24},{20,28},{24,16},{28,20},{1,9},{5... | collective-permute-start | bytes 884744 | tf_op jit(solution)/shard_map/ppermute | solution.py:37
  131.0 14.0 %collective-permute-start.17 = (f32[2,48,768]{2,1,0:T(8,128)S(1)}, f32[2,48,768]{2,1,0:T(8,128)S(1)}, u32[]{:S(2)}, u32[]{:S(2)}) collective-permute-start(f32[2,48,768]{2,1,0:T(8,128)S(1)} %dynamic-slice_bitcast_fusion.7), channel_id=1, source_target_pairs={{0,16},{4,20},{8,24},{12,28},{16,0},{20,4},{24,8},{28,12},{1,17},{... | collective-permute-start | bytes 884744 | tf_op jit(solution)/shard_map/ppermute | solution.py:37
  133.5 11.5 %collective-permute-start.18 = (f32[2,48,768]{2,1,0:T(8,128)S(1)}, f32[2,48,768]{2,1,0:T(8,128)S(1)}, u32[]{:S(2)}, u32[]{:S(2)}) collective-permute-start(f32[2,48,768]{2,1,0:T(8,128)S(1)} %dynamic-slice_bitcast_fusion.6), channel_id=1, source_target_pairs={{0,4},{4,0},{8,12},{12,8},{16,20},{20,16},{24,28},{28,24},{1,5},{5... | collective-permute-start | bytes 884744 | tf_op jit(solution)/shard_map/ppermute | solution.py:37
  135.0 10.0 %collective-permute-start.19 = (f32[1281]{0:T(1024)S(1)}, f32[1281]{0:T(1024)S(1)}, u32[]{:S(2)}, u32[]{:S(2)}) collective-permute-start(f32[1281]{0:T(1024)S(1)} %add.194), channel_id=1, source_target_pairs={{0,16},{4,20},{8,24},{12,28},{16,0},{20,4},{24,8},{28,12},{1,17},{... | collective-permute-start | bytes 15380 | tf_op jit(solution)/shard_map/ppermute | solution.py:37
  146.9 6.1 %collective-permute-start.22 = (f32[48,768]{1,0:T(8,128)S(1)}, f32[48,768]{1,0:T(8,128)S(1)}, u32[]{:S(2)}, u32[]{:S(2)}) collective-permute-start(f32[48,768]{1,0:T(8,128)S(1)} %dynamic-slice_bitcast_fusion.9), channel_id=1, source_target_pairs={{0,16},{4,20},{8,24},{12,28},{16,0},{20,4},{24,8},{28,12},{1,17},{... | collective-permute-start | bytes 442376 | tf_op jit(solution)/shard_map/ppermute | solution.py:37
  147.0 5.9 %collective-permute-start.21 = (f32[48,768]{1,0:T(8,128)S(1)}, f32[48,768]{1,0:T(8,128)S(1)}, u32[]{:S(2)}, u32[]{:S(2)}) collective-permute-start(f32[48,768]{1,0:T(8,128)S(1)} %dynamic-slice_bitcast_fusion.10), channel_id=1, source_target_pairs={{0,2},{1,3},{2,0},{3,1},{4,6},{5,7},{6,4},{7,5},{8,10},{9,11},{10,... | collective-permute-start | bytes 442376 | tf_op jit(solution)/shard_map/ppermute | solution.py:37
  148.4 7.8 %collective-permute-start.20 = (f32[48,768]{1,0:T(8,128)S(1)}, f32[48,768]{1,0:T(8,128)S(1)}, u32[]{:S(2)}, u32[]{:S(2)}) collective-permute-start(f32[48,768]{1,0:T(8,128)S(1)} %dynamic-slice_bitcast_fusion.11), channel_id=1, source_target_pairs={{0,16},{4,20},{8,24},{12,28},{16,0},{20,4},{24,8},{28,12},{1,17},{... | collective-permute-start | bytes 442376 | tf_op jit(solution)/shard_map/ppermute | solution.py:37
  (6 other events, 82.5 us)

commit v5 on v4

--- a/solution.py
+++ b/solution.py
@@ -38,7 +38,8 @@
 
 
 def butterfly_sum(x, axes):
-    for axis, bit in index_bits(axes):
+    steps = [a for a in axes if isinstance(a, tuple)] or index_bits(axes)
+    for axis, bit in steps:
         x = jax.tree.map(lambda v, w: v + w, x, exchange(x, axis, bit))
     return x
 
@@ -95,7 +96,12 @@
         jnp.sum(tile_stats[:, out_chans : 2 * out_chans] + local_pix * tile_means * tile_means, 0)
         / per_replica_part
     )
-    weight_total = butterfly_sum(jnp.sum(tile_stats[:, 2 * out_chans]), ("rep",))
+    weight_pair = butterfly_sum(jnp.sum(tile_stats[:, 2 * out_chans]), (("rep", 0),))
+    reps = lax.axis_size("rep")
+    weight_total = weight_pair
+    for k in range(1, reps // 2):
+        pairs = [(i, i ^ (k << 1)) for i in range(reps)]
+        weight_total = weight_total + lax.ppermute(weight_pair, "rep", pairs)
     centre_offset = yvals - column_sum / per_replica_part
     inverse_deviation = lax.rsqrt(variance + 1e-05)
     normalized_input = centre_offset * inverse_deviation

time: 160 us -> 163 us (1.019)
  waiting for transfers between devices: 35.5 us -> 42.9 us
  starting transfers between devices: 35.3 us -> 31.9 us
    ppermute x21 -> x19, starting transfers between devices: 32.7 us -> 20.9 us  [exchange(): return lax.ppermute(x, axis, pairs)]
    ppermute x0 -> x3, starting transfers between devices: none -> 8.34 us  [body(): weight_total = weight_total + lax.ppermute(weight_pair, 'rep', pairs)]
    ppermute x21 -> x19, waiting for transfers between devices: 35.5 us -> 40.3 us  [exchange(): return lax.ppermute(x, axis, pairs)]
    ppermute x0 -> x3, waiting for transfers between devices: none -> 2.67 us  [body(): weight_total = weight_total + lax.ppermute(weight_pair, 'rep', pairs)]
  transfers between devices with their start and end apart: 23 -> 24, of which waited for: 8 -> 9; matrix products, arithmetic and copies ran while one was open for 32% -> 31% of each run, Pallas kernels for 0% -> 0%
where the time goes in v5:
time: 163 us
  waiting for transfers between devices  42.9 us (26%)
  matrix products  40 us (25%)
  starting transfers between devices  31.9 us (20%)
  blocking collectives  19.2 us (12%)
  other arithmetic  15.6 us (10%)
  local copies, waits for them, and re-layouts  6.95 us (4%)
  between operations  6.22 us (4%)
    ppermute x19, waiting for transfers between devices, exchange(): return lax.ppermute(x, axis, pairs)  40.3 us
    ppermute x19, starting transfers between devices, exchange(): return lax.ppermute(x, axis, pairs)  20.9 us
    dot_general x3, matrix products, body(): lax.dot_general(flat_x, cols, (((0,), (0,)), ((), ())), preferred_element...  18 us
    dot_general x2, matrix products, body(): lax.dot_general(shifted.reshape(local_pix, taps, out_chans), conv_weight[...  17.2 us
    psum x1, blocking collectives, body(): tile_stats = lax.psum(slot[:, None] * local_stats[None, :], 'tile')  12.6 us
    ppermute x3, starting transfers between devices, body(): weight_total = weight_total + lax.ppermute(weight_pair, 'rep', pairs)  8.34 us
    psum x1, blocking collectives, body(): lax.psum((jnp.sum(preactivation_gradient, 0), jnp.sum(preactivation_gradi...  6.56 us
  transfers between devices with their start and end apart: 24, of which 9 were waited for; matrix products, arithmetic and copies ran while one was open for 31% of the time, Pallas kernels for 0%

profile of v5, /device:TPU:0, one launch (start us, length us, event | category | flops | bytes accessed | tf_op | source)
XLA Modules:
  0.0 162.8 jit_solution(343972637546819475)
XLA Ops:
  6.5 12.6 %psum.35 = f32[4,513]{1,0:T(4,128)S(1)} all-reduce(f32[4,513]{1,0:T(4,128)S(1)} %broadcast_multiply_fusion), channel_id=1, replica_groups=mesh['rep'=8,'tile'=4] {'tile'}, use_global_device_ids=true, to_apply=%region_3.0 | all-reduce | flops 2052 | bytes 16416 | tf_op jit(solution)/shard_map/psum | solution.py:91
  22.2 1.8 %fusion.47 = (f32[1728]{0:T(1024)S(1)}, f32[1728,3]{0,1:T(4,128)S(1)}) fusion(f32[3,256]{1,0:T(4,128)S(1)} %copy-done, f32[1728,256]{1,0:T(8,128)S(1)} %fusion.26, f32[256]{0:T(256)S(1)} %copy-done.4, f32[256]{0:T(256)S(1)} %copy-done.3), kind=kOutput, calls=%fused_computation.130 | convolution fusion | flops 17255808 | bytes 1802240 | tf_op jit(solution)/shard_map/dot_general | solution.py:110
  24.6 2.2 %fusion.45 = (f32[256]{0:T(256)S(1)}, f32[256]{0:T(256)S(1)}, f32[1728,256]{1,0:T(8,128)S(1)}) fusion(f32[256]{0:T(256)S(1)} %get-tuple-element.125, f32[256]{0:T(256)S(1)} %broadcast_multiply_fusion.2, bf16[2,12,72,256]{3,2,1,0:T(8,128)(2,1)S(1)} %copy-done.2, f32[3,256]{1,0:T(4,128)S(1)} %copy-done, f32[1728,3]{0,1:T(4,128)S(1)} %get-tuple-element.127, ...), kind=kOutput, calls=%fused_computation.128 | convolution fusion | flops 20374336 | bytes 4474368 | tf_op jit(solution)/shard_map/dot_general | solution.py:118
  27.8 6.6 %all-reduce.2 = (f32[1]{0:T(128)}, f32[768]{0:T(1024)S(1)}, f32[256]{0:T(256)S(1)}, f32[256]{0:T(256)S(1)}) all-reduce(f32[1]{0:T(128)} %bitcast.2, f32[768]{0:T(1024)S(1)} %reshape.126, f32[256]{0:T(256)S(1)} %get-tuple-element.99, f32[256]{0:T(256)S(1)} %get-tuple-element.98), channel_id=1, replica_groups=mesh['rep'=8,'tile'=4] {'tile'}, use_global_device_ids=true, to_apply=%region_16.17 | all-reduce | flops 1281 | bytes 10248 | tf_op jit(solution)/shard_map/psum | solution.py:120
  36.3 2.9 %collective-permute-start.1 = (f32[]{:T(128)}, f32[]{:T(128)}, u32[]{:S(2)}, u32[]{:S(2)}) collective-permute-start(f32[]{:T(128)} %add.178), channel_id=1, source_target_pairs={{0,8},{4,12},{8,0},{12,4},{16,24},{20,28},{24,16},{28,20},{1,9},{5... | collective-permute-start | bytes 20 | tf_op jit(solution)/shard_map/ppermute | solution.py:104
  39.3 3.9 %collective-permute-start.2 = (f32[]{:T(128)}, f32[]{:T(128)}, u32[]{:S(2)}, u32[]{:S(2)}) collective-permute-start(f32[]{:T(128)} %add.178), channel_id=1, source_target_pairs={{0,16},{4,20},{8,24},{12,28},{16,0},{20,4},{24,8},{28,12},{1,17},{... | collective-permute-start | bytes 20 | tf_op jit(solution)/shard_map/ppermute | solution.py:104
  45.9 2.7 %collective-permute-done.3 = f32[]{:T(128)} collective-permute-done((f32[]{:T(128)}, f32[]{:T(128)}, u32[]{:S(2)}, u32[]{:S(2)}) %collective-permute-start.3) | collective-permute-done | bytes 36 | tf_op jit(solution)/shard_map/ppermute | solution.py:104
  53.3 6.7 %fusion.14 = f32[1536,768]{1,0:T(8,128)S(1)} fusion(bf16[1728,1536]{1,0:T(8,128)(2,1)} %bitcast.142, bf16[1728,256]{1,0:T(8,128)(2,1)S(1)} %bitcast.133, bf16[1728,256]{1,0:T(8,128)(2,1)S(1)} %multiply_convert_fusion, bf16[1728,256]{1,0:T(8,128)(2,1)S(1)} %bitcast.135), kind=kOutput, calls=%fused_computation.20 | convolution fusion | flops 4084826112 | bytes 12681216 | tf_op jit(solution)/shard_map/dot_general | solution.py:174
  60.7 1.7 %collective-permute-start.7 = (f32[2,2,2,2,48,768]{5,4,3,1,0,2:T(8,128)S(1)}, f32[2,2,2,2,48,768]{5,4,3,1,0,2:T(8,128)S(1)}, u32[]{:S(2)}, u32[]{:S(2)}) collective-permute-start(f32[2,2,2,2,48,768]{5,4,3,1,0,2:T(8,128)S(1)} %bitcast.137), channel_id=1, source_target_pairs={{0,1},{1,0},{2,3},{3,2},{4,5},{5,4},{6,7},{7,6},{8,9},{9,8},{10,11... | collective-permute-start | bytes 7077896 | tf_op jit(solution)/shard_map/ppermute | solution.py:37
  62.3 1.9 %fusion.5 = bf16[2,36,96,256]{3,2,1,0:T(8,128)(2,1)S(1)} fusion(bf16[2,12,72,256]{3,2,1,0:T(8,128)(2,1)S(1)} %collective-permute-done.5, bf16[2,12,72,256]{3,2,1,0:T(8,128)(2,1)S(1)} %bitcast.116, bf16[2,12,72,256]{3,2,1,0:T(8,128)(2,1)S(1)} %collective-permute-done.4), kind=kLoop, calls=%fused_computation.10 | loop fusion | flops 21233664 | bytes 6193152 | tf_op jit(solution)/shard_map/concatenate | solution.py:21
  64.6 4.5 %fusion.20 = f32[1536,768]{1,0:T(8,128)S(1)} fusion(bf16[1728,1536]{1,0:T(8,128)(2,1)S(1)} %bitcast.146, bf16[1728,256]{1,0:T(8,128)(2,1)S(1)} %bitcast.125, bf16[1728,256]{1,0:T(8,128)(2,1)S(1)} %bitcast.121, bf16[1728,256]{1,0:T(8,128)(2,1)S(1)} %bitcast.127), kind=kOutput, calls=%fused_computation.26 | convolution fusion | flops 4084826112 | bytes 12681216 | tf_op jit(solution)/shard_map/dot_general | solution.py:174
  69.7 4.2 %collective-permute-start.8 = (f32[2,2,2,2,48,768]{5,4,3,2,0,1:T(8,128)S(1)}, f32[2,2,2,2,48,768]{5,4,3,2,0,1:T(8,128)S(1)}, u32[]{:S(2)}, u32[]{:S(2)}) collective-permute-start(f32[2,2,2,2,48,768]{5,4,3,2,0,1:T(8,128)S(1)} %bitcast.138), channel_id=1, source_target_pairs={{0,1},{1,0},{2,3},{3,2},{4,5},{5,4},{6,7},{7,6},{8,9},{9,8},{10,11... | collective-permute-start | bytes 7077896 | tf_op jit(solution)/shard_map/ppermute | solution.py:37
  73.9 6.7 %fusion.8 = f32[1536,768]{1,0:T(8,128)S(1)} fusion(bf16[1728,1536]{1,0:T(8,128)(2,1)} %bitcast.143, bf16[1728,256]{1,0:T(8,128)(2,1)S(1)} %bitcast.129, bf16[1728,256]{1,0:T(8,128)(2,1)S(1)} %bitcast.123, bf16[1728,256]{1,0:T(8,128)(2,1)S(1)} %bitcast.131), kind=kOutput, calls=%fused_computation.14 | convolution fusion | flops 4084826112 | bytes 12681216 | tf_op jit(solution)/shard_map/dot_general | solution.py:174
  82.0 3.9 %collective-permute-done.6 = f32[2,2,2,2,48,768]{5,4,2,1,0,3:T(8,128)S(1)} collective-permute-done((f32[2,2,2,2,48,768]{5,4,2,1,0,3:T(8,128)S(1)}, f32[2,2,2,2,48,768]{5,4,2,1,0,3:T(8,128)S(1)}, u32[]{:S(2)}, u32[]{:S(2)}) %collective-permute-start.6) | collective-permute-done | bytes 2359328 | tf_op jit(solution)/shard_map/ppermute | solution.py:37
  89.4 8.6 %bitcast_convert_fusion.1 = bf16[1728,768]{1,0:T(8,128)(2,1)S(1)} fusion(bf16[1728,9,256]{2,0,1:T(8,128)(2,1)S(1)} %constant_dynamic-update-slice_fusion, bf16[9,1536,256]{2,1,0:T(8,128)(2,1)} %param.10), kind=kOutput, calls=%fused_computation.5 | convolution fusion | flops 6116622336 | bytes 14155776 | tf_op jit(solution)/shard_map/dot_general | solution.py:182
  98.0 17.6 %collective-permute-done.12 = f32[1281]{0:T(1024)S(1)} collective-permute-done((f32[1281]{0:T(1024)S(1)}, f32[1281]{0:T(1024)S(1)}, u32[]{:S(2)}, u32[]{:S(2)}) %collective-permute-start.12) | collective-permute-done | bytes 5156 | tf_op jit(solution)/shard_map/ppermute | solution.py:37
  117.9 1.7 %collective-permute-start.14 = (f32[2,2,48,768]{3,2,1,0:T(8,128)S(1)}, f32[2,2,48,768]{3,2,1,0:T(8,128)S(1)}, u32[]{:S(2)}, u32[]{:S(2)}) collective-permute-start(f32[2,2,48,768]{3,2,1,0:T(8,128)S(1)} %dynamic-slice_bitcast_fusion.4), channel_id=1, source_target_pairs={{0,8},{4,12},{8,0},{12,4},{16,24},{20,28},{24,16},{28,20},{1,9},{5... | collective-permute-start | bytes 1769480 | tf_op jit(solution)/shard_map/ppermute | solution.py:37
  120.2 8.6 %bitcast_convert_fusion = bf16[1728,768]{1,0:T(8,128)(2,1)S(1)} fusion(bf16[1728,9,256]{2,0,1:T(8,128)(2,1)S(1)} %constant_dynamic-update-slice_fusion, bf16[9,1536,256]{2,1,0:T(8,128)(2,1)} %param.10), kind=kOutput, calls=%fused_computation.4 | convolution fusion | flops 6116622336 | bytes 14155776 | tf_op jit(solution)/shard_map/dot_general | solution.py:182
  128.7 3.2 %collective-permute-done.16 = f32[1281]{0:T(1024)S(1)} collective-permute-done((f32[1281]{0:T(1024)S(1)}, f32[1281]{0:T(1024)S(1)}, u32[]{:S(2)}, u32[]{:S(2)}) %collective-permute-start.16) | collective-permute-done | bytes 5156 | tf_op jit(solution)/shard_map/ppermute | solution.py:37
  135.4 2.3 %collective-permute-start.20 = (f32[1281]{0:T(1024)S(1)}, f32[1281]{0:T(1024)S(1)}, u32[]{:S(2)}, u32[]{:S(2)}) collective-permute-start(f32[1281]{0:T(1024)S(1)} %add.198), channel_id=1, source_target_pairs={{0,16},{4,20},{8,24},{12,28},{16,0},{20,4},{24,8},{28,12},{1,17},{... | collective-permute-start | bytes 15380 | tf_op jit(solution)/shard_map/ppermute | solution.py:37
  137.7 2.8 %pad_maximum_fusion = bf16[1728,1536]{1,0:T(8,128)(2,1)} fusion(bf16[1728,768]{1,0:T(8,128)(2,1)S(1)} %bitcast_convert_fusion, bf16[1728,768]{1,0:T(8,128)(2,1)S(1)} %bitcast_convert_fusion.1), kind=kLoop, calls=%fused_computation.3 | loop fusion | flops 10616832 | bytes 10616832 | tf_op jit(solution)/shard_map/concatenate | solution.py:230
  140.5 9.1 %collective-permute-done.20 = f32[1281]{0:T(1024)S(1)} collective-permute-done((f32[1281]{0:T(1024)S(1)}, f32[1281]{0:T(1024)S(1)}, u32[]{:S(2)}, u32[]{:S(2)}) %collective-permute-start.20) | collective-permute-done | bytes 5156 | tf_op jit(solution)/shard_map/ppermute | solution.py:37
  151.8 3.0 %collective-permute-start.21 = (f32[48,768]{1,0:T(8,128)S(1)}, f32[48,768]{1,0:T(8,128)S(1)}, u32[]{:S(2)}, u32[]{:S(2)}) collective-permute-start(f32[48,768]{1,0:T(8,128)S(1)} %dynamic-slice_bitcast_fusion.11), channel_id=1, source_target_pairs={{0,16},{4,20},{8,24},{12,28},{16,0},{20,4},{24,8},{28,12},{1,17},{... | collective-permute-start | bytes 442376 | tf_op jit(solution)/shard_map/ppermute | solution.py:37
  155.3 3.8 %collective-permute-done.23 = f32[48,768]{1,0:T(8,128)S(1)} collective-permute-done((f32[48,768]{1,0:T(8,128)S(1)}, f32[48,768]{1,0:T(8,128)S(1)}, u32[]{:S(2)}, u32[]{:S(2)}) %collective-permute-start.23) | collective-permute-done | bytes 147488 | tf_op jit(solution)/shard_map/ppermute | solution.py:37
  (125 shorter events, 33.7 us)
Async XLA Ops:
  19.8 15.3 %collective-permute-start = (f32[]{:T(128)}, f32[]{:T(128)}, u32[]{:S(2)}, u32[]{:S(2)}) collective-permute-start(f32[]{:T(128)} %slice_reduce_fusion.1), channel_id=1, source_target_pairs={{0,4},{4,0},{8,12},{12,8},{16,20},{20,16},{24,28},{28,24},{1,5},{5... | collective-permute-start | bytes 20 | tf_op jit(solution)/shard_map/ppermute | solution.py:37
  36.3 8.3 %collective-permute-start.1 = (f32[]{:T(128)}, f32[]{:T(128)}, u32[]{:S(2)}, u32[]{:S(2)}) collective-permute-start(f32[]{:T(128)} %add.178), channel_id=1, source_target_pairs={{0,8},{4,12},{8,0},{12,4},{16,24},{20,28},{24,16},{28,20},{1,9},{5... | collective-permute-start | bytes 20 | tf_op jit(solution)/shard_map/ppermute | solution.py:104
  39.3 6.0 %collective-permute-start.2 = (f32[]{:T(128)}, f32[]{:T(128)}, u32[]{:S(2)}, u32[]{:S(2)}) collective-permute-start(f32[]{:T(128)} %add.178), channel_id=1, source_target_pairs={{0,16},{4,20},{8,24},{12,28},{16,0},{20,4},{24,8},{28,12},{1,17},{... | collective-permute-start | bytes 20 | tf_op jit(solution)/shard_map/ppermute | solution.py:104
  43.1 5.4 %collective-permute-start.3 = (f32[]{:T(128)}, f32[]{:T(128)}, u32[]{:S(2)}, u32[]{:S(2)}) collective-permute-start(f32[]{:T(128)} %add.178), channel_id=1, source_target_pairs={{0,24},{4,28},{8,16},{12,20},{16,8},{20,12},{24,0},{28,4},{1,25},{... | collective-permute-start | bytes 20 | tf_op jit(solution)/shard_map/ppermute | solution.py:104
  49.8 12.5 %collective-permute-start.4 = (bf16[2,12,72,256]{3,2,1,0:T(8,128)(2,1)S(1)}, bf16[2,12,72,256]{3,2,1,0:T(8,128)(2,1)S(1)}, u32[]{:S(2)}, u32[]{:S(2)}) collective-permute-start(bf16[2,12,72,256]{3,2,1,0:T(8,128)(2,1)S(1)} %bitcast.113), channel_id=1, source_target_pairs={{0,1},{1,2},{2,3},{4,5},{5,6},{6,7},{8,9},{9,10},{10,11},{12,13},{... | collective-permute-start | bytes 2654216 | tf_op jit(solution)/shard_map/ppermute | solution.py:19
  51.2 11.2 %collective-permute-start.5 = (bf16[2,12,72,256]{3,2,1,0:T(8,128)(2,1)S(1)}, bf16[2,12,72,256]{3,2,1,0:T(8,128)(2,1)S(1)}, u32[]{:S(2)}, u32[]{:S(2)}) collective-permute-start(bf16[2,12,72,256]{3,2,1,0:T(8,128)(2,1)S(1)} %bitcast.114), channel_id=1, source_target_pairs={{1,0},{2,1},{3,2},{5,4},{6,5},{7,6},{9,8},{10,9},{11,10},{13,12},{... | collective-permute-start | bytes 2654216 | tf_op jit(solution)/shard_map/ppermute | solution.py:20
  60.7 21.4 %collective-permute-start.7 = (f32[2,2,2,2,48,768]{5,4,3,1,0,2:T(8,128)S(1)}, f32[2,2,2,2,48,768]{5,4,3,1,0,2:T(8,128)S(1)}, u32[]{:S(2)}, u32[]{:S(2)}) collective-permute-start(f32[2,2,2,2,48,768]{5,4,3,1,0,2:T(8,128)S(1)} %bitcast.137), channel_id=1, source_target_pairs={{0,1},{1,0},{2,3},{3,2},{4,5},{5,4},{6,7},{7,6},{8,9},{9,8},{10,11... | collective-permute-start | bytes 7077896 | tf_op jit(solution)/shard_map/ppermute | solution.py:37
  69.7 12.3 %collective-permute-start.8 = (f32[2,2,2,2,48,768]{5,4,3,2,0,1:T(8,128)S(1)}, f32[2,2,2,2,48,768]{5,4,3,2,0,1:T(8,128)S(1)}, u32[]{:S(2)}, u32[]{:S(2)}) collective-permute-start(f32[2,2,2,2,48,768]{5,4,3,2,0,1:T(8,128)S(1)} %bitcast.138), channel_id=1, source_target_pairs={{0,1},{1,0},{2,3},{3,2},{4,5},{5,4},{6,7},{7,6},{8,9},{9,8},{10,11... | collective-permute-start | bytes 7077896 | tf_op jit(solution)/shard_map/ppermute | solution.py:37
  81.3 4.6 %collective-permute-start.6 = (f32[2,2,2,2,48,768]{5,4,2,1,0,3:T(8,128)S(1)}, f32[2,2,2,2,48,768]{5,4,2,1,0,3:T(8,128)S(1)}, u32[]{:S(2)}, u32[]{:S(2)}) collective-permute-start(f32[2,2,2,2,48,768]{5,4,2,1,0,3:T(8,128)S(1)} %bitcast.139), channel_id=1, source_target_pairs={{0,1},{1,0},{2,3},{3,2},{4,5},{5,4},{6,7},{7,6},{8,9},{9,8},{10,11... | collective-permute-start | bytes 7077896 | tf_op jit(solution)/shard_map/ppermute | solution.py:37
  87.3 28.3 %collective-permute-start.10 = (f32[2,2,2,48,768]{4,3,2,1,0:T(8,128)S(1)}, f32[2,2,2,48,768]{4,3,2,1,0:T(8,128)S(1)}, u32[]{:S(2)}, u32[]{:S(2)}) collective-permute-start(f32[2,2,2,48,768]{4,3,2,1,0:T(8,128)S(1)} %dynamic-slice_bitcast_fusion.1), channel_id=1, source_target_pairs={{0,4},{4,0},{8,12},{12,8},{16,20},{20,16},{24,28},{28,24},{1,5},{5... | collective-permute-start | bytes 3538952 | tf_op jit(solution)/shard_map/ppermute | solution.py:37
  87.9 27.7 %collective-permute-start.11 = (f32[2,2,2,48,768]{4,3,2,1,0:T(8,128)S(1)}, f32[2,2,2,48,768]{4,3,2,1,0:T(8,128)S(1)}, u32[]{:S(2)}, u32[]{:S(2)}) collective-permute-start(f32[2,2,2,48,768]{4,3,2,1,0:T(8,128)S(1)} %dynamic-slice_bitcast_fusion), channel_id=1, source_target_pairs={{0,8},{4,12},{8,0},{12,4},{16,24},{20,28},{24,16},{28,20},{1,9},{5... | collective-permute-start | bytes 3538952 | tf_op jit(solution)/shard_map/ppermute | solution.py:37
  87.9 27.7 %collective-permute-start.9 = (f32[2,2,2,48,768]{4,3,2,1,0:T(8,128)S(1)}, f32[2,2,2,48,768]{4,3,2,1,0:T(8,128)S(1)}, u32[]{:S(2)}, u32[]{:S(2)}) collective-permute-start(f32[2,2,2,48,768]{4,3,2,1,0:T(8,128)S(1)} %dynamic-slice_bitcast_fusion.2), channel_id=1, source_target_pairs={{0,2},{1,3},{2,0},{3,1},{4,6},{5,7},{6,4},{7,5},{8,10},{9,11},{10,... | collective-permute-start | bytes 3538952 | tf_op jit(solution)/shard_map/ppermute | solution.py:37
  87.9 27.6 %collective-permute-start.12 = (f32[1281]{0:T(1024)S(1)}, f32[1281]{0:T(1024)S(1)}, u32[]{:S(2)}, u32[]{:S(2)}) collective-permute-start(f32[1281]{0:T(1024)S(1)} %pad_maximum_fusion.2), channel_id=1, source_target_pairs={{0,4},{4,0},{8,12},{12,8},{16,20},{20,16},{24,28},{28,24},{1,5},{5... | collective-permute-start | bytes 15380 | tf_op jit(solution)/shard_map/ppermute | solution.py:37
  116.3 15.7 %collective-permute-start.13 = (f32[2,2,48,768]{3,2,1,0:T(8,128)S(1)}, f32[2,2,48,768]{3,2,1,0:T(8,128)S(1)}, u32[]{:S(2)}, u32[]{:S(2)}) collective-permute-start(f32[2,2,48,768]{3,2,1,0:T(8,128)S(1)} %dynamic-slice_bitcast_fusion.5), channel_id=1, source_target_pairs={{0,4},{4,0},{8,12},{12,8},{16,20},{20,16},{24,28},{28,24},{1,5},{5... | collective-permute-start | bytes 1769480 | tf_op jit(solution)/shard_map/ppermute | solution.py:37
  117.9 14.1 %collective-permute-start.14 = (f32[2,2,48,768]{3,2,1,0:T(8,128)S(1)}, f32[2,2,48,768]{3,2,1,0:T(8,128)S(1)}, u32[]{:S(2)}, u32[]{:S(2)}) collective-permute-start(f32[2,2,48,768]{3,2,1,0:T(8,128)S(1)} %dynamic-slice_bitcast_fusion.4), channel_id=1, source_target_pairs={{0,8},{4,12},{8,0},{12,4},{16,24},{20,28},{24,16},{28,20},{1,9},{5... | collective-permute-start | bytes 1769480 | tf_op jit(solution)/shard_map/ppermute | solution.py:37
  119.6 13.3 %collective-permute-start.15 = (f32[2,2,48,768]{3,2,1,0:T(8,128)S(1)}, f32[2,2,48,768]{3,2,1,0:T(8,128)S(1)}, u32[]{:S(2)}, u32[]{:S(2)}) collective-permute-start(f32[2,2,48,768]{3,2,1,0:T(8,128)S(1)} %dynamic-slice_bitcast_fusion.3), channel_id=1, source_target_pairs={{0,2},{1,3},{2,0},{3,1},{4,6},{5,7},{6,4},{7,5},{8,10},{9,11},{10,... | collective-permute-start | bytes 1769480 | tf_op jit(solution)/shard_map/ppermute | solution.py:37
  119.9 12.1 %collective-permute-start.16 = (f32[1281]{0:T(1024)S(1)}, f32[1281]{0:T(1024)S(1)}, u32[]{:S(2)}, u32[]{:S(2)}) collective-permute-start(f32[1281]{0:T(1024)S(1)} %add.190), channel_id=1, source_target_pairs={{0,8},{4,12},{8,0},{12,4},{16,24},{20,28},{24,16},{28,20},{1,9},{5... | collective-permute-start | bytes 15380 | tf_op jit(solution)/shard_map/ppermute | solution.py:37
  133.3 16.3 %collective-permute-start.17 = (f32[2,48,768]{2,1,0:T(8,128)S(1)}, f32[2,48,768]{2,1,0:T(8,128)S(1)}, u32[]{:S(2)}, u32[]{:S(2)}) collective-permute-start(f32[2,48,768]{2,1,0:T(8,128)S(1)} %dynamic-slice_bitcast_fusion.8), channel_id=1, source_target_pairs={{0,8},{4,12},{8,0},{12,4},{16,24},{20,28},{24,16},{28,20},{1,9},{5... | collective-permute-start | bytes 884744 | tf_op jit(solution)/shard_map/ppermute | solution.py:37
  134.0 15.6 %collective-permute-start.18 = (f32[2,48,768]{2,1,0:T(8,128)S(1)}, f32[2,48,768]{2,1,0:T(8,128)S(1)}, u32[]{:S(2)}, u32[]{:S(2)}) collective-permute-start(f32[2,48,768]{2,1,0:T(8,128)S(1)} %dynamic-slice_bitcast_fusion.7), channel_id=1, source_target_pairs={{0,16},{4,20},{8,24},{12,28},{16,0},{20,4},{24,8},{28,12},{1,17},{... | collective-permute-start | bytes 884744 | tf_op jit(solution)/shard_map/ppermute | solution.py:37
  134.9 14.7 %collective-permute-start.19 = (f32[2,48,768]{2,1,0:T(8,128)S(1)}, f32[2,48,768]{2,1,0:T(8,128)S(1)}, u32[]{:S(2)}, u32[]{:S(2)}) collective-permute-start(f32[2,48,768]{2,1,0:T(8,128)S(1)} %dynamic-slice_bitcast_fusion.6), channel_id=1, source_target_pairs={{0,4},{4,0},{8,12},{12,8},{16,20},{20,16},{24,28},{28,24},{1,5},{5... | collective-permute-start | bytes 884744 | tf_op jit(solution)/shard_map/ppermute | solution.py:37
  135.4 14.2 %collective-permute-start.20 = (f32[1281]{0:T(1024)S(1)}, f32[1281]{0:T(1024)S(1)}, u32[]{:S(2)}, u32[]{:S(2)}) collective-permute-start(f32[1281]{0:T(1024)S(1)} %add.198), channel_id=1, source_target_pairs={{0,16},{4,20},{8,24},{12,28},{16,0},{20,4},{24,8},{28,12},{1,17},{... | collective-permute-start | bytes 15380 | tf_op jit(solution)/shard_map/ppermute | solution.py:37
  151.5 7.7 %collective-permute-start.23 = (f32[48,768]{1,0:T(8,128)S(1)}, f32[48,768]{1,0:T(8,128)S(1)}, u32[]{:S(2)}, u32[]{:S(2)}) collective-permute-start(f32[48,768]{1,0:T(8,128)S(1)} %dynamic-slice_bitcast_fusion.9), channel_id=1, source_target_pairs={{0,16},{4,20},{8,24},{12,28},{16,0},{20,4},{24,8},{28,12},{1,17},{... | collective-permute-start | bytes 442376 | tf_op jit(solution)/shard_map/ppermute | solution.py:37
  151.6 7.5 %collective-permute-start.22 = (f32[48,768]{1,0:T(8,128)S(1)}, f32[48,768]{1,0:T(8,128)S(1)}, u32[]{:S(2)}, u32[]{:S(2)}) collective-permute-start(f32[48,768]{1,0:T(8,128)S(1)} %dynamic-slice_bitcast_fusion.10), channel_id=1, source_target_pairs={{0,2},{1,3},{2,0},{3,1},{4,6},{5,7},{6,4},{7,5},{8,10},{9,11},{10,... | collective-permute-start | bytes 442376 | tf_op jit(solution)/shard_map/ppermute | solution.py:37
  151.8 9.0 %collective-permute-start.21 = (f32[48,768]{1,0:T(8,128)S(1)}, f32[48,768]{1,0:T(8,128)S(1)}, u32[]{:S(2)}, u32[]{:S(2)}) collective-permute-start(f32[48,768]{1,0:T(8,128)S(1)} %dynamic-slice_bitcast_fusion.11), channel_id=1, source_target_pairs={{0,16},{4,20},{8,24},{12,28},{16,0},{20,4},{24,8},{28,12},{1,17},{... | collective-permute-start | bytes 442376 | tf_op jit(solution)/shard_map/ppermute | solution.py:37
  (7 other events, 104.0 us)

commit v6 on v4

--- a/solution.py
+++ b/solution.py
@@ -189,7 +189,7 @@
     sends = [lax.dynamic_index_in_dim(p, 1 - mine, ax, keepdims=False) for p in parts]
     received = lax.optimization_barrier([exchange(v, axis, bit) for v in sends])
     bit_axes.pop(ax)
-    pieces = [keeps[s] + received[s] for s in range(3)]
+    pieces = [(keeps[s], received[s]) for s in range(3)]
     small_bits = index_bits(("rep",))
     axes_of = [list(bit_axes) for s in range(3)]
     for step in range(len(rest)):
@@ -198,8 +198,15 @@
             axis, bit, combined = orders[s][step]
             ax = axes_of[s].index(combined)
             mine = (lax.axis_index(axis) >> bit) & 1
-            keeps.append(lax.dynamic_index_in_dim(pieces[s], mine, ax, keepdims=False))
-            sends.append(lax.dynamic_index_in_dim(pieces[s], 1 - mine, ax, keepdims=False))
+            own, other = pieces[s]
+            keeps.append(
+                lax.dynamic_index_in_dim(own, mine, ax, keepdims=False)
+                + lax.dynamic_index_in_dim(other, mine, ax, keepdims=False)
+            )
+            sends.append(
+                lax.dynamic_index_in_dim(own, 1 - mine, ax, keepdims=False)
+                + lax.dynamic_index_in_dim(other, 1 - mine, ax, keepdims=False)
+            )
             axes_of[s].pop(ax)
         received = []
         if step < len(small_bits):
@@ -212,8 +219,8 @@
             received = lax.optimization_barrier(received)
         if step < len(small_bits):
             packed = packed + received.pop()
-        pieces = [keeps[s] + received[s] for s in range(3)]
-    grad_weight = jnp.concatenate(pieces, 1).reshape(rows, taps, out_chans)
+        pieces = [(keeps[s], received[s]) for s in range(3)]
+    grad_weight = jnp.concatenate([own + other for own, other in pieces], 1).reshape(rows, taps, out_chans)
 
     for step in range(len(rest), len(small_bits)):
         packed = packed + exchange(packed, *small_bits[step])

time: 160 us -> 168 us (1.050)
  local copies, waits for them, and re-layouts: 6.95 us -> 14.2 us
  waiting for transfers between devices: 35.5 us -> 41 us
  matrix products: 40 us -> 38.1 us
    unnamed x23 -> x27, local copies, waits for them, and re-layouts: 1.31 us -> 8.7 us
    ppermute x21, waiting for transfers between devices: 35.5 us -> 41 us  [exchange(): return lax.ppermute(x, axis, pairs)]
    dot_general x2, matrix products: 17.2 us -> 13.4 us  [body(): lax.dot_general(shifted.reshape(local_pix, taps, out_chans), conv_weight[...]
    ppermute x21, starting transfers between devices: 32.7 us -> 29.8 us  [exchange(): return lax.ppermute(x, axis, pairs)]
    dynamic_slice x6 -> x0, local copies, waits for them, and re-layouts: 1.86 us -> none  [the longest x3 1.29 us: body(): lax.dynamic_index_in_dim(p, mine, ax, keepdims=False)]
    dot_general x3, matrix products: 18 us -> 19.7 us  [body(): lax.dot_general(flat_x, cols, (((0,), (0,)), ((), ())), preferred_element...]
    ppermute x1, starting transfers between devices: 1.35 us -> 3.09 us  [padded(): before = lax.ppermute(last, axis, up)]
  transfers between devices with their start and end apart: 23 -> 23, of which waited for: 8 -> 13; matrix products, arithmetic and copies ran while one was open for 32% -> 34% of each run, Pallas kernels for 0% -> 0%
where the time goes in v6:
time: 168 us
  waiting for transfers between devices  41 us (24%)
  matrix products  38.1 us (23%)
  starting transfers between devices  34.2 us (20%)
  blocking collectives  19.2 us (11%)
  other arithmetic  15.7 us (9%)
  local copies, waits for them, and re-layouts  14.2 us (8%)
  between operations  5.48 us (3%)
    ppermute x21, waiting for transfers between devices, exchange(): return lax.ppermute(x, axis, pairs)  41 us
    ppermute x21, starting transfers between devices, exchange(): return lax.ppermute(x, axis, pairs)  29.8 us
    dot_general x3, matrix products, body(): lax.dot_general(flat_x, cols, (((0,), (0,)), ((), ())), preferred_element...  19.7 us
    dot_general x2, matrix products, body(): lax.dot_general(shifted.reshape(local_pix, taps, out_chans), conv_weight[...  13.4 us
    psum x1, blocking collectives, body(): tile_stats = lax.psum(slot[:, None] * local_stats[None, :], 'tile')  12.6 us
    unnamed x27, local copies, waits for them, and re-layouts  8.7 us
    psum x1, blocking collectives, body(): lax.psum((jnp.sum(preactivation_gradient, 0), jnp.sum(preactivation_gradi...  6.58 us
  transfers between devices with their start and end apart: 23, of which 13 were waited for; matrix products, arithmetic and copies ran while one was open for 34% of the time, Pallas kernels for 0%

profile of v6, /device:TPU:0, one launch (start us, length us, event | category | flops | bytes accessed | tf_op | source)
XLA Modules:
  0.0 167.9 jit_solution(15483555510008098320)
XLA Ops:
  6.5 12.6 %psum.35 = f32[4,513]{1,0:T(4,128)S(1)} all-reduce(f32[4,513]{1,0:T(4,128)S(1)} %broadcast_multiply_fusion), channel_id=1, replica_groups=mesh['rep'=8,'tile'=4] {'tile'}, use_global_device_ids=true, to_apply=%region_3.0 | all-reduce | flops 2052 | bytes 16416 | tf_op jit(solution)/shard_map/psum | solution.py:90
  22.2 1.8 %fusion.53 = (f32[1728]{0:T(1024)S(1)}, f32[1728,3]{0,1:T(4,128)S(1)}) fusion(f32[3,256]{1,0:T(4,128)S(1)} %copy-done, f32[1728,256]{1,0:T(8,128)S(1)} %fusion.26, f32[256]{0:T(256)S(1)} %copy-done.4, f32[256]{0:T(256)S(1)} %copy-done.3), kind=kOutput, calls=%fused_computation.138 | convolution fusion | flops 17255808 | bytes 1802240 | tf_op jit(solution)/shard_map/dot_general | solution.py:104
  25.6 2.2 %fusion.51 = (f32[256]{0:T(256)S(1)}, f32[256]{0:T(256)S(1)}, f32[1728,256]{1,0:T(8,128)S(1)}) fusion(f32[256]{0:T(256)S(1)} %get-tuple-element.153, f32[256]{0:T(256)S(1)} %broadcast_multiply_fusion.2, bf16[2,12,72,256]{3,2,1,0:T(8,128)(2,1)S(1)} %copy-done.2, f32[3,256]{1,0:T(4,128)S(1)} %copy-done, f32[1728,3]{0,1:T(4,128)S(1)} %get-tuple-element.155, ...), kind=kOutput, calls=%fused_computation.136 | convolution fusion | flops 20374336 | bytes 4474368 | tf_op jit(solution)/shard_map/dot_general | solution.py:112
  27.9 6.6 %all-reduce.2 = (f32[1]{0:T(128)}, f32[768]{0:T(1024)S(1)}, f32[256]{0:T(256)S(1)}, f32[256]{0:T(256)S(1)}) all-reduce(f32[1]{0:T(128)} %bitcast.2, f32[768]{0:T(1024)S(1)} %reshape.168, f32[256]{0:T(256)S(1)} %get-tuple-element.111, f32[256]{0:T(256)S(1)} %get-tuple-element.110), channel_id=1, replica_groups=mesh['rep'=8,'tile'=4] {'tile'}, use_global_device_ids=true, to_apply=%region_16.17 | all-reduce | flops 1281 | bytes 10248 | tf_op jit(solution)/shard_map/psum | solution.py:114
  36.4 2.9 %collective-permute-start.1 = (f32[]{:T(128)}, f32[]{:T(128)}, u32[]{:S(2)}, u32[]{:S(2)}) collective-permute-start(f32[]{:T(128)} %add.319), channel_id=1, source_target_pairs={{0,8},{4,12},{8,0},{12,4},{16,24},{20,28},{24,16},{28,20},{1,9},{5... | collective-permute-start | bytes 20 | tf_op jit(solution)/shard_map/ppermute | solution.py:37
  40.6 4.0 %collective-permute-start.2 = (f32[]{:T(128)}, f32[]{:T(128)}, u32[]{:S(2)}, u32[]{:S(2)}) collective-permute-start(f32[]{:T(128)} %add.320), channel_id=1, source_target_pairs={{0,16},{4,20},{8,24},{12,28},{16,0},{20,4},{24,8},{28,12},{1,17},{... | collective-permute-start | bytes 20 | tf_op jit(solution)/shard_map/ppermute | solution.py:37
  47.6 3.1 %collective-permute-start.3 = (bf16[2,12,72,256]{3,2,1,0:T(8,128)(2,1)S(1)}, bf16[2,12,72,256]{3,2,1,0:T(8,128)(2,1)S(1)}, u32[]{:S(2)}, u32[]{:S(2)}) collective-permute-start(bf16[2,12,72,256]{3,2,1,0:T(8,128)(2,1)S(1)} %bitcast.161), channel_id=1, source_target_pairs={{0,1},{1,2},{2,3},{4,5},{5,6},{6,7},{8,9},{9,10},{10,11},{12,13},{... | collective-permute-start | bytes 2654216 | tf_op jit(solution)/shard_map/ppermute | solution.py:19
  51.5 6.7 %fusion.14 = f32[1536,768]{1,0:T(8,128)S(1)} fusion(bf16[1728,1536]{1,0:T(8,128)(2,1)} %bitcast.193, bf16[1728,256]{1,0:T(8,128)(2,1)S(1)} %bitcast.183, bf16[1728,256]{1,0:T(8,128)(2,1)S(1)} %multiply_convert_fusion, bf16[1728,256]{1,0:T(8,128)(2,1)S(1)} %bitcast.185), kind=kOutput, calls=%fused_computation.20 | convolution fusion | flops 4084826112 | bytes 12681216 | tf_op jit(solution)/shard_map/dot_general | solution.py:168
  58.7 1.9 %fusion.5 = bf16[2,36,96,256]{3,2,1,0:T(8,128)(2,1)S(1)} fusion(bf16[2,12,72,256]{3,2,1,0:T(8,128)(2,1)S(1)} %collective-permute-done.4, bf16[2,12,72,256]{3,2,1,0:T(8,128)(2,1)S(1)} %bitcast.163, bf16[2,12,72,256]{3,2,1,0:T(8,128)(2,1)S(1)} %collective-permute-done.3), kind=kLoop, calls=%fused_computation.10 | loop fusion | flops 21233664 | bytes 6193152 | tf_op jit(solution)/shard_map/concatenate | solution.py:21
  61.0 6.5 %fusion.20 = f32[1536,768]{1,0:T(8,128)S(1)} fusion(bf16[1728,1536]{1,0:T(8,128)(2,1)} %bitcast.194, bf16[1728,256]{1,0:T(8,128)(2,1)S(1)} %bitcast.175, bf16[1728,256]{1,0:T(8,128)(2,1)S(1)} %bitcast.171, bf16[1728,256]{1,0:T(8,128)(2,1)S(1)} %bitcast.177), kind=kOutput, calls=%fused_computation.26 | convolution fusion | flops 4084826112 | bytes 12681216 | tf_op jit(solution)/shard_map/dot_general | solution.py:168
  67.7 2.0 %collective-permute-start.7 = (f32[2,2,2,2,48,768]{5,4,3,2,1,0:T(8,128)S(1)}, f32[2,2,2,2,48,768]{5,4,3,2,1,0:T(8,128)S(1)}, u32[]{:S(2)}, u32[]{:S(2)}) collective-permute-start(f32[2,2,2,2,48,768]{5,4,3,2,1,0:T(8,128)S(1)} %dynamic-slice_bitcast_fusion), channel_id=1, source_target_pairs={{0,1},{1,0},{2,3},{3,2},{4,5},{5,4},{6,7},{7,6},{8,9},{9,8},{10,11... | collective-permute-start | bytes 7077896 | tf_op jit(solution)/shard_map/ppermute | solution.py:37
  69.6 6.5 %fusion.8 = f32[1536,768]{1,0:T(8,128)S(1)} fusion(bf16[1728,1536]{1,0:T(8,128)(2,1)} %bitcast.195, bf16[1728,256]{1,0:T(8,128)(2,1)S(1)} %bitcast.179, bf16[1728,256]{1,0:T(8,128)(2,1)S(1)} %bitcast.173, bf16[1728,256]{1,0:T(8,128)(2,1)S(1)} %bitcast.181), kind=kOutput, calls=%fused_computation.14 | convolution fusion | flops 4084826112 | bytes 12681216 | tf_op jit(solution)/shard_map/dot_general | solution.py:168
  87.9 2.8 %collective-permute-start.8 = (f32[2,2,2,48,768]{4,3,2,1,0:T(8,128)S(1)}, f32[2,2,2,48,768]{4,3,2,1,0:T(8,128)S(1)}, u32[]{:S(2)}, u32[]{:S(2)}) collective-permute-start(f32[2,2,2,48,768]{4,3,2,1,0:T(8,128)S(1)} %get-tuple-element.45), channel_id=1, source_target_pairs={{0,2},{1,3},{2,0},{3,1},{4,6},{5,7},{6,4},{7,5},{8,10},{9,11},{10,... | collective-permute-start | bytes 3538952 | tf_op jit(solution)/shard_map/ppermute | solution.py:37
  93.8 6.8 %bitcast_convert_fusion.1 = bf16[1728,768]{1,0:T(8,128)(2,1)S(1)} fusion(bf16[1728,9,256]{2,0,1:T(8,128)(2,1)S(1)} %bitcast.190, bf16[9,1536,256]{2,1,0:T(8,128)(2,1)S(1)} %bitcast.192), kind=kOutput, calls=%fused_computation.5 | convolution fusion | flops 6116622336 | bytes 14155776 | tf_op jit(solution)/shard_map/dot_general | solution.py:176
  100.6 15.9 %collective-permute-done.8 = f32[2,2,2,48,768]{4,3,2,1,0:T(8,128)S(1)} collective-permute-done((f32[2,2,2,48,768]{4,3,2,1,0:T(8,128)S(1)}, f32[2,2,2,48,768]{4,3,2,1,0:T(8,128)S(1)}, u32[]{:S(2)}, u32[]{:S(2)}) %collective-permute-start.8) | collective-permute-done | bytes 1179680 | tf_op jit(solution)/shard_map/ppermute | solution.py:37
  119.7 1.6 collective-permute-start.15
  122.5 6.6 %bitcast_convert_fusion = bf16[1728,768]{1,0:T(8,128)(2,1)S(1)} fusion(bf16[1728,9,256]{2,0,1:T(8,128)(2,1)S(1)} %bitcast.190, bf16[9,1536,256]{2,1,0:T(8,128)(2,1)S(1)} %bitcast.192), kind=kOutput, calls=%fused_computation.4 | convolution fusion | flops 6116622336 | bytes 14155776 | tf_op jit(solution)/shard_map/dot_general | solution.py:176
  129.1 5.4 %collective-permute-done.12 = f32[2,2,48,768]{3,2,1,0:T(8,128)S(1)} collective-permute-done((f32[2,2,48,768]{3,2,1,0:T(8,128)S(1)}, f32[2,2,48,768]{3,2,1,0:T(8,128)S(1)}, u32[]{:S(2)}, u32[]{:S(2)}) %collective-permute-start.12) | collective-permute-done | bytes 589856 | tf_op jit(solution)/shard_map/ppermute | solution.py:37
  135.2 2.8 %collective-permute-start.19 = (f32[1281]{0:T(1024)S(1)}, f32[1281]{0:T(1024)S(1)}, u32[]{:S(2)}, u32[]{:S(2)}) collective-permute-start(f32[1281]{0:T(1024)S(1)} %add.346), channel_id=1, source_target_pairs={{0,16},{4,20},{8,24},{12,28},{16,0},{20,4},{24,8},{28,12},{1,17},{... | collective-permute-start | bytes 15380 | tf_op jit(solution)/shard_map/ppermute | solution.py:37
  141.2 2.8 %pad_maximum_fusion = bf16[1728,1536]{1,0:T(8,128)(2,1)} fusion(bf16[1728,768]{1,0:T(8,128)(2,1)S(1)} %bitcast_convert_fusion, bf16[1728,768]{1,0:T(8,128)(2,1)S(1)} %bitcast_convert_fusion.1), kind=kLoop, calls=%fused_computation.3 | loop fusion | flops 10616832 | bytes 10616832 | tf_op jit(solution)/shard_map/concatenate | solution.py:231
  144.0 3.8 %collective-permute-done.16 = f32[2,48,768]{2,1,0:T(8,128)S(1)} collective-permute-done((f32[2,48,768]{2,1,0:T(8,128)S(1)}, f32[2,48,768]{2,1,0:T(8,128)S(1)}, u32[]{:S(2)}, u32[]{:S(2)}) %collective-permute-start.16) | collective-permute-done | bytes 294944 | tf_op jit(solution)/shard_map/ppermute | solution.py:37
  147.8 7.8 %collective-permute-done.17 = f32[2,48,768]{2,1,0:T(8,128)S(1)} collective-permute-done((f32[2,48,768]{2,1,0:T(8,128)S(1)}, f32[2,48,768]{2,1,0:T(8,128)S(1)}, u32[]{:S(2)}, u32[]{:S(2)}) %collective-permute-start.17) | collective-permute-done | bytes 294944 | tf_op jit(solution)/shard_map/ppermute | solution.py:37
  157.6 3.0 %collective-permute-start.20 = (f32[48,768]{1,0:T(8,128)S(1)}, f32[48,768]{1,0:T(8,128)S(1)}, u32[]{:S(2)}, u32[]{:S(2)}) collective-permute-start(f32[48,768]{1,0:T(8,128)S(1)} %fusion.42), channel_id=1, source_target_pairs={{0,16},{4,20},{8,24},{12,28},{16,0},{20,4},{24,8},{28,12},{1,17},{... | collective-permute-start | bytes 442376 | tf_op jit(solution)/shard_map/ppermute | solution.py:37
  162.0 1.6 collective-permute-done.22
  (118 shorter events, 44.8 us)
Async XLA Ops:
  0.6 21.5 %copy-start = (f32[3,256]{1,0:T(4,128)S(1)}, f32[3,256]{1,0:T(4,128)}, u32[]{:S(2)}) copy-start(f32[3,256]{1,0:T(4,128)} %param.13) | copy-start | bytes 9220
  19.8 15.3 %collective-permute-start = (f32[]{:T(128)}, f32[]{:T(128)}, u32[]{:S(2)}, u32[]{:S(2)}) collective-permute-start(f32[]{:T(128)} %slice_reduce_fusion.1), channel_id=1, source_target_pairs={{0,4},{4,0},{8,12},{12,8},{16,20},{20,16},{24,28},{28,24},{1,5},{5... | collective-permute-start | bytes 20 | tf_op jit(solution)/shard_map/ppermute | solution.py:37
  36.4 3.6 %collective-permute-start.1 = (f32[]{:T(128)}, f32[]{:T(128)}, u32[]{:S(2)}, u32[]{:S(2)}) collective-permute-start(f32[]{:T(128)} %add.319), channel_id=1, source_target_pairs={{0,8},{4,12},{8,0},{12,4},{16,24},{20,28},{24,16},{28,20},{1,9},{5... | collective-permute-start | bytes 20 | tf_op jit(solution)/shard_map/ppermute | solution.py:37
  40.6 4.5 %collective-permute-start.2 = (f32[]{:T(128)}, f32[]{:T(128)}, u32[]{:S(2)}, u32[]{:S(2)}) collective-permute-start(f32[]{:T(128)} %add.320), channel_id=1, source_target_pairs={{0,16},{4,20},{8,24},{12,28},{16,0},{20,4},{24,8},{28,12},{1,17},{... | collective-permute-start | bytes 20 | tf_op jit(solution)/shard_map/ppermute | solution.py:37
  46.3 12.5 %collective-permute-start.4 = (bf16[2,12,72,256]{3,2,1,0:T(8,128)(2,1)S(1)}, bf16[2,12,72,256]{3,2,1,0:T(8,128)(2,1)S(1)}, u32[]{:S(2)}, u32[]{:S(2)}) collective-permute-start(bf16[2,12,72,256]{3,2,1,0:T(8,128)(2,1)S(1)} %bitcast.160), channel_id=1, source_target_pairs={{1,0},{2,1},{3,2},{5,4},{6,5},{7,6},{9,8},{10,9},{11,10},{13,12},{... | collective-permute-start | bytes 2654216 | tf_op jit(solution)/shard_map/ppermute | solution.py:20
  47.6 11.2 %collective-permute-start.3 = (bf16[2,12,72,256]{3,2,1,0:T(8,128)(2,1)S(1)}, bf16[2,12,72,256]{3,2,1,0:T(8,128)(2,1)S(1)}, u32[]{:S(2)}, u32[]{:S(2)}) collective-permute-start(bf16[2,12,72,256]{3,2,1,0:T(8,128)(2,1)S(1)} %bitcast.161), channel_id=1, source_target_pairs={{0,1},{1,2},{2,3},{4,5},{5,6},{6,7},{8,9},{9,10},{10,11},{12,13},{... | collective-permute-start | bytes 2654216 | tf_op jit(solution)/shard_map/ppermute | solution.py:19
  58.4 27.3 %collective-permute-start.6 = (f32[2,2,2,2,48,768]{5,4,3,2,1,0:T(8,128)S(1)}, f32[2,2,2,2,48,768]{5,4,3,2,1,0:T(8,128)S(1)}, u32[]{:S(2)}, u32[]{:S(2)}) collective-permute-start(f32[2,2,2,2,48,768]{5,4,3,2,1,0:T(8,128)S(1)} %dynamic-slice_bitcast_fusion.1), channel_id=1, source_target_pairs={{0,1},{1,0},{2,3},{3,2},{4,5},{5,4},{6,7},{7,6},{8,9},{9,8},{10,11... | collective-permute-start | bytes 7077896 | tf_op jit(solution)/shard_map/ppermute | solution.py:37
  67.7 18.0 %collective-permute-start.7 = (f32[2,2,2,2,48,768]{5,4,3,2,1,0:T(8,128)S(1)}, f32[2,2,2,2,48,768]{5,4,3,2,1,0:T(8,128)S(1)}, u32[]{:S(2)}, u32[]{:S(2)}) collective-permute-start(f32[2,2,2,2,48,768]{5,4,3,2,1,0:T(8,128)S(1)} %dynamic-slice_bitcast_fusion), channel_id=1, source_target_pairs={{0,1},{1,0},{2,3},{3,2},{4,5},{5,4},{6,7},{7,6},{8,9},{9,8},{10,11... | collective-permute-start | bytes 7077896 | tf_op jit(solution)/shard_map/ppermute | solution.py:37
  76.3 9.3 %collective-permute-start.5 = (f32[2,2,2,2,48,768]{5,4,3,2,1,0:T(8,128)S(1)}, f32[2,2,2,2,48,768]{5,4,3,2,1,0:T(8,128)S(1)}, u32[]{:S(2)}, u32[]{:S(2)}) collective-permute-start(f32[2,2,2,2,48,768]{5,4,3,2,1,0:T(8,128)S(1)} %dynamic-slice_bitcast_fusion.2), channel_id=1, source_target_pairs={{0,1},{1,0},{2,3},{3,2},{4,5},{5,4},{6,7},{7,6},{8,9},{9,8},{10,11... | collective-permute-start | bytes 7077896 | tf_op jit(solution)/shard_map/ppermute | solution.py:37
  87.3 13.3 %collective-permute-start.11 = (f32[1281]{0:T(1024)S(1)}, f32[1281]{0:T(1024)S(1)}, u32[]{:S(2)}, u32[]{:S(2)}) collective-permute-start(f32[1281]{0:T(1024)S(1)} %pad_maximum_fusion.2), channel_id=1, source_target_pairs={{0,4},{4,0},{8,12},{12,8},{16,20},{20,16},{24,28},{28,24},{1,5},{5... | collective-permute-start | bytes 15380 | tf_op jit(solution)/shard_map/ppermute | solution.py:37
  87.9 28.6 %collective-permute-start.8 = (f32[2,2,2,48,768]{4,3,2,1,0:T(8,128)S(1)}, f32[2,2,2,48,768]{4,3,2,1,0:T(8,128)S(1)}, u32[]{:S(2)}, u32[]{:S(2)}) collective-permute-start(f32[2,2,2,48,768]{4,3,2,1,0:T(8,128)S(1)} %get-tuple-element.45), channel_id=1, source_target_pairs={{0,2},{1,3},{2,0},{3,1},{4,6},{5,7},{6,4},{7,5},{8,10},{9,11},{10,... | collective-permute-start | bytes 3538952 | tf_op jit(solution)/shard_map/ppermute | solution.py:37
  90.6 27.3 %collective-permute-start.9 = (f32[2,2,2,48,768]{4,3,2,0,1:T(8,128)S(1)}, f32[2,2,2,48,768]{4,3,2,0,1:T(8,128)S(1)}, u32[]{:S(2)}, u32[]{:S(2)}) collective-permute-start(f32[2,2,2,48,768]{4,3,2,0,1:T(8,128)S(1)} %get-tuple-element.46), channel_id=1, source_target_pairs={{0,4},{4,0},{8,12},{12,8},{16,20},{20,16},{24,28},{28,24},{1,5},{5... | collective-permute-start | bytes 3538952 | tf_op jit(solution)/shard_map/ppermute | solution.py:37
  92.2 27.0 %collective-permute-start.10 = (f32[2,2,2,48,768]{4,3,0,1,2:T(8,128)S(1)}, f32[2,2,2,48,768]{4,3,0,1,2:T(8,128)S(1)}, u32[]{:S(2)}, u32[]{:S(2)}) collective-permute-start(f32[2,2,2,48,768]{4,3,0,1,2:T(8,128)S(1)} %get-tuple-element.47), channel_id=1, source_target_pairs={{0,8},{4,12},{8,0},{12,4},{16,24},{20,28},{24,16},{28,20},{1,9},{5... | collective-permute-start | bytes 3538952 | tf_op jit(solution)/shard_map/ppermute | solution.py:37
  119.7 9.5 %collective-permute-start.15 = (f32[1281]{0:T(1024)S(1)}, f32[1281]{0:T(1024)S(1)}, u32[]{:S(2)}, u32[]{:S(2)}) collective-permute-start(f32[1281]{0:T(1024)S(1)} %add.330), channel_id=1, source_target_pairs={{0,8},{4,12},{8,0},{12,4},{16,24},{20,28},{24,16},{28,20},{1,9},{5... | collective-permute-start | bytes 15380 | tf_op jit(solution)/shard_map/ppermute | solution.py:37
  121.3 13.2 %collective-permute-start.12 = (f32[2,2,48,768]{3,2,1,0:T(8,128)S(1)}, f32[2,2,48,768]{3,2,1,0:T(8,128)S(1)}, u32[]{:S(2)}, u32[]{:S(2)}) collective-permute-start(f32[2,2,48,768]{3,2,1,0:T(8,128)S(1)} %get-tuple-element.54), channel_id=1, source_target_pairs={{0,4},{4,0},{8,12},{12,8},{16,20},{20,16},{24,28},{28,24},{1,5},{5... | collective-permute-start | bytes 1769480 | tf_op jit(solution)/shard_map/ppermute | solution.py:37
  121.8 13.0 %collective-permute-start.13 = (f32[2,2,48,768]{3,2,1,0:T(8,128)S(1)}, f32[2,2,48,768]{3,2,1,0:T(8,128)S(1)}, u32[]{:S(2)}, u32[]{:S(2)}) collective-permute-start(f32[2,2,48,768]{3,2,1,0:T(8,128)S(1)} %get-tuple-element.55), channel_id=1, source_target_pairs={{0,8},{4,12},{8,0},{12,4},{16,24},{20,28},{24,16},{28,20},{1,9},{5... | collective-permute-start | bytes 1769480 | tf_op jit(solution)/shard_map/ppermute | solution.py:37
  122.3 12.7 %collective-permute-start.14 = (f32[2,2,48,768]{3,2,0,1:T(8,128)S(1)}, f32[2,2,48,768]{3,2,0,1:T(8,128)S(1)}, u32[]{:S(2)}, u32[]{:S(2)}) collective-permute-start(f32[2,2,48,768]{3,2,0,1:T(8,128)S(1)} %get-tuple-element.56), channel_id=1, source_target_pairs={{0,2},{1,3},{2,0},{3,1},{4,6},{5,7},{6,4},{7,5},{8,10},{9,11},{10,... | collective-permute-start | bytes 1769480 | tf_op jit(solution)/shard_map/ppermute | solution.py:37
  135.2 8.8 %collective-permute-start.19 = (f32[1281]{0:T(1024)S(1)}, f32[1281]{0:T(1024)S(1)}, u32[]{:S(2)}, u32[]{:S(2)}) collective-permute-start(f32[1281]{0:T(1024)S(1)} %add.346), channel_id=1, source_target_pairs={{0,16},{4,20},{8,24},{12,28},{16,0},{20,4},{24,8},{28,12},{1,17},{... | collective-permute-start | bytes 15380 | tf_op jit(solution)/shard_map/ppermute | solution.py:37
  138.0 9.8 %collective-permute-start.16 = (f32[2,48,768]{2,1,0:T(8,128)S(1)}, f32[2,48,768]{2,1,0:T(8,128)S(1)}, u32[]{:S(2)}, u32[]{:S(2)}) collective-permute-start(f32[2,48,768]{2,1,0:T(8,128)S(1)} %get-tuple-element.63), channel_id=1, source_target_pairs={{0,8},{4,12},{8,0},{12,4},{16,24},{20,28},{24,16},{28,20},{1,9},{5... | collective-permute-start | bytes 884744 | tf_op jit(solution)/shard_map/ppermute | solution.py:37
  139.4 16.2 %collective-permute-start.17 = (f32[2,48,768]{2,1,0:T(8,128)S(1)}, f32[2,48,768]{2,1,0:T(8,128)S(1)}, u32[]{:S(2)}, u32[]{:S(2)}) collective-permute-start(f32[2,48,768]{2,1,0:T(8,128)S(1)} %get-tuple-element.64), channel_id=1, source_target_pairs={{0,16},{4,20},{8,24},{12,28},{16,0},{20,4},{24,8},{28,12},{1,17},{... | collective-permute-start | bytes 884744 | tf_op jit(solution)/shard_map/ppermute | solution.py:37
  139.8 15.9 %collective-permute-start.18 = (f32[2,48,768]{2,1,0:T(8,128)S(1)}, f32[2,48,768]{2,1,0:T(8,128)S(1)}, u32[]{:S(2)}, u32[]{:S(2)}) collective-permute-start(f32[2,48,768]{2,1,0:T(8,128)S(1)} %get-tuple-element.65), channel_id=1, source_target_pairs={{0,4},{4,0},{8,12},{12,8},{16,20},{20,16},{24,28},{28,24},{1,5},{5... | collective-permute-start | bytes 884744 | tf_op jit(solution)/shard_map/ppermute | solution.py:37
  157.5 6.1 %collective-permute-start.22 = (f32[48,768]{1,0:T(8,128)S(1)}, f32[48,768]{1,0:T(8,128)S(1)}, u32[]{:S(2)}, u32[]{:S(2)}) collective-permute-start(f32[48,768]{1,0:T(8,128)S(1)} %fusion.40), channel_id=1, source_target_pairs={{0,16},{4,20},{8,24},{12,28},{16,0},{20,4},{24,8},{28,12},{1,17},{... | collective-permute-start | bytes 442376 | tf_op jit(solution)/shard_map/ppermute | solution.py:37
  157.6 7.6 %collective-permute-start.20 = (f32[48,768]{1,0:T(8,128)S(1)}, f32[48,768]{1,0:T(8,128)S(1)}, u32[]{:S(2)}, u32[]{:S(2)}) collective-permute-start(f32[48,768]{1,0:T(8,128)S(1)} %fusion.42), channel_id=1, source_target_pairs={{0,16},{4,20},{8,24},{12,28},{16,0},{20,4},{24,8},{28,12},{1,17},{... | collective-permute-start | bytes 442376 | tf_op jit(solution)/shard_map/ppermute | solution.py:37
  160.6 5.2 %collective-permute-start.21 = (f32[48,768]{1,0:T(8,128)S(1)}, f32[48,768]{1,0:T(8,128)S(1)}, u32[]{:S(2)}, u32[]{:S(2)}) collective-permute-start(f32[48,768]{1,0:T(8,128)S(1)} %fusion.41), channel_id=1, source_target_pairs={{0,2},{1,3},{2,0},{3,1},{4,6},{5,7},{6,4},{7,5},{8,10},{9,11},{10,... | collective-permute-start | bytes 442376 | tf_op jit(solution)/shard_map/ppermute | solution.py:37
  (8 other events, 103.4 us)

commit v7 on v4

--- a/solution.py
+++ b/solution.py
@@ -187,7 +187,7 @@
     mine = (lax.axis_index(axis) >> bit) & 1
     keeps = [lax.dynamic_index_in_dim(p, mine, ax, keepdims=False) for p in parts]
     sends = [lax.dynamic_index_in_dim(p, 1 - mine, ax, keepdims=False) for p in parts]
-    received = lax.optimization_barrier([exchange(v, axis, bit) for v in sends])
+    received = [exchange(v, axis, bit) for v in sends]
     bit_axes.pop(ax)
     pieces = [keeps[s] + received[s] for s in range(3)]
     small_bits = index_bits(("rep",))
@@ -203,7 +203,7 @@
             axes_of[s].pop(ax)
         received = []
         if step < len(small_bits):
-            packed, sends = lax.optimization_barrier((packed, sends))
+            packed, sends[0] = lax.optimization_barrier((packed, sends[0]))
             received.append(exchange(packed, *small_bits[step]))
         received = [exchange(sends[s], orders[s][step][0], orders[s][step][1]) for s in range(3)] + received
         if step < halves:

time: 160 us -> 176 us (1.10)
  local copies, waits for them, and re-layouts: 6.95 us -> 20.2 us
  matrix products: 40 us -> 44.5 us
    unnamed x23 -> x37, local copies, waits for them, and re-layouts: 1.31 us -> 9.99 us
    dynamic_slice x3 -> x2, local copies, waits for them, and re-layouts: 1.29 us -> 4.1 us  [body(): lax.dynamic_index_in_dim(p, mine, ax, keepdims=False)]
    dot_general x2, matrix products: 17.2 us -> 19.6 us  [body(): lax.dot_general(shifted.reshape(local_pix, taps, out_chans), conv_weight[...]
    dot_general x3, matrix products: 18 us -> 20 us  [body(): lax.dot_general(flat_x, cols, (((0,), (0,)), ((), ())), preferred_element...]
  transfers between devices with their start and end apart: 23 -> 23, of which waited for: 8 -> 10; matrix products, arithmetic and copies ran while one was open for 32% -> 31% of each run, Pallas kernels for 0% -> 0%
where the time goes in v7:
time: 176 us; the launch traced here: 175 us
  matrix products  44.5 us (25%)
  starting transfers between devices  35.9 us (20%)
  waiting for transfers between devices  34.6 us (20%)
  local copies, waits for them, and re-layouts  20.2 us (11%)
  blocking collectives  19.2 us (11%)
  other arithmetic  15.3 us (9%)
  between operations  5.65 us (3%)
    ppermute x21, waiting for transfers between devices, exchange(): return lax.ppermute(x, axis, pairs)  34.6 us
    ppermute x21, starting transfers between devices, exchange(): return lax.ppermute(x, axis, pairs)  33.3 us
    dot_general x3, matrix products, body(): lax.dot_general(flat_x, cols, (((0,), (0,)), ((), ())), preferred_element...  20 us
    dot_general x2, matrix products, body(): lax.dot_general(shifted.reshape(local_pix, taps, out_chans), conv_weight[...  19.6 us
    psum x1, blocking collectives, body(): tile_stats = lax.psum(slot[:, None] * local_stats[None, :], 'tile')  12.6 us
    unnamed x37, local copies, waits for them, and re-layouts  9.99 us
    psum x1, blocking collectives, body(): lax.psum((jnp.sum(preactivation_gradient, 0), jnp.sum(preactivation_gradi...  6.56 us
    dynamic_slice x2, local copies, waits for them, and re-layouts, body(): lax.dynamic_index_in_dim(p, mine, ax, keepdims=False)  4.1 us
  transfers between devices with their start and end apart: 23, of which 10 were waited for; matrix products, arithmetic and copies ran while one was open for 31% of the time, Pallas kernels for 0%

profile of v7, /device:TPU:0, one launch (start us, length us, event | category | flops | bytes accessed | tf_op | source)
XLA Modules:
  0.0 175.5 jit_solution(12458693270944836269)
XLA Ops:
  6.5 12.6 %psum.35 = f32[4,513]{1,0:T(4,128)S(1)} all-reduce(f32[4,513]{1,0:T(4,128)S(1)} %broadcast_multiply_fusion), channel_id=1, replica_groups=mesh['rep'=8,'tile'=4] {'tile'}, use_global_device_ids=true, to_apply=%region_3.0 | all-reduce | flops 2052 | bytes 16416 | tf_op jit(solution)/shard_map/psum | solution.py:90
  22.2 1.8 %fusion.47 = (f32[1728]{0:T(1024)S(1)}, f32[1728,3]{0,1:T(4,128)S(1)}) fusion(f32[3,256]{1,0:T(4,128)S(1)} %copy-done, f32[1728,256]{1,0:T(8,128)S(1)} %fusion.26, f32[256]{0:T(256)S(1)} %copy-done.11, f32[256]{0:T(256)S(1)} %copy-done.10), kind=kOutput, calls=%fused_computation.130 | convolution fusion | flops 17255808 | bytes 1802240 | tf_op jit(solution)/shard_map/dot_general | solution.py:104
  24.6 2.1 %fusion.45 = (f32[256]{0:T(256)S(1)}, f32[256]{0:T(256)S(1)}, f32[1728,256]{1,0:T(8,128)S(1)}) fusion(f32[256]{0:T(256)S(1)} %get-tuple-element.107, f32[256]{0:T(256)S(1)} %broadcast_multiply_fusion.2, bf16[2,12,72,256]{3,2,1,0:T(8,128)(2,1)S(1)} %copy-done.2, f32[3,256]{1,0:T(4,128)S(1)} %copy-done, f32[1728,3]{0,1:T(4,128)S(1)} %get-tuple-element.109, ...), kind=kOutput, calls=%fused_computation.128 | convolution fusion | flops 20374336 | bytes 4474368 | tf_op jit(solution)/shard_map/dot_general | solution.py:112
  27.8 6.6 %all-reduce.2 = (f32[1]{0:T(128)}, f32[768]{0:T(1024)S(1)}, f32[256]{0:T(256)S(1)}, f32[256]{0:T(256)S(1)}) all-reduce(f32[1]{0:T(128)} %bitcast.2, f32[768]{0:T(1024)S(1)} %reshape.126, f32[256]{0:T(256)S(1)} %get-tuple-element.81, f32[256]{0:T(256)S(1)} %get-tuple-element.80), channel_id=1, replica_groups=mesh['rep'=8,'tile'=4] {'tile'}, use_global_device_ids=true, to_apply=%region_16.17 | all-reduce | flops 1281 | bytes 10248 | tf_op jit(solution)/shard_map/psum | solution.py:114
  36.3 2.9 %collective-permute-start.1 = (f32[]{:T(128)}, f32[]{:T(128)}, u32[]{:S(2)}, u32[]{:S(2)}) collective-permute-start(f32[]{:T(128)} %add.175), channel_id=1, source_target_pairs={{0,8},{4,12},{8,0},{12,4},{16,24},{20,28},{24,16},{28,20},{1,9},{5... | collective-permute-start | bytes 20 | tf_op jit(solution)/shard_map/ppermute | solution.py:37
  40.6 4.0 %collective-permute-start.2 = (f32[]{:T(128)}, f32[]{:T(128)}, u32[]{:S(2)}, u32[]{:S(2)}) collective-permute-start(f32[]{:T(128)} %add.176), channel_id=1, source_target_pairs={{0,16},{4,20},{8,24},{12,28},{16,0},{20,4},{24,8},{28,12},{1,17},{... | collective-permute-start | bytes 20 | tf_op jit(solution)/shard_map/ppermute | solution.py:37
  49.8 7.3 %fusion.14 = f32[1536,768]{1,0:T(8,128)S(1)} fusion(bf16[1728,1536]{1,0:T(8,128)(2,1)} %bitcast.142, bf16[1728,256]{1,0:T(8,128)(2,1)S(1)} %bitcast.133, bf16[1728,256]{1,0:T(8,128)(2,1)S(1)} %multiply_convert_fusion, bf16[1728,256]{1,0:T(8,128)(2,1)S(1)} %bitcast.135), kind=kOutput, calls=%fused_computation.20 | convolution fusion | flops 4084826112 | bytes 12681216 | tf_op jit(solution)/shard_map/dot_general | solution.py:168
  57.2 1.9 %fusion.5 = bf16[2,36,96,256]{3,2,1,0:T(8,128)(2,1)S(1)} fusion(bf16[2,12,72,256]{3,2,1,0:T(8,128)(2,1)S(1)} %collective-permute-done.4, bf16[2,12,72,256]{3,2,1,0:T(8,128)(2,1)S(1)} %bitcast.116, bf16[2,12,72,256]{3,2,1,0:T(8,128)(2,1)S(1)} %collective-permute-done.3), kind=kLoop, calls=%fused_computation.10 | loop fusion | flops 21233664 | bytes 6193152 | tf_op jit(solution)/shard_map/concatenate | solution.py:21
  61.3 6.2 %fusion.20 = f32[1536,768]{1,0:T(8,128)} fusion(bf16[1728,1536]{1,0:T(8,128)(2,1)S(1)} %bitcast.146, bf16[1728,256]{1,0:T(8,128)(2,1)S(1)} %bitcast.123, bf16[1728,256]{1,0:T(8,128)(2,1)S(1)} %bitcast.121, bf16[1728,256]{1,0:T(8,128)(2,1)S(1)} %bitcast.127), kind=kOutput, calls=%fused_computation.26 | convolution fusion | flops 4084826112 | bytes 12681216 | tf_op jit(solution)/shard_map/dot_general | solution.py:168
  67.6 3.8 %constant_dynamic-slice_fusion.1 = (f32[2,2,2,2,1,48,768]{6,5,4,3,2,1,0:T(8,128)S(1)}, f32[2,2,2,2,1,48,768]{6,5,4,3,2,1,0:T(8,128)S(1)}, f32[2,2,2,2,1,48,768]{...) fusion(f32[2,2,2,2,2,48,768]{6,5,4,3,2,1,0:T(8,128)} %bitcast.120, s32[]{:T(128)S(6)} %select_n.64, s32[]{:T(128)S(6)} %select_n.65, ...), kind=kLoop, calls=%fused_computation.102 | loop fusion | bytes 18874376 | tf_op jit(solution)/shard_map/jit(dynamic_index_in_dim)/dynamic_slice | solution.py:188
  71.5 5.9 %collective-permute-start.9 = (f32[2,2,2,2,48,768]{5,4,3,2,0,1:T(8,128)S(1)}, f32[2,2,2,2,48,768]{5,4,3,2,0,1:T(8,128)S(1)}, u32[]{:S(2)}, u32[]{:S(2)}) collective-permute-start(f32[2,2,2,2,48,768]{5,4,3,2,0,1:T(8,128)S(1)} %bitcast.139), channel_id=1, source_target_pairs={{0,1},{1,0},{2,3},{3,2},{4,5},{5,4},{6,7},{7,6},{8,9},{9,8},{10,11... | collective-permute-start | bytes 7077896 | tf_op jit(solution)/shard_map/ppermute | solution.py:37
  78.9 6.5 %fusion.8 = f32[1536,768]{1,0:T(8,128)S(1)} fusion(bf16[1728,1536]{1,0:T(8,128)(2,1)} %bitcast.143, bf16[1728,256]{1,0:T(8,128)(2,1)S(1)} %bitcast.129, bf16[1728,256]{1,0:T(8,128)(2,1)S(1)} %bitcast.125, bf16[1728,256]{1,0:T(8,128)(2,1)S(1)} %bitcast.132), kind=kOutput, calls=%fused_computation.14 | convolution fusion | flops 4084826112 | bytes 12681216 | tf_op jit(solution)/shard_map/dot_general | solution.py:168
  94.3 1.6 collective-permute-start.10
  99.1 9.8 %bitcast_convert_fusion.1 = bf16[1728,768]{1,0:T(8,128)(2,1)S(1)} fusion(bf16[1728,9,256]{2,0,1:T(8,128)(2,1)} %constant_dynamic-update-slice_fusion, bf16[9,1536,256]{2,1,0:T(8,128)(2,1)} %param.10), kind=kOutput, calls=%fused_computation.5 | convolution fusion | flops 6116622336 | bytes 14155776 | tf_op jit(solution)/shard_map/dot_general | solution.py:176
  108.9 15.8 %collective-permute-done.11 = f32[1281]{0:T(1024)S(1)} collective-permute-done((f32[1281]{0:T(1024)S(1)}, f32[1281]{0:T(1024)S(1)}, u32[]{:S(2)}, u32[]{:S(2)}) %collective-permute-start.11) | collective-permute-done | bytes 5156 | tf_op jit(solution)/shard_map/ppermute | solution.py:37
  126.7 1.6 collective-permute-start.12
  129.9 9.8 %bitcast_convert_fusion = bf16[1728,768]{1,0:T(8,128)(2,1)S(1)} fusion(bf16[1728,9,256]{2,0,1:T(8,128)(2,1)} %constant_dynamic-update-slice_fusion, bf16[9,1536,256]{2,1,0:T(8,128)(2,1)} %param.10), kind=kOutput, calls=%fused_computation.4 | convolution fusion | flops 6116622336 | bytes 14155776 | tf_op jit(solution)/shard_map/dot_general | solution.py:176
  140.8 1.6 collective-permute-start.18
  142.5 2.7 %collective-permute-start.17 = (f32[2,48,768]{2,1,0:T(8,128)S(1)}, f32[2,48,768]{2,1,0:T(8,128)S(1)}, u32[]{:S(2)}, u32[]{:S(2)}) collective-permute-start(f32[2,48,768]{2,1,0:T(8,128)S(1)} %dynamic-slice_bitcast_fusion.7), channel_id=1, source_target_pairs={{0,16},{4,20},{8,24},{12,28},{16,0},{20,4},{24,8},{28,12},{1,17},{... | collective-permute-start | bytes 884744 | tf_op jit(solution)/shard_map/ppermute | solution.py:37
  145.2 1.6 collective-permute-start.16
  147.2 2.8 %pad_maximum_fusion = bf16[1728,1536]{1,0:T(8,128)(2,1)} fusion(bf16[1728,768]{1,0:T(8,128)(2,1)S(1)} %bitcast_convert_fusion, bf16[1728,768]{1,0:T(8,128)(2,1)S(1)} %bitcast_convert_fusion.1), kind=kLoop, calls=%fused_computation.3 | loop fusion | flops 10616832 | bytes 10616832 | tf_op jit(solution)/shard_map/concatenate | solution.py:224
  150.0 6.5 %collective-permute-done.19 = f32[1281]{0:T(1024)S(1)} collective-permute-done((f32[1281]{0:T(1024)S(1)}, f32[1281]{0:T(1024)S(1)}, u32[]{:S(2)}, u32[]{:S(2)}) %collective-permute-start.19) | collective-permute-done | bytes 5156 | tf_op jit(solution)/shard_map/ppermute | solution.py:37
  158.6 2.3 %collective-permute-start.22 = (f32[48,768]{1,0:T(8,128)S(1)}, f32[48,768]{1,0:T(8,128)S(1)}, u32[]{:S(2)}, u32[]{:S(2)}) collective-permute-start(f32[48,768]{1,0:T(8,128)S(1)} %dynamic-slice_bitcast_fusion.9), channel_id=1, source_target_pairs={{0,16},{4,20},{8,24},{12,28},{16,0},{20,4},{24,8},{28,12},{1,17},{... | collective-permute-start | bytes 442376 | tf_op jit(solution)/shard_map/ppermute | solution.py:37
  163.9 7.9 %collective-permute-done.22 = f32[48,768]{1,0:T(8,128)S(1)} collective-permute-done((f32[48,768]{1,0:T(8,128)S(1)}, f32[48,768]{1,0:T(8,128)S(1)}, u32[]{:S(2)}, u32[]{:S(2)}) %collective-permute-start.22) | collective-permute-done | bytes 147488 | tf_op jit(solution)/shard_map/ppermute | solution.py:37
  (137 shorter events, 44.2 us)
Async XLA Ops:
  0.6 21.5 %copy-start = (f32[3,256]{1,0:T(4,128)S(1)}, f32[3,256]{1,0:T(4,128)}, u32[]{:S(2)}) copy-start(f32[3,256]{1,0:T(4,128)} %param.13) | copy-start | bytes 9220
  19.8 15.2 %collective-permute-start = (f32[]{:T(128)}, f32[]{:T(128)}, u32[]{:S(2)}, u32[]{:S(2)}) collective-permute-start(f32[]{:T(128)} %slice_reduce_fusion.1), channel_id=1, source_target_pairs={{0,4},{4,0},{8,12},{12,8},{16,20},{20,16},{24,28},{28,24},{1,5},{5... | collective-permute-start | bytes 20 | tf_op jit(solution)/shard_map/ppermute | solution.py:37
  36.3 3.6 %collective-permute-start.1 = (f32[]{:T(128)}, f32[]{:T(128)}, u32[]{:S(2)}, u32[]{:S(2)}) collective-permute-start(f32[]{:T(128)} %add.175), channel_id=1, source_target_pairs={{0,8},{4,12},{8,0},{12,4},{16,24},{20,28},{24,16},{28,20},{1,9},{5... | collective-permute-start | bytes 20 | tf_op jit(solution)/shard_map/ppermute | solution.py:37
  40.6 4.5 %collective-permute-start.2 = (f32[]{:T(128)}, f32[]{:T(128)}, u32[]{:S(2)}, u32[]{:S(2)}) collective-permute-start(f32[]{:T(128)} %add.176), channel_id=1, source_target_pairs={{0,16},{4,20},{8,24},{12,28},{16,0},{20,4},{24,8},{28,12},{1,17},{... | collective-permute-start | bytes 20 | tf_op jit(solution)/shard_map/ppermute | solution.py:37
  46.3 10.8 %collective-permute-start.3 = (bf16[2,12,72,256]{3,2,1,0:T(8,128)(2,1)S(1)}, bf16[2,12,72,256]{3,2,1,0:T(8,128)(2,1)S(1)}, u32[]{:S(2)}, u32[]{:S(2)}) collective-permute-start(bf16[2,12,72,256]{3,2,1,0:T(8,128)(2,1)S(1)} %bitcast.113), channel_id=1, source_target_pairs={{0,1},{1,2},{2,3},{4,5},{5,6},{6,7},{8,9},{9,10},{10,11},{12,13},{... | collective-permute-start | bytes 2654216 | tf_op jit(solution)/shard_map/ppermute | solution.py:19
  47.7 9.5 %collective-permute-start.4 = (bf16[2,12,72,256]{3,2,1,0:T(8,128)(2,1)S(1)}, bf16[2,12,72,256]{3,2,1,0:T(8,128)(2,1)S(1)}, u32[]{:S(2)}, u32[]{:S(2)}) collective-permute-start(bf16[2,12,72,256]{3,2,1,0:T(8,128)(2,1)S(1)} %bitcast.114), channel_id=1, source_target_pairs={{1,0},{2,1},{3,2},{5,4},{6,5},{7,6},{9,8},{10,9},{11,10},{13,12},{... | collective-permute-start | bytes 2654216 | tf_op jit(solution)/shard_map/ppermute | solution.py:20
  71.5 22.4 %collective-permute-start.9 = (f32[2,2,2,2,48,768]{5,4,3,2,0,1:T(8,128)S(1)}, f32[2,2,2,2,48,768]{5,4,3,2,0,1:T(8,128)S(1)}, u32[]{:S(2)}, u32[]{:S(2)}) collective-permute-start(f32[2,2,2,2,48,768]{5,4,3,2,0,1:T(8,128)S(1)} %bitcast.139), channel_id=1, source_target_pairs={{0,1},{1,0},{2,3},{3,2},{4,5},{5,4},{6,7},{7,6},{8,9},{9,8},{10,11... | collective-permute-start | bytes 7077896 | tf_op jit(solution)/shard_map/ppermute | solution.py:37
  77.6 18.3 %collective-permute-start.7 = (f32[2,2,2,2,48,768]{5,4,3,1,0,2:T(8,128)S(1)}, f32[2,2,2,2,48,768]{5,4,3,1,0,2:T(8,128)S(1)}, u32[]{:S(2)}, u32[]{:S(2)}) collective-permute-start(f32[2,2,2,2,48,768]{5,4,3,1,0,2:T(8,128)S(1)} %bitcast.137), channel_id=1, source_target_pairs={{0,1},{1,0},{2,3},{3,2},{4,5},{5,4},{6,7},{7,6},{8,9},{9,8},{10,11... | collective-permute-start | bytes 7077896 | tf_op jit(solution)/shard_map/ppermute | solution.py:37
  85.9 11.1 %collective-permute-start.5 = (f32[2,2,2,2,48,768]{5,4,2,1,0,3:T(8,128)S(1)}, f32[2,2,2,2,48,768]{5,4,2,1,0,3:T(8,128)S(1)}, u32[]{:S(2)}, u32[]{:S(2)}) collective-permute-start(f32[2,2,2,2,48,768]{5,4,2,1,0,3:T(8,128)S(1)} %bitcast.138), channel_id=1, source_target_pairs={{0,1},{1,0},{2,3},{3,2},{4,5},{5,4},{6,7},{7,6},{8,9},{9,8},{10,11... | collective-permute-start | bytes 7077896 | tf_op jit(solution)/shard_map/ppermute | solution.py:37
  94.3 30.4 %collective-permute-start.10 = (f32[2,2,2,48,768]{4,3,2,1,0:T(8,128)S(1)}, f32[2,2,2,48,768]{4,3,2,1,0:T(8,128)S(1)}, u32[]{:S(2)}, u32[]{:S(2)}) collective-permute-start(f32[2,2,2,48,768]{4,3,2,1,0:T(8,128)S(1)} %dynamic-slice_bitcast_fusion), channel_id=1, source_target_pairs={{0,8},{4,12},{8,0},{12,4},{16,24},{20,28},{24,16},{28,20},{1,9},{5... | collective-permute-start | bytes 3538952 | tf_op jit(solution)/shard_map/ppermute | solution.py:37
  96.4 28.3 %collective-permute-start.8 = (f32[2,2,2,48,768]{4,3,2,1,0:T(8,128)S(1)}, f32[2,2,2,48,768]{4,3,2,1,0:T(8,128)S(1)}, u32[]{:S(2)}, u32[]{:S(2)}) collective-permute-start(f32[2,2,2,48,768]{4,3,2,1,0:T(8,128)S(1)} %dynamic-slice_bitcast_fusion.1), channel_id=1, source_target_pairs={{0,4},{4,0},{8,12},{12,8},{16,20},{20,16},{24,28},{28,24},{1,5},{5... | collective-permute-start | bytes 3538952 | tf_op jit(solution)/shard_map/ppermute | solution.py:37
  97.4 27.9 %collective-permute-start.6 = (f32[2,2,2,48,768]{4,3,2,1,0:T(8,128)S(1)}, f32[2,2,2,48,768]{4,3,2,1,0:T(8,128)S(1)}, u32[]{:S(2)}, u32[]{:S(2)}) collective-permute-start(f32[2,2,2,48,768]{4,3,2,1,0:T(8,128)S(1)} %dynamic-slice_bitcast_fusion.2), channel_id=1, source_target_pairs={{0,2},{1,3},{2,0},{3,1},{4,6},{5,7},{6,4},{7,5},{8,10},{9,11},{10,... | collective-permute-start | bytes 3538952 | tf_op jit(solution)/shard_map/ppermute | solution.py:37
  97.6 27.1 %collective-permute-start.11 = (f32[1281]{0:T(1024)S(1)}, f32[1281]{0:T(1024)S(1)}, u32[]{:S(2)}, u32[]{:S(2)}) collective-permute-start(f32[1281]{0:T(1024)S(1)} %pad_maximum_fusion.2), channel_id=1, source_target_pairs={{0,4},{4,0},{8,12},{12,8},{16,20},{20,16},{24,28},{28,24},{1,5},{5... | collective-permute-start | bytes 15380 | tf_op jit(solution)/shard_map/ppermute | solution.py:37
  125.5 14.9 %collective-permute-start.14 = (f32[2,2,48,768]{3,2,1,0:T(8,128)S(1)}, f32[2,2,48,768]{3,2,1,0:T(8,128)S(1)}, u32[]{:S(2)}, u32[]{:S(2)}) collective-permute-start(f32[2,2,48,768]{3,2,1,0:T(8,128)S(1)} %dynamic-slice_bitcast_fusion.3), channel_id=1, source_target_pairs={{0,2},{1,3},{2,0},{3,1},{4,6},{5,7},{6,4},{7,5},{8,10},{9,11},{10,... | collective-permute-start | bytes 1769480 | tf_op jit(solution)/shard_map/ppermute | solution.py:37
  126.0 14.4 %collective-permute-start.13 = (f32[2,2,48,768]{3,2,1,0:T(8,128)S(1)}, f32[2,2,48,768]{3,2,1,0:T(8,128)S(1)}, u32[]{:S(2)}, u32[]{:S(2)}) collective-permute-start(f32[2,2,48,768]{3,2,1,0:T(8,128)S(1)} %dynamic-slice_bitcast_fusion.4), channel_id=1, source_target_pairs={{0,8},{4,12},{8,0},{12,4},{16,24},{20,28},{24,16},{28,20},{1,9},{5... | collective-permute-start | bytes 1769480 | tf_op jit(solution)/shard_map/ppermute | solution.py:37
  126.7 13.9 %collective-permute-start.12 = (f32[2,2,48,768]{3,2,1,0:T(8,128)S(1)}, f32[2,2,48,768]{3,2,1,0:T(8,128)S(1)}, u32[]{:S(2)}, u32[]{:S(2)}) collective-permute-start(f32[2,2,48,768]{3,2,1,0:T(8,128)S(1)} %dynamic-slice_bitcast_fusion.5), channel_id=1, source_target_pairs={{0,4},{4,0},{8,12},{12,8},{16,20},{20,16},{24,28},{28,24},{1,5},{5... | collective-permute-start | bytes 1769480 | tf_op jit(solution)/shard_map/ppermute | solution.py:37
  128.3 12.1 %collective-permute-start.15 = (f32[1281]{0:T(1024)S(1)}, f32[1281]{0:T(1024)S(1)}, u32[]{:S(2)}, u32[]{:S(2)}) collective-permute-start(f32[1281]{0:T(1024)S(1)} %add.186), channel_id=1, source_target_pairs={{0,8},{4,12},{8,0},{12,4},{16,24},{20,28},{24,16},{28,20},{1,9},{5... | collective-permute-start | bytes 15380 | tf_op jit(solution)/shard_map/ppermute | solution.py:37
  140.8 15.7 %collective-permute-start.18 = (f32[2,48,768]{2,1,0:T(8,128)S(1)}, f32[2,48,768]{2,1,0:T(8,128)S(1)}, u32[]{:S(2)}, u32[]{:S(2)}) collective-permute-start(f32[2,48,768]{2,1,0:T(8,128)S(1)} %dynamic-slice_bitcast_fusion.6), channel_id=1, source_target_pairs={{0,4},{4,0},{8,12},{12,8},{16,20},{20,16},{24,28},{28,24},{1,5},{5... | collective-permute-start | bytes 884744 | tf_op jit(solution)/shard_map/ppermute | solution.py:37
  142.5 14.0 %collective-permute-start.17 = (f32[2,48,768]{2,1,0:T(8,128)S(1)}, f32[2,48,768]{2,1,0:T(8,128)S(1)}, u32[]{:S(2)}, u32[]{:S(2)}) collective-permute-start(f32[2,48,768]{2,1,0:T(8,128)S(1)} %dynamic-slice_bitcast_fusion.7), channel_id=1, source_target_pairs={{0,16},{4,20},{8,24},{12,28},{16,0},{20,4},{24,8},{28,12},{1,17},{... | collective-permute-start | bytes 884744 | tf_op jit(solution)/shard_map/ppermute | solution.py:37
  145.2 11.5 %collective-permute-start.16 = (f32[2,48,768]{2,1,0:T(8,128)S(1)}, f32[2,48,768]{2,1,0:T(8,128)S(1)}, u32[]{:S(2)}, u32[]{:S(2)}) collective-permute-start(f32[2,48,768]{2,1,0:T(8,128)S(1)} %dynamic-slice_bitcast_fusion.8), channel_id=1, source_target_pairs={{0,8},{4,12},{8,0},{12,4},{16,24},{20,28},{24,16},{28,20},{1,9},{5... | collective-permute-start | bytes 884744 | tf_op jit(solution)/shard_map/ppermute | solution.py:37
  146.9 9.6 %collective-permute-start.19 = (f32[1281]{0:T(1024)S(1)}, f32[1281]{0:T(1024)S(1)}, u32[]{:S(2)}, u32[]{:S(2)}) collective-permute-start(f32[1281]{0:T(1024)S(1)} %add.194), channel_id=1, source_target_pairs={{0,16},{4,20},{8,24},{12,28},{16,0},{20,4},{24,8},{28,12},{1,17},{... | collective-permute-start | bytes 15380 | tf_op jit(solution)/shard_map/ppermute | solution.py:37
  158.6 13.2 %collective-permute-start.22 = (f32[48,768]{1,0:T(8,128)S(1)}, f32[48,768]{1,0:T(8,128)S(1)}, u32[]{:S(2)}, u32[]{:S(2)}) collective-permute-start(f32[48,768]{1,0:T(8,128)S(1)} %dynamic-slice_bitcast_fusion.9), channel_id=1, source_target_pairs={{0,16},{4,20},{8,24},{12,28},{16,0},{20,4},{24,8},{28,12},{1,17},{... | collective-permute-start | bytes 442376 | tf_op jit(solution)/shard_map/ppermute | solution.py:37
  161.0 10.8 %collective-permute-start.21 = (f32[48,768]{1,0:T(8,128)S(1)}, f32[48,768]{1,0:T(8,128)S(1)}, u32[]{:S(2)}, u32[]{:S(2)}) collective-permute-start(f32[48,768]{1,0:T(8,128)S(1)} %dynamic-slice_bitcast_fusion.10), channel_id=1, source_target_pairs={{0,2},{1,3},{2,0},{3,1},{4,6},{5,7},{6,4},{7,5},{8,10},{9,11},{10,... | collective-permute-start | bytes 442376 | tf_op jit(solution)/shard_map/ppermute | solution.py:37
  162.6 10.8 %collective-permute-start.20 = (f32[48,768]{1,0:T(8,128)S(1)}, f32[48,768]{1,0:T(8,128)S(1)}, u32[]{:S(2)}, u32[]{:S(2)}) collective-permute-start(f32[48,768]{1,0:T(8,128)S(1)} %dynamic-slice_bitcast_fusion.11), channel_id=1, source_target_pairs={{0,16},{4,20},{8,24},{12,28},{16,0},{20,4},{24,8},{28,12},{1,17},{... | collective-permute-start | bytes 442376 | tf_op jit(solution)/shard_map/ppermute | solution.py:37
  (13 other events, 113.8 us)

commit v8 on v4

--- a/solution.py
+++ b/solution.py
@@ -202,21 +202,22 @@
             sends.append(lax.dynamic_index_in_dim(pieces[s], 1 - mine, ax, keepdims=False))
             axes_of[s].pop(ax)
         received = []
-        if step < len(small_bits):
+        small = step - 1
+        if 0 <= small < len(small_bits):
             packed, sends = lax.optimization_barrier((packed, sends))
-            received.append(exchange(packed, *small_bits[step]))
+            received.append(exchange(packed, *small_bits[small]))
         received = [exchange(sends[s], orders[s][step][0], orders[s][step][1]) for s in range(3)] + received
         if step < halves:
             received, grad_chunks[step] = lax.optimization_barrier((received, grad_chunks[step]))
         else:
             received = lax.optimization_barrier(received)
-        if step < len(small_bits):
+        if 0 <= small < len(small_bits):
             packed = packed + received.pop()
         pieces = [keeps[s] + received[s] for s in range(3)]
     grad_weight = jnp.concatenate(pieces, 1).reshape(rows, taps, out_chans)
 
-    for step in range(len(rest), len(small_bits)):
-        packed = packed + exchange(packed, *small_bits[step])
+    for small in range(len(rest) - 1, len(small_bits)):
+        packed = packed + exchange(packed, *small_bits[small])
     grad_shift = packed[:out_chans] / mean_weight
     grad_gain = packed[out_chans : 2 * out_chans] / mean_weight
     grad_class = packed[2 * out_chans : (2 + classes) * out_chans].reshape(classes, out_chans) / mean_weight

time: 160 us -> 168 us (1.050)
  other arithmetic: 15.6 us -> 21.6 us
  waiting for transfers between devices: 35.5 us -> 40.7 us
  starting transfers between devices: 35.3 us -> 32.5 us
  local copies, waits for them, and re-layouts: 6.95 us -> 9.27 us
    ppermute x21, waiting for transfers between devices: 35.5 us -> 40.7 us  [exchange(): return lax.ppermute(x, axis, pairs)]
    add x14, other arithmetic: 1.95 us -> 7.11 us  [body(): pieces = [keeps[s] + received[s] for s in range(3)]]
    ppermute x21, starting transfers between devices: 32.7 us -> 29.9 us  [exchange(): return lax.ppermute(x, axis, pairs)]
    dot_general x3, matrix products: 18 us -> 15.6 us  [body(): lax.dot_general(flat_x, cols, (((0,), (0,)), ((), ())), preferred_element...]
    squeeze x12, local copies, waits for them, and re-layouts: 0.54 us -> 2.84 us  [body(): lax.dynamic_index_in_dim(pieces[s], 1 - mine, ax, keepdims=False)]
  transfers between devices with their start and end apart: 23 -> 23, of which waited for: 8 -> 12; matrix products, arithmetic and copies ran while one was open for 32% -> 30% of each run, Pallas kernels for 0% -> 0%
where the time goes in v8:
time: 168 us; the launch traced here: 167 us
  waiting for transfers between devices  40.7 us (24%)
  matrix products  38.7 us (23%)
  starting transfers between devices  32.5 us (19%)
  other arithmetic  21.6 us (13%)
  blocking collectives  19.2 us (11%)
  local copies, waits for them, and re-layouts  9.27 us (6%)
  between operations  5.35 us (3%)
    ppermute x21, waiting for transfers between devices, exchange(): return lax.ppermute(x, axis, pairs)  40.7 us
    ppermute x21, starting transfers between devices, exchange(): return lax.ppermute(x, axis, pairs)  29.9 us
    dot_general x2, matrix products, body(): lax.dot_general(shifted.reshape(local_pix, taps, out_chans), conv_weight[...  18.2 us
    dot_general x3, matrix products, body(): lax.dot_general(flat_x, cols, (((0,), (0,)), ((), ())), preferred_element...  15.6 us
    psum x1, blocking collectives, body(): tile_stats = lax.psum(slot[:, None] * local_stats[None, :], 'tile')  12.6 us
    add x14, other arithmetic, body(): pieces = [keeps[s] + received[s] for s in range(3)]  7.11 us
    psum x1, blocking collectives, body(): lax.psum((jnp.sum(preactivation_gradient, 0), jnp.sum(preactivation_gradi...  6.56 us
  transfers between devices with their start and end apart: 23, of which 12 were waited for; matrix products, arithmetic and copies ran while one was open for 30% of the time, Pallas kernels for 0%

profile of v8, /device:TPU:0, one launch (start us, length us, event | category | flops | bytes accessed | tf_op | source)
XLA Modules:
  0.0 167.4 jit_solution(11044151389848052341)
XLA Ops:
  6.5 12.6 %psum.35 = f32[4,513]{1,0:T(4,128)S(1)} all-reduce(f32[4,513]{1,0:T(4,128)S(1)} %broadcast_multiply_fusion), channel_id=1, replica_groups=mesh['rep'=8,'tile'=4] {'tile'}, use_global_device_ids=true, to_apply=%region_3.0 | all-reduce | flops 2052 | bytes 16416 | tf_op jit(solution)/shard_map/psum | solution.py:90
  22.2 1.8 %fusion.47 = (f32[1728]{0:T(1024)S(1)}, f32[1728,3]{0,1:T(4,128)S(1)}) fusion(f32[3,256]{1,0:T(4,128)S(1)} %copy-done, f32[1728,256]{1,0:T(8,128)S(1)} %fusion.26, f32[256]{0:T(256)S(1)} %copy-done.10, f32[256]{0:T(256)S(1)} %copy-done.9), kind=kOutput, calls=%fused_computation.130 | convolution fusion | flops 17255808 | bytes 1802240 | tf_op jit(solution)/shard_map/dot_general | solution.py:104
  24.6 2.1 %fusion.45 = (f32[256]{0:T(256)S(1)}, f32[256]{0:T(256)S(1)}, f32[1728,256]{1,0:T(8,128)S(1)}) fusion(f32[256]{0:T(256)S(1)} %get-tuple-element.125, f32[256]{0:T(256)S(1)} %broadcast_multiply_fusion.2, bf16[2,12,72,256]{3,2,1,0:T(8,128)(2,1)S(1)} %copy-done.2, f32[3,256]{1,0:T(4,128)S(1)} %copy-done, f32[1728,3]{0,1:T(4,128)S(1)} %get-tuple-element.127, ...), kind=kOutput, calls=%fused_computation.128 | convolution fusion | flops 20374336 | bytes 4474368 | tf_op jit(solution)/shard_map/dot_general | solution.py:112
  27.8 6.6 %all-reduce.2 = (f32[1]{0:T(128)}, f32[768]{0:T(1024)S(1)}, f32[256]{0:T(256)S(1)}, f32[256]{0:T(256)S(1)}) all-reduce(f32[1]{0:T(128)} %bitcast.2, f32[768]{0:T(1024)S(1)} %reshape.126, f32[256]{0:T(256)S(1)} %get-tuple-element.99, f32[256]{0:T(256)S(1)} %get-tuple-element.98), channel_id=1, replica_groups=mesh['rep'=8,'tile'=4] {'tile'}, use_global_device_ids=true, to_apply=%region_16.17 | all-reduce | flops 1281 | bytes 10248 | tf_op jit(solution)/shard_map/psum | solution.py:114
  36.2 2.9 %collective-permute-start.1 = (f32[]{:T(128)}, f32[]{:T(128)}, u32[]{:S(2)}, u32[]{:S(2)}) collective-permute-start(f32[]{:T(128)} %add.175), channel_id=1, source_target_pairs={{0,8},{4,12},{8,0},{12,4},{16,24},{20,28},{24,16},{28,20},{1,9},{5... | collective-permute-start | bytes 20 | tf_op jit(solution)/shard_map/ppermute | solution.py:37
  40.5 4.0 %collective-permute-start.2 = (f32[]{:T(128)}, f32[]{:T(128)}, u32[]{:S(2)}, u32[]{:S(2)}) collective-permute-start(f32[]{:T(128)} %add.176), channel_id=1, source_target_pairs={{0,16},{4,20},{8,24},{12,28},{16,0},{20,4},{24,8},{28,12},{1,17},{... | collective-permute-start | bytes 20 | tf_op jit(solution)/shard_map/ppermute | solution.py:37
  49.7 6.5 %fusion.14 = f32[1536,768]{1,0:T(8,128)S(1)} fusion(bf16[1728,1536]{1,0:T(8,128)(2,1)} %bitcast.142, bf16[1728,256]{1,0:T(8,128)(2,1)S(1)} %bitcast.133, bf16[1728,256]{1,0:T(8,128)(2,1)S(1)} %multiply_convert_fusion, bf16[1728,256]{1,0:T(8,128)(2,1)S(1)} %bitcast.135), kind=kOutput, calls=%fused_computation.20 | convolution fusion | flops 4084826112 | bytes 12681216 | tf_op jit(solution)/shard_map/dot_general | solution.py:168
  56.9 1.7 collective-permute-start.6
  58.6 2.0 %fusion.5 = bf16[2,36,96,256]{3,2,1,0:T(8,128)(2,1)S(1)} fusion(bf16[2,12,72,256]{3,2,1,0:T(8,128)(2,1)S(1)} %collective-permute-done.4, bf16[2,12,72,256]{3,2,1,0:T(8,128)(2,1)S(1)} %bitcast.116, bf16[2,12,72,256]{3,2,1,0:T(8,128)(2,1)S(1)} %collective-permute-done.3), kind=kLoop, calls=%fused_computation.10 | loop fusion | flops 21233664 | bytes 6193152 | tf_op jit(solution)/shard_map/concatenate | solution.py:21
  61.0 4.5 %fusion.20 = f32[1536,768]{1,0:T(8,128)S(1)} fusion(bf16[1728,1536]{1,0:T(8,128)(2,1)S(1)} %bitcast.145, bf16[1728,256]{1,0:T(8,128)(2,1)S(1)} %bitcast.125, bf16[1728,256]{1,0:T(8,128)(2,1)S(1)} %bitcast.121, bf16[1728,256]{1,0:T(8,128)(2,1)S(1)} %bitcast.127), kind=kOutput, calls=%fused_computation.26 | convolution fusion | flops 4084826112 | bytes 12681216 | tf_op jit(solution)/shard_map/dot_general | solution.py:168
  66.2 4.4 %collective-permute-start.7 = (f32[2,2,2,2,48,768]{5,4,3,2,0,1:T(8,128)S(1)}, f32[2,2,2,2,48,768]{5,4,3,2,0,1:T(8,128)S(1)}, u32[]{:S(2)}, u32[]{:S(2)}) collective-permute-start(f32[2,2,2,2,48,768]{5,4,3,2,0,1:T(8,128)S(1)} %bitcast.138), channel_id=1, source_target_pairs={{0,1},{1,0},{2,3},{3,2},{4,5},{5,4},{6,7},{7,6},{8,9},{9,8},{10,11... | collective-permute-start | bytes 7077896 | tf_op jit(solution)/shard_map/ppermute | solution.py:37
  70.6 4.5 %fusion.8 = f32[1536,768]{1,0:T(8,128)S(1)} fusion(bf16[1728,1536]{1,0:T(8,128)(2,1)S(1)} %bitcast.146, bf16[1728,256]{1,0:T(8,128)(2,1)S(1)} %bitcast.129, bf16[1728,256]{1,0:T(8,128)(2,1)S(1)} %bitcast.123, bf16[1728,256]{1,0:T(8,128)(2,1)S(1)} %bitcast.131), kind=kOutput, calls=%fused_computation.14 | convolution fusion | flops 4084826112 | bytes 12681216 | tf_op jit(solution)/shard_map/dot_general | solution.py:168
  76.4 3.9 %collective-permute-done.5 = f32[2,2,2,2,48,768]{5,4,2,1,0,3:T(8,128)S(1)} collective-permute-done((f32[2,2,2,2,48,768]{5,4,2,1,0,3:T(8,128)S(1)}, f32[2,2,2,2,48,768]{5,4,2,1,0,3:T(8,128)S(1)}, u32[]{:S(2)}, u32[]{:S(2)}) %collective-permute-start.5) | collective-permute-done | bytes 2359328 | tf_op jit(solution)/shard_map/ppermute | solution.py:37
  84.2 8.6 %bitcast_convert_fusion.1 = bf16[1728,768]{1,0:T(8,128)(2,1)S(1)} fusion(bf16[1728,9,256]{2,0,1:T(8,128)(2,1)S(1)} %constant_dynamic-update-slice_fusion, bf16[9,1536,256]{2,1,0:T(8,128)(2,1)} %param.10), kind=kOutput, calls=%fused_computation.5 | convolution fusion | flops 6116622336 | bytes 14155776 | tf_op jit(solution)/shard_map/dot_general | solution.py:176
  92.8 16.0 %collective-permute-done.10 = f32[2,2,2,48,768]{4,3,2,1,0:T(8,128)S(1)} collective-permute-done((f32[2,2,2,48,768]{4,3,2,1,0:T(8,128)S(1)}, f32[2,2,2,48,768]{4,3,2,1,0:T(8,128)S(1)}, u32[]{:S(2)}, u32[]{:S(2)}) %collective-permute-start.10) | collective-permute-done | bytes 1179680 | tf_op jit(solution)/shard_map/ppermute | solution.py:37
  108.8 2.0 %collective-permute-done.9 = f32[2,2,2,48,768]{4,3,2,1,0:T(8,128)S(1)} collective-permute-done((f32[2,2,2,48,768]{4,3,2,1,0:T(8,128)S(1)}, f32[2,2,2,48,768]{4,3,2,1,0:T(8,128)S(1)}, u32[]{:S(2)}, u32[]{:S(2)}) %collective-permute-start.9) | collective-permute-done | bytes 1179680 | tf_op jit(solution)/shard_map/ppermute | solution.py:37
  115.1 9.6 %bitcast_convert_fusion = bf16[1728,768]{1,0:T(8,128)(2,1)} fusion(bf16[1728,9,256]{2,0,1:T(8,128)(2,1)S(1)} %constant_dynamic-update-slice_fusion, bf16[9,1536,256]{2,1,0:T(8,128)(2,1)} %param.10), kind=kOutput, calls=%fused_computation.4 | convolution fusion | flops 6116622336 | bytes 14155776 | tf_op jit(solution)/shard_map/dot_general | solution.py:176
  124.7 1.7 %collective-permute-done.14 = f32[1281]{0:T(1024)S(1)} collective-permute-done((f32[1281]{0:T(1024)S(1)}, f32[1281]{0:T(1024)S(1)}, u32[]{:S(2)}, u32[]{:S(2)}) %collective-permute-start.14) | collective-permute-done | bytes 5156 | tf_op jit(solution)/shard_map/ppermute | solution.py:37
  131.9 2.6 %collective-permute-start.16 = (f32[2,48,768]{2,1,0:T(8,128)}, f32[2,48,768]{2,1,0:T(8,128)}, u32[]{:S(2)}, u32[]{:S(2)}) collective-permute-start(f32[2,48,768]{2,1,0:T(8,128)} %dynamic-slice_bitcast_fusion.7), channel_id=1, source_target_pairs={{0,16},{4,20},{8,24},{12,28},{16,0},{20,4},{24,8},{28,12},{1,17},{... | collective-permute-start | bytes 884744 | tf_op jit(solution)/shard_map/ppermute | solution.py:37
  135.4 7.9 %collective-permute-done.18 = f32[1281]{0:T(1024)} collective-permute-done((f32[1281]{0:T(1024)S(1)}, f32[1281]{0:T(1024)}, u32[]{:S(2)}, u32[]{:S(2)}) %collective-permute-start.18) | collective-permute-done | bytes 5156 | tf_op jit(solution)/shard_map/ppermute | solution.py:37
  143.3 2.0 %collective-permute-done.16 = f32[2,48,768]{2,1,0:T(8,128)} collective-permute-done((f32[2,48,768]{2,1,0:T(8,128)}, f32[2,48,768]{2,1,0:T(8,128)}, u32[]{:S(2)}, u32[]{:S(2)}) %collective-permute-start.16) | collective-permute-done | bytes 294944 | tf_op jit(solution)/shard_map/ppermute | solution.py:37
  151.6 1.7 collective-permute-start.21
  154.6 2.8 %pad_maximum_fusion = bf16[1728,1536]{1,0:T(8,128)(2,1)} fusion(bf16[1728,768]{1,0:T(8,128)(2,1)S(1)} %copy-done.3, bf16[1728,768]{1,0:T(8,128)(2,1)S(1)} %bitcast_convert_fusion.1), kind=kLoop, calls=%fused_computation.3 | loop fusion | flops 10616832 | bytes 10616832 | tf_op jit(solution)/shard_map/concatenate | solution.py:225
  157.4 3.7 %collective-permute-done.22 = f32[1281]{0:T(1024)S(1)} collective-permute-done((f32[1281]{0:T(1024)S(1)}, f32[1281]{0:T(1024)S(1)}, u32[]{:S(2)}, u32[]{:S(2)}) %collective-permute-start.22) | collective-permute-done | bytes 5156 | tf_op jit(solution)/shard_map/ppermute | solution.py:37
  (135 shorter events, 45.9 us)
Async XLA Ops:
  0.6 21.5 %copy-start = (f32[3,256]{1,0:T(4,128)S(1)}, f32[3,256]{1,0:T(4,128)}, u32[]{:S(2)}) copy-start(f32[3,256]{1,0:T(4,128)} %param.13) | copy-start | bytes 9220
  19.8 15.2 %collective-permute-start = (f32[]{:T(128)}, f32[]{:T(128)}, u32[]{:S(2)}, u32[]{:S(2)}) collective-permute-start(f32[]{:T(128)} %slice_reduce_fusion.1), channel_id=1, source_target_pairs={{0,4},{4,0},{8,12},{12,8},{16,20},{20,16},{24,28},{28,24},{1,5},{5... | collective-permute-start | bytes 20 | tf_op jit(solution)/shard_map/ppermute | solution.py:37
  36.2 3.7 %collective-permute-start.1 = (f32[]{:T(128)}, f32[]{:T(128)}, u32[]{:S(2)}, u32[]{:S(2)}) collective-permute-start(f32[]{:T(128)} %add.175), channel_id=1, source_target_pairs={{0,8},{4,12},{8,0},{12,4},{16,24},{20,28},{24,16},{28,20},{1,9},{5... | collective-permute-start | bytes 20 | tf_op jit(solution)/shard_map/ppermute | solution.py:37
  40.5 4.6 %collective-permute-start.2 = (f32[]{:T(128)}, f32[]{:T(128)}, u32[]{:S(2)}, u32[]{:S(2)}) collective-permute-start(f32[]{:T(128)} %add.176), channel_id=1, source_target_pairs={{0,16},{4,20},{8,24},{12,28},{16,0},{20,4},{24,8},{28,12},{1,17},{... | collective-permute-start | bytes 20 | tf_op jit(solution)/shard_map/ppermute | solution.py:37
  46.2 12.3 %collective-permute-start.3 = (bf16[2,12,72,256]{3,2,1,0:T(8,128)(2,1)S(1)}, bf16[2,12,72,256]{3,2,1,0:T(8,128)(2,1)S(1)}, u32[]{:S(2)}, u32[]{:S(2)}) collective-permute-start(bf16[2,12,72,256]{3,2,1,0:T(8,128)(2,1)S(1)} %bitcast.113), channel_id=1, source_target_pairs={{0,1},{1,2},{2,3},{4,5},{5,6},{6,7},{8,9},{9,10},{10,11},{12,13},{... | collective-permute-start | bytes 2654216 | tf_op jit(solution)/shard_map/ppermute | solution.py:19
  47.6 11.0 %collective-permute-start.4 = (bf16[2,12,72,256]{3,2,1,0:T(8,128)(2,1)S(1)}, bf16[2,12,72,256]{3,2,1,0:T(8,128)(2,1)S(1)}, u32[]{:S(2)}, u32[]{:S(2)}) collective-permute-start(bf16[2,12,72,256]{3,2,1,0:T(8,128)(2,1)S(1)} %bitcast.114), channel_id=1, source_target_pairs={{1,0},{2,1},{3,2},{5,4},{6,5},{7,6},{9,8},{10,9},{11,10},{13,12},{... | collective-permute-start | bytes 2654216 | tf_op jit(solution)/shard_map/ppermute | solution.py:20
  56.9 19.5 %collective-permute-start.6 = (f32[2,2,2,2,48,768]{5,4,3,1,0,2:T(8,128)S(1)}, f32[2,2,2,2,48,768]{5,4,3,1,0,2:T(8,128)S(1)}, u32[]{:S(2)}, u32[]{:S(2)}) collective-permute-start(f32[2,2,2,2,48,768]{5,4,3,1,0,2:T(8,128)S(1)} %bitcast.137), channel_id=1, source_target_pairs={{0,1},{1,0},{2,3},{3,2},{4,5},{5,4},{6,7},{7,6},{8,9},{9,8},{10,11... | collective-permute-start | bytes 7077896 | tf_op jit(solution)/shard_map/ppermute | solution.py:37
  66.2 10.3 %collective-permute-start.7 = (f32[2,2,2,2,48,768]{5,4,3,2,0,1:T(8,128)S(1)}, f32[2,2,2,2,48,768]{5,4,3,2,0,1:T(8,128)S(1)}, u32[]{:S(2)}, u32[]{:S(2)}) collective-permute-start(f32[2,2,2,2,48,768]{5,4,3,2,0,1:T(8,128)S(1)} %bitcast.138), channel_id=1, source_target_pairs={{0,1},{1,0},{2,3},{3,2},{4,5},{5,4},{6,7},{7,6},{8,9},{9,8},{10,11... | collective-permute-start | bytes 7077896 | tf_op jit(solution)/shard_map/ppermute | solution.py:37
  75.7 4.6 %collective-permute-start.5 = (f32[2,2,2,2,48,768]{5,4,2,1,0,3:T(8,128)S(1)}, f32[2,2,2,2,48,768]{5,4,2,1,0,3:T(8,128)S(1)}, u32[]{:S(2)}, u32[]{:S(2)}) collective-permute-start(f32[2,2,2,2,48,768]{5,4,2,1,0,3:T(8,128)S(1)} %bitcast.139), channel_id=1, source_target_pairs={{0,1},{1,0},{2,3},{3,2},{4,5},{5,4},{6,7},{7,6},{8,9},{9,8},{10,11... | collective-permute-start | bytes 7077896 | tf_op jit(solution)/shard_map/ppermute | solution.py:37
  80.7 28.1 %collective-permute-start.10 = (f32[2,2,2,48,768]{4,3,2,1,0:T(8,128)S(1)}, f32[2,2,2,48,768]{4,3,2,1,0:T(8,128)S(1)}, u32[]{:S(2)}, u32[]{:S(2)}) collective-permute-start(f32[2,2,2,48,768]{4,3,2,1,0:T(8,128)S(1)} %dynamic-slice_bitcast_fusion), channel_id=1, source_target_pairs={{0,8},{4,12},{8,0},{12,4},{16,24},{20,28},{24,16},{28,20},{1,9},{5... | collective-permute-start | bytes 3538952 | tf_op jit(solution)/shard_map/ppermute | solution.py:37
  83.0 27.8 %collective-permute-start.9 = (f32[2,2,2,48,768]{4,3,2,1,0:T(8,128)S(1)}, f32[2,2,2,48,768]{4,3,2,1,0:T(8,128)S(1)}, u32[]{:S(2)}, u32[]{:S(2)}) collective-permute-start(f32[2,2,2,48,768]{4,3,2,1,0:T(8,128)S(1)} %dynamic-slice_bitcast_fusion.1), channel_id=1, source_target_pairs={{0,4},{4,0},{8,12},{12,8},{16,20},{20,16},{24,28},{28,24},{1,5},{5... | collective-permute-start | bytes 3538952 | tf_op jit(solution)/shard_map/ppermute | solution.py:37
  84.1 27.5 %collective-permute-start.8 = (f32[2,2,2,48,768]{4,3,2,1,0:T(8,128)S(1)}, f32[2,2,2,48,768]{4,3,2,1,0:T(8,128)S(1)}, u32[]{:S(2)}, u32[]{:S(2)}) collective-permute-start(f32[2,2,2,48,768]{4,3,2,1,0:T(8,128)S(1)} %dynamic-slice_bitcast_fusion.2), channel_id=1, source_target_pairs={{0,2},{1,3},{2,0},{3,1},{4,6},{5,7},{6,4},{7,5},{8,10},{9,11},{10,... | collective-permute-start | bytes 3538952 | tf_op jit(solution)/shard_map/ppermute | solution.py:37
  112.3 14.1 %collective-permute-start.11 = (f32[2,2,48,768]{3,2,1,0:T(8,128)S(1)}, f32[2,2,48,768]{3,2,1,0:T(8,128)S(1)}, u32[]{:S(2)}, u32[]{:S(2)}) collective-permute-start(f32[2,2,48,768]{3,2,1,0:T(8,128)S(1)} %dynamic-slice_bitcast_fusion.5), channel_id=1, source_target_pairs={{0,4},{4,0},{8,12},{12,8},{16,20},{20,16},{24,28},{28,24},{1,5},{5... | collective-permute-start | bytes 1769480 | tf_op jit(solution)/shard_map/ppermute | solution.py:37
  113.9 13.6 %collective-permute-start.12 = (f32[2,2,48,768]{3,2,1,0:T(8,128)S(1)}, f32[2,2,48,768]{3,2,1,0:T(8,128)S(1)}, u32[]{:S(2)}, u32[]{:S(2)}) collective-permute-start(f32[2,2,48,768]{3,2,1,0:T(8,128)S(1)} %dynamic-slice_bitcast_fusion.4), channel_id=1, source_target_pairs={{0,8},{4,12},{8,0},{12,4},{16,24},{20,28},{24,16},{28,20},{1,9},{5... | collective-permute-start | bytes 1769480 | tf_op jit(solution)/shard_map/ppermute | solution.py:37
  114.3 13.3 %collective-permute-start.13 = (f32[2,2,48,768]{3,2,1,0:T(8,128)S(1)}, f32[2,2,48,768]{3,2,1,0:T(8,128)S(1)}, u32[]{:S(2)}, u32[]{:S(2)}) collective-permute-start(f32[2,2,48,768]{3,2,1,0:T(8,128)S(1)} %dynamic-slice_bitcast_fusion.3), channel_id=1, source_target_pairs={{0,2},{1,3},{2,0},{3,1},{4,6},{5,7},{6,4},{7,5},{8,10},{9,11},{10,... | collective-permute-start | bytes 1769480 | tf_op jit(solution)/shard_map/ppermute | solution.py:37
  114.6 11.8 %collective-permute-start.14 = (f32[1281]{0:T(1024)S(1)}, f32[1281]{0:T(1024)S(1)}, u32[]{:S(2)}, u32[]{:S(2)}) collective-permute-start(f32[1281]{0:T(1024)S(1)} %pad_maximum_fusion.2), channel_id=1, source_target_pairs={{0,4},{4,0},{8,12},{12,8},{16,20},{20,16},{24,28},{28,24},{1,5},{5... | collective-permute-start | bytes 15380 | tf_op jit(solution)/shard_map/ppermute | solution.py:37
  130.3 13.0 %collective-permute-start.15 = (f32[2,48,768]{2,1,0:T(8,128)}, f32[2,48,768]{2,1,0:T(8,128)S(1)}, u32[]{:S(2)}, u32[]{:S(2)}) collective-permute-start(f32[2,48,768]{2,1,0:T(8,128)} %dynamic-slice_bitcast_fusion.8), channel_id=1, source_target_pairs={{0,8},{4,12},{8,0},{12,4},{16,24},{20,28},{24,16},{28,20},{1,9},{5... | collective-permute-start | bytes 884744 | tf_op jit(solution)/shard_map/ppermute | solution.py:37
  131.9 13.5 %collective-permute-start.16 = (f32[2,48,768]{2,1,0:T(8,128)}, f32[2,48,768]{2,1,0:T(8,128)}, u32[]{:S(2)}, u32[]{:S(2)}) collective-permute-start(f32[2,48,768]{2,1,0:T(8,128)} %dynamic-slice_bitcast_fusion.7), channel_id=1, source_target_pairs={{0,16},{4,20},{8,24},{12,28},{16,0},{20,4},{24,8},{28,12},{1,17},{... | collective-permute-start | bytes 884744 | tf_op jit(solution)/shard_map/ppermute | solution.py:37
  134.4 10.9 %collective-permute-start.17 = (f32[2,48,768]{2,1,0:T(8,128)}, f32[2,48,768]{2,1,0:T(8,128)}, u32[]{:S(2)}, u32[]{:S(2)}) collective-permute-start(f32[2,48,768]{2,1,0:T(8,128)} %dynamic-slice_bitcast_fusion.6), channel_id=1, source_target_pairs={{0,4},{4,0},{8,12},{12,8},{16,20},{20,16},{24,28},{28,24},{1,5},{5... | collective-permute-start | bytes 884744 | tf_op jit(solution)/shard_map/ppermute | solution.py:37
  135.0 8.3 %collective-permute-start.18 = (f32[1281]{0:T(1024)S(1)}, f32[1281]{0:T(1024)}, u32[]{:S(2)}, u32[]{:S(2)}) collective-permute-start(f32[1281]{0:T(1024)S(1)} %add.193), channel_id=1, source_target_pairs={{0,8},{4,12},{8,0},{12,4},{16,24},{20,28},{24,16},{28,20},{1,9},{5... | collective-permute-start | bytes 15380 | tf_op jit(solution)/shard_map/ppermute | solution.py:37
  149.5 11.6 %collective-permute-start.19 = (f32[48,768]{1,0:T(8,128)S(1)}, f32[48,768]{1,0:T(8,128)S(1)}, u32[]{:S(2)}, u32[]{:S(2)}) collective-permute-start(f32[48,768]{1,0:T(8,128)S(1)} %dynamic-slice_bitcast_fusion.11), channel_id=1, source_target_pairs={{0,16},{4,20},{8,24},{12,28},{16,0},{20,4},{24,8},{28,12},{1,17},{... | collective-permute-start | bytes 442376 | tf_op jit(solution)/shard_map/ppermute | solution.py:37
  150.8 10.3 %collective-permute-start.20 = (f32[48,768]{1,0:T(8,128)S(1)}, f32[48,768]{1,0:T(8,128)S(1)}, u32[]{:S(2)}, u32[]{:S(2)}) collective-permute-start(f32[48,768]{1,0:T(8,128)S(1)} %dynamic-slice_bitcast_fusion.10), channel_id=1, source_target_pairs={{0,2},{1,3},{2,0},{3,1},{4,6},{5,7},{6,4},{7,5},{8,10},{9,11},{10,... | collective-permute-start | bytes 442376 | tf_op jit(solution)/shard_map/ppermute | solution.py:37
  151.6 9.5 %collective-permute-start.21 = (f32[48,768]{1,0:T(8,128)S(1)}, f32[48,768]{1,0:T(8,128)S(1)}, u32[]{:S(2)}, u32[]{:S(2)}) collective-permute-start(f32[48,768]{1,0:T(8,128)S(1)} %dynamic-slice_bitcast_fusion.9), channel_id=1, source_target_pairs={{0,16},{4,20},{8,24},{12,28},{16,0},{20,4},{24,8},{28,12},{1,17},{... | collective-permute-start | bytes 442376 | tf_op jit(solution)/shard_map/ppermute | solution.py:37
  153.3 7.8 %collective-permute-start.22 = (f32[1281]{0:T(1024)S(1)}, f32[1281]{0:T(1024)S(1)}, u32[]{:S(2)}, u32[]{:S(2)}) collective-permute-start(f32[1281]{0:T(1024)S(1)} %add.199), channel_id=1, source_target_pairs={{0,16},{4,20},{8,24},{12,28},{16,0},{20,4},{24,8},{28,12},{1,17},{... | collective-permute-start | bytes 15380 | tf_op jit(solution)/shard_map/ppermute | solution.py:37
  (12 other events, 126.8 us)
